TPU v7x, 512 devices: a whole 4x4x16 slice. The times are simulated.
512 devices in a mesh: ctx: 16 (over z_lo, y), ch: 32 (over z_hi, x, core).
Axes of the slice: x: 4, y: 4, z: 16 (z_hi: 4, z_lo: 4; z = z_hi * 4 + z_lo), core: 2. Of those that a mesh axis runs over, the one named last changes fastest.
Arguments:
- bases_in: bfloat16 [6144, 4096], P('ctx', 'ch'), may hold values from -70 to 70
- norm_gain: float32 [4096], replicated, may hold values from 0.1 to 1.9
- w_in: bfloat16 [4096, 3, 4096], P(None, None, 'ch'), may hold values from -0.09375 to 0.09375
- feat_taps: float32 [3, 3, 4096], P(None, None, 'ch'), may hold values from -3.5 to 3.5
- long_filter: bfloat16 [4096, 128], P('ch'), may hold values from -0.5 to 0.5
- skip_gain: float32 [4096], P('ch'), may hold values from -4 to 4
- w_out: bfloat16 [4096, 4096], P('ch'), may hold values from -0.1875 to 0.1875
Outputs:
- mixed: bfloat16 [6144, 4096], P('ctx', 'ch')
All inputs are finite; a program needn't handle non-finite values.
Results may differ from a plain program's by a relative error of at most 0.02.
Values may be sent and summed in bfloat16 or wider, within the bound.
No kernel may reach another device: no remote copies, remote signals or barrier semaphores. Data moves between devices by JAX's collectives and lax.ppermute only.
A program may use at most 128 MiB of HBM per device.

v0:
```python
import jax
import jax.numpy as jnp
from jax import lax
from jax.sharding import PartitionSpec as P


def passed_along(value, axis, steps):
    count = lax.axis_size(axis)
    initial, last = (max(0, -steps), min(count, count - steps))
    return lax.ppermute(value, axis, [(source, source + steps) for source in range(initial, last)])


def featurize(extended, feat_taps, count):
    feat_len = feat_taps.shape[1]
    chans = feat_taps.shape[2]
    shaped = extended.reshape(extended.shape[0], 3, chans)
    feats = jnp.zeros((count, 3, chans), jnp.float32)
    for tap in range(feat_len):
        feats = feats + feat_taps[:, tap, :] * shaped[
            feat_len - 1 - tap : feat_len - 1 - tap + count
        ].astype(jnp.float32)
    return feats


def band_matrix(long_filter):
    chans, taps = long_filter.shape
    row_len = 3 * taps - 1
    reversed_taps = long_filter[:, ::-1]
    padded_row = jnp.concatenate(
        [
            jnp.zeros((chans, taps), jnp.bfloat16),
            reversed_taps,
            jnp.zeros((chans, taps - 1), jnp.bfloat16),
        ],
        axis=1,
    )
    tiled = jnp.broadcast_to(padded_row[:, None, :], (chans, taps, row_len)).reshape(
        chans, taps * row_len
    )
    skewed = tiled[:, taps - 1 : taps - 1 + taps * (row_len - 1)].reshape(chans, taps, row_len - 1)
    return skewed[:, :, : 2 * taps]


def shards(bases_in, norm_gain, w_in, feat_taps, long_filter, skip_gain, w_out):
    tok, chans = bases_in.shape
    width = norm_gain.shape[0]
    taps = long_filter.shape[1]
    feat_len = feat_taps.shape[1]
    w_flat = w_in.reshape(width, 3 * chans)
    whole = lax.all_gather(bases_in, "ch", axis=1, tiled=True)
    wide = whole.astype(jnp.float32)
    inverse = lax.rsqrt(jnp.mean(wide * wide, axis=1, keepdims=True) + 1e-05)
    normed = (wide * inverse * norm_gain).astype(jnp.bfloat16)
    mixed_in = jnp.dot(normed, w_flat, preferred_element_type=jnp.float32)
    projected = mixed_in.astype(jnp.bfloat16)
    earlier = passed_along(projected[tok - (feat_len - 1) :], "ctx", 1)
    feats = featurize(jnp.concatenate([earlier, projected], axis=0), feat_taps, tok)
    query = feats[:, 0, :]
    product = (feats[:, 1, :] * feats[:, 2, :]).astype(jnp.bfloat16)
    before = passed_along(product[tok - (taps - 1) :], "ctx", 1)
    extended = jnp.concatenate([jnp.zeros((1, chans), jnp.bfloat16), before, product], axis=0)
    toeplitz = band_matrix(long_filter)
    blocks = tok // taps
    older = extended[:tok].reshape(blocks, taps, chans)
    newer = extended[taps:].reshape(blocks, taps, chans)
    window = jnp.concatenate([older, newer], axis=1)
    filtered = jnp.einsum(
        "cij,bjc->bic", toeplitz, window, preferred_element_type=jnp.float32
    ).reshape(tok, chans)
    gated = (query * (filtered + skip_gain * product.astype(jnp.float32))).astype(jnp.bfloat16)
    terms = jnp.dot(gated, w_out, preferred_element_type=jnp.float32)
    return lax.psum_scatter(terms.astype(jnp.bfloat16), "ch", scatter_dimension=1, tiled=True)


def solution(mesh):
    in_specs = (
        P("ctx", "ch"),
        P(),
        P(None, None, "ch"),
        P(None, None, "ch"),
        P("ch", None),
        P("ch"),
        P("ch", None),
    )
    out_specs = P("ctx", "ch")
    return jax.shard_map(shards, mesh=mesh, in_specs=in_specs, out_specs=out_specs, check_vma=False)
```

profile of v0, /device:TPU:1, one launch (start us, length us, event | category | flops | bytes accessed | tf_op | source)
XLA Modules:
  0.0 345.5 jit_solution(9485300635172362352)
XLA Ops:
  6.5 0.7 all-gather.2.cloned.1.call-update
  7.3 0.0 reduce-scatter.4.cloned.1.call-start
  7.3 4.7 %copy.25 = bf16[4096,3,128]{0,2,1:T(8,128)(2,1)} copy(bf16[4096,3,128]{2,0,1:T(8,128)(2,1)} %param.9) | data formatting | bytes 6291456 | tf_op args[2]
  12.1 96.0 %all-gather.2.cloned.1.call-done = bf16[384,4096]{1,0:T(8,128)(2,1)} async-done(((bf16[384,128]{1,0:T(8,128)(2,1)}), bf16[384,4096]{1,0:T(8,128)(2,1)}) %all-gather.2.cloned.1.call-update) | async-done | bytes 3145744 | tf_op jit(solution)/shard_map/all_gather | solution.py:50
  108.1 2.6 fusion.2
  110.7 4.7 %fusion.9 = bf16[384,384]{1,0:T(8,128)(2,1)S(1)} fusion(bf16[4096,384]{0,1:T(8,128)(2,1)} %bitcast.38, bf16[384,4096]{1,0:T(8,128)(2,1)} %all-gather.2.cloned.1.call-done, f32[4096]{0:T(1024)S(1)} %copy-done.4, f32[384]{0:T(512)S(1)} %add_rsqrt_fusion), kind=kOutput, calls=%fused_computation.11 | convolution fusion | flops 1214398464 | bytes 6604288 | tf_op jit(solution)/shard_map/dot_general | solution.py:54
  115.4 2.9 collective-permute-start
  118.3 0.1 rev.3
  118.5 0.2 copy.26
  118.6 0.4 collective-permute-done
  119.0 0.1 fusion.16
  119.1 0.2 copy.28
  119.3 0.2 copy.27
  119.6 0.2 multiply_add_fusion
  119.8 0.1 slice_bitcast_fusion.1
  119.9 3.6 %collective-permute-start.1 = (bf16[127,128]{0,1:T(8,128)(2,1)S(1)}, bf16[127,128]{0,1:T(8,128)(2,1)S(1)}, u32[]{:S(2)}, u32[]{:S(2)}) collective-permute-start(bf16[127,128]{0,1:T(8,128)(2,1)S(1)} %slice_bitcast_fusion.1), channel_id=1, source_target_pairs={{0,32},{32,64},{64,96},{96,128},{128,160},{160,192},{192,224},{224... | collective-permute-start | bytes 97544 | tf_op jit(solution)/shard_map/ppermute | solution.py:10
  123.6 5.6 %broadcast_in_dim.21 = bf16[128,128,383]{2,1,0:T(8,128)(2,1)} broadcast(bf16[128,383]{1,0:T(8,128)(2,1)S(1)} %maximum_maximum_fusion), dimensions={0,2} | broadcast | bytes 12648192 | tf_op jit(solution)/shard_map/broadcast_in_dim | solution.py:37
  129.2 22.9 %reshape.49 = bf16[128,49024]{1,0:T(8,128)(2,1)} reshape(bf16[128,128,383]{2,1,0:T(8,128)(2,1)} %broadcast_in_dim.21) | data formatting | bytes 25100288 | tf_op jit(solution)/shard_map/reshape | solution.py:37
  152.1 11.6 %slice.68 = bf16[128,48896]{1,0:T(8,128)(2,1)} slice(bf16[128,49024]{1,0:T(8,128)(2,1)} %reshape.49), slice={[0:128], [127:49023]} | slice | bytes 25034752 | tf_op jit(solution)/shard_map/slice | solution.py:40
  163.8 33.8 %reshape.50 = bf16[128,128,382]{2,1,0:T(8,128)(2,1)} reshape(bf16[128,48896]{1,0:T(8,128)(2,1)} %slice.68) | data formatting | bytes 25034752 | tf_op jit(solution)/shard_map/reshape | solution.py:40
  197.6 0.1 copy.29
  197.7 0.1 copy.33
  197.9 0.1 copy.30
  198.0 0.1 pad_maximum_fusion.1
  198.1 0.1 copy.32
  198.3 5.6 %fusion.12 = f32[3,128,128]{1,0,2:T(4,128)S(1)} fusion(bf16[128,128,382]{2,1,0:T(8,128)(2,1)} %reshape.50, bf16[3,128,128]{1,0,2:T(4,128)(2,1)S(1)} %copy.33, bf16[3,128,128]{1,0,2:T(4,128)(2,1)S(1)} %copy.32), kind=kOutput, calls=%fused_computation.12 | convolution fusion | flops 25559040 | bytes 8781824 | tf_op jit(solution)/shard_map/cij,bjc->bic/dot_general | solution.py:67
  203.9 0.1 copy.34
  204.1 0.1 copy.36
  204.2 2.8 convolution_convert_fusion
  207.0 4.6 %copy.38 = bf16[384,4096]{0,1:T(8,128)(2,1)} copy(bf16[384,4096]{1,0:T(8,128)(2,1)} %convolution_convert_fusion) | data formatting | bytes 6291456
  211.7 125.4 %reduce-scatter.4.cloned.1.call-done = bf16[128,384]{1,0:T(8,128)(2,1)} async-done(((bf16[4096,384]{1,0:T(8,128)(2,1)}), bf16[128,384]{1,0:T(8,128)(2,1)}) %reduce-scatter.4.cloned.1.call-update) | async-done | bytes 98320
  337.0 1.6 copy.39
  (25 shorter events, 0.1 us)
Async XLA Ops:
  6.5 197.7 %copy-start = (bf16[128,4096]{1,0:T(8,128)(2,1)S(1)}, bf16[128,4096]{1,0:T(8,128)(2,1)}, u32[]{:S(2)}) copy-start(bf16[128,4096]{1,0:T(8,128)(2,1)} %param.13) | copy-start | bytes 3145732
  6.5 5.5 %copy-start.2 = (f32[3,3,128]{2,1,0:T(4,128)S(1)}, f32[3,3,128]{2,1,0:T(4,128)}, u32[]{:S(2)}) copy-start(f32[3,3,128]{2,1,0:T(4,128)} %param.10) | copy-start | bytes 13828
  6.5 104.1 %copy-start.4 = (f32[4096]{0:T(1024)S(1)}, f32[4096]{0:T(1024)}, u32[]{:S(2)}) copy-start(f32[4096]{0:T(1024)} %param.8) | copy-start | bytes 49156
  6.5 101.5 %all-gather.2.cloned.1.call-start = ((), (), s32[]{:S(2)}) async-start(), calls=%async_computation.1 | async-start | bytes 3244032 | tf_op jit(solution)/shard_map/all_gather | solution.py:50
  7.3 329.8 %reduce-scatter.4.cloned.1.call-start = ((), (), s32[]{:S(2)}) async-start(), calls=%async_computation.2 | async-start | bytes 3244032
  110.7 7.7 %copy-start.1 = (bf16[128,128]{1,0:T(8,128)(2,1)S(1)}, bf16[128,128]{1,0:T(8,128)(2,1)}, u32[]{:S(2)}) copy-start(bf16[128,128]{1,0:T(8,128)(2,1)} %param.11) | copy-start | bytes 98308
  115.4 3.6 %collective-permute-start = (bf16[2,384]{1,0:T(2,128)(2,1)S(1)}, bf16[2,384]{1,0:T(2,128)(2,1)S(1)}, u32[]{:S(2)}, u32[]{:S(2)}) collective-permute-start(bf16[2,384]{1,0:T(2,128)(2,1)S(1)} %slice.60), channel_id=1, source_target_pairs={{0,32},{32,64},{64,96},{96,128},{128,160},{160,192},{192,224},{224... | collective-permute-start | bytes 4616 | tf_op jit(solution)/shard_map/ppermute | solution.py:10
  119.9 77.9 %collective-permute-start.1 = (bf16[127,128]{0,1:T(8,128)(2,1)S(1)}, bf16[127,128]{0,1:T(8,128)(2,1)S(1)}, u32[]{:S(2)}, u32[]{:S(2)}) collective-permute-start(bf16[127,128]{0,1:T(8,128)(2,1)S(1)} %slice_bitcast_fusion.1), channel_id=1, source_target_pairs={{0,32},{32,64},{64,96},{96,128},{128,160},{160,192},{192,224},{224... | collective-permute-start | bytes 97544 | tf_op jit(solution)/shard_map/ppermute | solution.py:10
  197.6 6.6 %copy-start.3 = (f32[128]{0:T(128)S(1)}, f32[128]{0:T(128)}, u32[]{:S(2)}) copy-start(f32[128]{0:T(128)} %param.12) | copy-start | bytes 1540
Sparse Core Ops, SparseCore 0:
  10.4 97.6 all-gather.1
  211.8 125.1 reduce-scatter.3
where the time goes:
time: 346 us; the launch traced here: 345 us
  waiting for transfers between devices  222 us (64%)
  local copies, waits for them, and re-layouts  86.7 us (25%)
  between operations  13.6 us (4%)
  matrix products  13.1 us (4%)
  starting transfers between devices  6.54 us (2%)
    unnamed x3, waiting for transfers between devices  126 us
    all_gather x1, waiting for transfers between devices, shards(): whole = lax.all_gather(bases_in, 'ch', axis=1, tiled=True)  96 us
    reshape x1, local copies, waits for them, and re-layouts, band_matrix(): tiled[:, taps - 1:taps - 1 + taps * (row_len - 1)]  33.8 us
    reshape x1, local copies, waits for them, and re-layouts, band_matrix(): jnp.broadcast_to(padded_row[:, None, :], (chans, taps, row_len))  22.9 us
    slice x1, local copies, waits for them, and re-layouts, band_matrix(): tiled[:, taps - 1:taps - 1 + taps * (row_len - 1)]  11.6 us
    unnamed x15, local copies, waits for them, and re-layouts  11 us
  transfers between devices with their start and end apart: 4, of which 3 were waited for; matrix products, arithmetic and copies ran while one was open for 23% of the time, Pallas kernels for 0%

commit v1 on v0

v1 whole, which is shorter than its diff:
```python
import jax
import jax.numpy as jnp
from jax import lax
from jax.experimental import pallas as pl
from jax.experimental.pallas import tpu as pltpu
from jax.sharding import Mesh, PartitionSpec as P

CTX_PARTS = (("z_lo", 4), ("y", 4))
CH_PARTS = (("z_hi", 4), ("x", 4), ("core", 2))
CTX = tuple(name for name, _ in CTX_PARTS)
CH = tuple(name for name, _ in CH_PARTS)
CTX_COUNT = 16
FILTER_ROWS = 64


def passed_along(value, axis, count, steps):
    initial, last = (max(0, -steps), min(count, count - steps))
    return lax.ppermute(value, axis, [(source, source + steps) for source in range(initial, last)])


def featurize(extended, feat_taps, count):
    feat_len = feat_taps.shape[1]
    chans = feat_taps.shape[2]
    shaped = extended.reshape(extended.shape[0], 3, chans)
    feats = jnp.zeros((count, 3, chans), jnp.float32)
    for tap in range(feat_len):
        feats = feats + feat_taps[:, tap, :] * shaped[
            feat_len - 1 - tap : feat_len - 1 - tap + count
        ].astype(jnp.float32)
    return feats


def filter_kernel(ext_ref, filt_ref, out_ref, shift_ref):
    taps = filt_ref.shape[0]
    rows = shift_ref.shape[1]
    count = out_ref.shape[0]
    for b in range(8):
        shift_ref[b] = ext_ref[pl.ds(8 - b, rows), :]

    def tile(index, carry):
        base = pl.multiple_of(index * FILTER_ROWS, 8)
        acc = jnp.zeros((FILTER_ROWS, out_ref.shape[1]), jnp.float32)
        for group in range(taps // 8):
            for b in range(8):
                tap = 8 * group + b
                acc = acc + filt_ref[pl.ds(tap, 1), :] * shift_ref[
                    b, pl.ds(base + taps - 8 - 8 * group, FILTER_ROWS), :
                ]
        out_ref[pl.ds(base, FILTER_ROWS), :] = acc
        return carry

    lax.fori_loop(0, count // FILTER_ROWS, tile, 0)


def causal_filter(extended, filt_rows):
    taps, chans = filt_rows.shape
    count = extended.shape[0] - taps
    rows = extended.shape[0] - 8
    return pl.pallas_call(
        filter_kernel,
        out_shape=jax.ShapeDtypeStruct((count, chans), jnp.float32),
        scratch_shapes=[pltpu.VMEM((8, rows, chans), jnp.float32)],
    )(extended, filt_rows)


def shards(bases_in, norm_gain, w_in, feat_taps, long_filter, skip_gain, w_out):
    tok, chans = bases_in.shape
    width = norm_gain.shape[0]
    taps = long_filter.shape[1]
    feat_len = feat_taps.shape[1]
    w_flat = w_in.reshape(width, 3 * chans)
    stacked = bases_in
    for name, _ in CH_PARTS:
        stacked = lax.all_gather(stacked, name, axis=0)
    whole = stacked.transpose(3, 2, 1, 0, 4).reshape(tok, width)
    wide = whole.astype(jnp.float32)
    inverse = lax.rsqrt(jnp.mean(wide * wide, axis=1, keepdims=True) + 1e-05)
    normed = (wide * inverse * norm_gain).astype(jnp.bfloat16)
    mixed_in = jnp.dot(normed, w_flat, preferred_element_type=jnp.float32)
    projected = mixed_in.astype(jnp.bfloat16)
    earlier = passed_along(projected[tok - (feat_len - 1) :], CTX, CTX_COUNT, 1)
    feats = featurize(jnp.concatenate([earlier, projected], axis=0), feat_taps, tok)
    query = feats[:, 0, :]
    product = (feats[:, 1, :] * feats[:, 2, :]).astype(jnp.bfloat16)
    before = passed_along(product[tok - (taps - 1) :], CTX, CTX_COUNT, 1)
    extended = jnp.concatenate(
        [jnp.zeros((1, chans), jnp.bfloat16), before, product], axis=0
    ).astype(jnp.float32)
    filtered = causal_filter(extended, long_filter.astype(jnp.float32).T)
    gated = (query * (filtered + skip_gain * product.astype(jnp.float32))).astype(jnp.bfloat16)
    terms = jnp.dot(gated, w_out, preferred_element_type=jnp.float32).astype(jnp.bfloat16)
    sizes = [size for _, size in CH_PARTS]
    split = terms.reshape(tok, *sizes, chans).transpose(3, 2, 1, 0, 4)
    for name, _ in CH_PARTS[::-1]:
        split = lax.psum_scatter(split, name, scatter_dimension=0)
    return split


def solution(mesh):
    shape = [size for _, size in CTX_PARTS] + [size for _, size in CH_PARTS]
    fine = Mesh(mesh.devices.reshape(shape), CTX + CH)
    in_specs = (
        P(CTX, CH),
        P(),
        P(None, None, CH),
        P(None, None, CH),
        P(CH, None),
        P(CH),
        P(CH, None),
    )
    out_specs = P(CTX, CH)
    return jax.shard_map(shards, mesh=fine, in_specs=in_specs, out_specs=out_specs, check_vma=False)
```

time: 346 us -> 254 us (0.73)
  the two profiles are of different devices: /device:TPU:1 before, /device:TPU:2 now
where the time goes in v1:
time: 254 us
  waiting for transfers between devices  158 us (62%)
  blocking collectives  31 us (12%)
  local copies, waits for them, and re-layouts  23.3 us (9%)
  between operations  13.3 us (5%)
  other arithmetic  8.36 us (3%)
  matrix products  8.2 us (3%)
  starting transfers between devices  7.73 us (3%)
  Pallas kernels  4.34 us (2%)
    reduce_scatter x3, waiting for transfers between devices, shards(): split = lax.psum_scatter(split, name, scatter_dimension=0)  106 us
    all_gather x2, waiting for transfers between devices, shards(): stacked = lax.all_gather(stacked, name, axis=0)  49 us
    all_gather x1, blocking collectives, shards(): stacked = lax.all_gather(stacked, name, axis=0)  31 us
    reshape x2, local copies, waits for them, and re-layouts, shards(): split = terms.reshape(tok, *sizes, chans).transpose(3, 2, 1, 0, 4)  10.8 us
    ppermute x2, starting transfers between devices, passed_along(): lax.ppermute(value, axis, [(source, source + steps) for source in range(i...  7.57 us
  transfers between devices with their start and end apart: 7, of which 7 were waited for; matrix products, arithmetic and copies ran while one was open for 3% of the time, Pallas kernels for 0%

profile of v1, /device:TPU:2, one launch (start us, length us, event | category | flops | bytes accessed | tf_op | source)
XLA Modules:
  0.0 253.8 jit_solution(4941209393648174246)
XLA Ops:
  6.5 31.0 %all-gather = bf16[1536,128]{1,0:T(8,128)(2,1)} all-gather(bf16[384,128]{1,0:T(8,128)(2,1)} %param.7), channel_id=2, replica_groups=mesh['z_lo'=4,'y'=4,'z_hi'=4,'x'=4,'core'=2] {'z_hi'}, dimensions={0}, use_global_device_ids=true | all-gather | bytes 491520 | tf_op jit(solution)/shard_map/all_gather | solution.py:74
  37.6 29.4 %all-gather.6.cloned.1.call-done = bf16[16,384,128]{2,1,0:T(8,128)(2,1)} async-done(((bf16[4,384,128]{2,1,0:T(8,128)(2,1)}), bf16[16,384,128]{2,1,0:T(8,128)(2,1)}) %all-gather.6.cloned.1.call-update) | async-done | bytes 1572880 | tf_op jit(solution)/shard_map/all_gather | solution.py:74
  67.1 0.7 copy.30
  67.8 4.7 %copy.32 = bf16[4096,3,128]{0,2,1:T(8,128)(2,1)} copy(bf16[4096,3,128]{2,0,1:T(8,128)(2,1)} %param.9) | data formatting | bytes 6291456 | tf_op args[2]
  72.6 0.1 copy.39
  72.7 0.6 convert_bitcast_fusion.filt_ref
  73.3 19.6 %all-gather.8.cloned.1.call-done = bf16[8,4,384,128]{3,2,1,0:T(8,128)(2,1)} async-done(((bf16[4,4,384,128]{3,2,1,0:T(8,128)(2,1)}), bf16[8,4,384,128]{3,2,1,0:T(8,128)(2,1)}) %all-gather.8.cloned.1.call-update) | async-done | bytes 3145744 | tf_op jit(solution)/shard_map/all_gather | solution.py:74
  92.9 2.7 %fusion = f32[384]{0:T(512)S(1)} fusion(bf16[2,4,4,384,128]{4,3,2,1,0:T(8,128)(2,1)} %bitcast.51), kind=kLoop, calls=%fused_computation.2 | loop fusion | flops 4718208 | bytes 3147264 | tf_op jit(solution)/shard_map/reduce_sum | solution.py:77
  95.7 0.1 copy-done.1
  95.8 2.8 %fusion.3 = bf16[384,4,4,2,128]{4,0,1,2,3:T(8,128)(2,1)} fusion(f32[4,4,2,128]{3,0,1,2:T(4,128)S(1)} %copy.30, f32[384]{0:T(512)S(1)} %add_rsqrt_fusion, bf16[8,4,384,128]{3,2,1,0:T(8,128)(2,1)S(1)} %copy-done.1), kind=kLoop, calls=%fused_computation.5 | loop fusion | flops 6291456 | bytes 6309376 | tf_op jit(solution)/shard_map/convert_element_type | solution.py:78
  98.6 4.7 %copy.31 = bf16[384,4,4,2,128]{0,4,3,2,1:T(8,128)(2,1)} copy(bf16[384,4,4,2,128]{4,0,1,2,3:T(8,128)(2,1)} %fusion.3) | data formatting | bytes 6291456 | tf_op jit(solution)/shard_map/convert_element_type | solution.py:78
  103.2 4.7 %convolution_convert_fusion.1 = bf16[384,384]{1,0:T(8,128)(2,1)S(1)} fusion(bf16[384,4096]{0,1:T(8,128)(2,1)} %bitcast.54, bf16[4096,384]{0,1:T(8,128)(2,1)} %bitcast.53), kind=kOutput, calls=%fused_computation.8 | convolution fusion | flops 1208107008 | bytes 6586368 | tf_op jit(solution)/shard_map/dot_general | solution.py:79
  107.9 3.4 %collective-permute-start = (bf16[2,384]{1,0:T(2,128)(2,1)S(1)}, bf16[2,384]{1,0:T(2,128)(2,1)S(1)}, u32[]{:S(2)}, u32[]{:S(2)}) collective-permute-start(bf16[2,384]{1,0:T(2,128)(2,1)S(1)} %slice.48), channel_id=1, source_target_pairs={{0,32},{32,64},{64,96},{96,128},{128,160},{160,192},{192,224},{224... | collective-permute-start | bytes 4616 | tf_op jit(solution)/shard_map/ppermute | solution.py:18
  111.4 0.2 copy.33
  111.5 0.2 copy.34
  111.8 0.8 collective-permute-done
  112.6 0.1 fusion.5
  112.7 0.2 copy.35
  113.0 1.1 copy.36
  114.0 0.2 copy.37
  114.2 0.2 copy.38
  114.5 1.2 multiply_add_fusion
  115.7 4.2 %collective-permute-start.1 = (bf16[127,128]{1,0:T(8,128)(2,1)S(1)}, bf16[127,128]{1,0:T(8,128)(2,1)S(1)}, u32[]{:S(2)}, u32[]{:S(2)}) collective-permute-start(bf16[127,128]{1,0:T(8,128)(2,1)S(1)} %slice_bitcast_fusion.1), channel_id=1, source_target_pairs={{0,32},{32,64},{64,96},{96,128},{128,160},{160,192},{192,224},{224... | collective-permute-start | bytes 97544 | tf_op jit(solution)/shard_map/ppermute | solution.py:18
  119.9 1.5 collective-permute-done.1
  121.5 0.8 maximum_convert_fusion.ext_ref
  122.3 4.3 %shard_map.73 = f32[384,128]{1,0:T(8,128)} custom-call(f32[512,128]{1,0:T(8,128)} %maximum_convert_fusion.ext_ref, f32[128,128]{1,0:T(8,128)} %convert_bitcast_fusion.filt_ref), custom_call_target="tpu_custom_call" | custom-call | tf_op jit(solution)/shard_map/pallas_call | solution.py:59
  126.6 3.5 %convolution_convert_fusion = bf16[384,4096]{1,0:T(8,128)(2,1)} fusion(bf16[128,4096]{1,0:T(8,128)(2,1)S(1)} %copy-done, f32[384,3,128]{2,0,1:T(8,128)S(1)} %multiply_add_fusion, f32[384,128]{1,0:T(8,128)} %shard_map.73, f32[128]{0:T(128)S(1)} %copy-done.4, bf16[384,1,128]{2,0,1:T(8,128)(2,1)S(1)} %fusion.7), kind=kOutput, calls=%fused_computation.6 | convolution fusion | flops 404471808 | bytes 4686336 | tf_op jit(solution)/shard_map/dot_general | solution.py:91
  130.2 6.1 %reshape.45 = bf16[384,4,4,2,128]{4,3,2,1,0:T(2,128)(2,1)} reshape(bf16[384,4096]{1,0:T(8,128)(2,1)} %convolution_convert_fusion) | data formatting | bytes 6291456 | tf_op jit(solution)/shard_map/reshape | solution.py:93
  136.3 4.7 %copy.48 = bf16[384,4,4,2,128]{4,0,1,2,3:T(8,128)(2,1)} copy(bf16[384,4,4,2,128]{4,3,2,1,0:T(2,128)(2,1)} %reshape.45) | data formatting | bytes 6291456 | tf_op jit(solution)/shard_map/reshape | solution.py:93
  141.1 24.6 %reduce-scatter.4.cloned.1.call-done = bf16[1,4,4,384,128]{4,3,2,1,0:T(8,128)(2,1)} async-done(((bf16[2,4,4,384,128]{4,3,2,1,0:T(8,128)(2,1)}), bf16[1,4,4,384,128]{4,3,2,1,0:T(8,128)(2,1)}) %reduce-scatter.4.cloned.1.call-update) | async-done | bytes 1572880 | tf_op jit(solution)/shard_map/reduce_scatter | solution.py:95
  165.7 36.7 %reduce-scatter.6.cloned.1.call-done = bf16[1,4,384,128]{3,2,1,0:T(8,128)(2,1)} async-done(((bf16[4,4,384,128]{3,2,1,0:T(8,128)(2,1)}), bf16[1,4,384,128]{3,2,1,0:T(8,128)(2,1)}) %reduce-scatter.6.cloned.1.call-update) | async-done | bytes 393232 | tf_op jit(solution)/shard_map/reduce_scatter | solution.py:95
  202.4 44.8 %reduce-scatter.8.cloned.1.call-done = bf16[1,384,128]{2,1,0:T(8,128)(2,1)} async-done(((bf16[4,384,128]{2,1,0:T(8,128)(2,1)}), bf16[1,384,128]{2,1,0:T(8,128)(2,1)}) %reduce-scatter.8.cloned.1.call-update) | async-done | bytes 98320 | tf_op jit(solution)/shard_map/reduce_scatter | solution.py:95
  (28 shorter events, 0.4 us)
Async XLA Ops:
  6.5 120.1 %copy-start = (bf16[128,4096]{1,0:T(8,128)(2,1)S(1)}, bf16[128,4096]{1,0:T(8,128)(2,1)}, u32[]{:S(2)}) copy-start(bf16[128,4096]{1,0:T(8,128)(2,1)} %param.13) | copy-start | bytes 3145732
  6.5 60.5 %all-gather.6.cloned.1.call-start = ((), (), s32[]{:S(2)}) async-start(), calls=%async_computation.6 | async-start | bytes 1966080 | tf_op jit(solution)/shard_map/all_gather | solution.py:74
  37.6 55.3 %all-gather.8.cloned.1.call-start = ((), (), s32[]{:S(2)}) async-start(), calls=%async_computation.7 | async-start | bytes 4718592 | tf_op jit(solution)/shard_map/all_gather | solution.py:74
  67.1 98.6 %reduce-scatter.4.cloned.1.call-start = ((), (), s32[]{:S(2)}) async-start(), calls=%async_computation.3 | async-start | bytes 4718592 | tf_op jit(solution)/shard_map/reduce_scatter | solution.py:95
  67.8 4.7 %copy-start.2 = (bf16[128,128]{1,0:T(8,128)(2,1)S(1)}, bf16[128,128]{1,0:T(8,128)(2,1)}, u32[]{:S(2)}) copy-start(bf16[128,128]{1,0:T(8,128)(2,1)} %param.11) | copy-start | bytes 98308
  67.8 4.8 %copy-start.3 = (f32[3,3,128]{2,1,0:T(4,128)S(1)}, f32[3,3,128]{2,1,0:T(4,128)}, u32[]{:S(2)}) copy-start(f32[3,3,128]{2,1,0:T(4,128)} %param.10) | copy-start | bytes 13828
  92.9 2.8 %copy-start.1 = (bf16[8,4,384,128]{3,2,1,0:T(8,128)(2,1)S(1)}, bf16[8,4,384,128]{3,2,1,0:T(8,128)(2,1)}, u32[]{:S(2)}) copy-start(bf16[8,4,384,128]{3,2,1,0:T(8,128)(2,1)} %all-gather.8.cloned.1.call-done) | copy-start | bytes 9437188
  107.9 4.7 %collective-permute-start = (bf16[2,384]{1,0:T(2,128)(2,1)S(1)}, bf16[2,384]{1,0:T(2,128)(2,1)S(1)}, u32[]{:S(2)}, u32[]{:S(2)}) collective-permute-start(bf16[2,384]{1,0:T(2,128)(2,1)S(1)} %slice.48), channel_id=1, source_target_pairs={{0,32},{32,64},{64,96},{96,128},{128,160},{160,192},{192,224},{224... | collective-permute-start | bytes 4616 | tf_op jit(solution)/shard_map/ppermute | solution.py:18
  114.0 12.6 %copy-start.4 = (f32[128]{0:T(128)S(1)}, f32[128]{0:T(128)}, u32[]{:S(2)}) copy-start(f32[128]{0:T(128)} %param.12) | copy-start | bytes 1540
  115.7 5.8 %collective-permute-start.1 = (bf16[127,128]{1,0:T(8,128)(2,1)S(1)}, bf16[127,128]{1,0:T(8,128)(2,1)S(1)}, u32[]{:S(2)}, u32[]{:S(2)}) collective-permute-start(bf16[127,128]{1,0:T(8,128)(2,1)S(1)} %slice_bitcast_fusion.1), channel_id=1, source_target_pairs={{0,32},{32,64},{64,96},{96,128},{128,160},{160,192},{192,224},{224... | collective-permute-start | bytes 97544 | tf_op jit(solution)/shard_map/ppermute | solution.py:18
  141.0 61.4 %reduce-scatter.6.cloned.1.call-start = ((), (), s32[]{:S(2)}) async-start(), calls=%async_computation.4 | async-start | bytes 1966080 | tf_op jit(solution)/shard_map/reduce_scatter | solution.py:95
  165.7 81.6 %reduce-scatter.8.cloned.1.call-start = ((), (), s32[]{:S(2)}) async-start(), calls=%async_computation.5 | async-start | bytes 491520 | tf_op jit(solution)/shard_map/reduce_scatter | solution.py:95
Sparse Core Ops, SparseCore 0:
  37.7 29.2 all-gather.5
  69.1 23.7 all-gather.7
  141.2 24.4 reduce-scatter.3
  168.6 33.7 reduce-scatter.5
  205.3 41.8 reduce-scatter.7

commit v2 on v1

--- a/solution.py
+++ b/solution.py
@@ -16,6 +16,26 @@
 def passed_along(value, axis, count, steps):
     initial, last = (max(0, -steps), min(count, count - steps))
     return lax.ppermute(value, axis, [(source, source + steps) for source in range(initial, last)])
+
+
+def gathered(block, name, count):
+    index = lax.axis_index(name)
+    out = jnp.zeros((count,) + block.shape, block.dtype)
+    out = lax.dynamic_update_index_in_dim(out, block, index, 0)
+    for shift in range(1, count):
+        got = lax.ppermute(block, name, [(k, (k + shift) % count) for k in range(count)])
+        out = lax.dynamic_update_index_in_dim(out, got, (index - shift) % count, 0)
+    return out
+
+
+def reduced(stack, name, count):
+    index = lax.axis_index(name)
+    total = lax.dynamic_index_in_dim(stack, index, 0, keepdims=False).astype(jnp.float32)
+    for shift in range(1, count):
+        part = lax.dynamic_index_in_dim(stack, (index + shift) % count, 0, keepdims=False)
+        got = lax.ppermute(part, name, [(k, (k + shift) % count) for k in range(count)])
+        total = total + got.astype(jnp.float32)
+    return total
 
 
 def featurize(extended, feat_taps, count):
@@ -70,8 +90,8 @@
     feat_len = feat_taps.shape[1]
     w_flat = w_in.reshape(width, 3 * chans)
     stacked = bases_in
-    for name, _ in CH_PARTS:
-        stacked = lax.all_gather(stacked, name, axis=0)
+    for name, size in CH_PARTS:
+        stacked = gathered(stacked, name, size)
     whole = stacked.transpose(3, 2, 1, 0, 4).reshape(tok, width)
     wide = whole.astype(jnp.float32)
     inverse = lax.rsqrt(jnp.mean(wide * wide, axis=1, keepdims=True) + 1e-05)
@@ -91,8 +111,8 @@
     terms = jnp.dot(gated, w_out, preferred_element_type=jnp.float32).astype(jnp.bfloat16)
     sizes = [size for _, size in CH_PARTS]
     split = terms.reshape(tok, *sizes, chans).transpose(3, 2, 1, 0, 4)
-    for name, _ in CH_PARTS[::-1]:
-        split = lax.psum_scatter(split, name, scatter_dimension=0)
+    for name, size in CH_PARTS[::-1]:
+        split = reduced(split, name, size).astype(jnp.bfloat16)
     return split
 
 

time: 254 us -> 197 us (0.78)
  the two profiles are of different devices: /device:TPU:2 before, /device:TPU:3 now
where the time goes in v2:
time: 197 us; the launch traced here: 196 us
  starting transfers between devices  75 us (38%)
  waiting for transfers between devices  66.9 us (34%)
  local copies, waits for them, and re-layouts  33.5 us (17%)
  other arithmetic  10.1 us (5%)
  matrix products  5.35 us (3%)
  Pallas kernels  4.32 us (2%)
    ppermute x7, waiting for transfers between devices, reduced(): lax.ppermute(part, name, [(k, (k + shift) % count) for k in range(count)])  36.9 us
    ppermute x7, starting transfers between devices, gathered(): lax.ppermute(block, name, [(k, (k + shift) % count) for k in range(count)])  36.7 us
    ppermute x7, starting transfers between devices, reduced(): lax.ppermute(part, name, [(k, (k + shift) % count) for k in range(count)])  31.3 us
    ppermute x7, waiting for transfers between devices, gathered(): lax.ppermute(block, name, [(k, (k + shift) % count) for k in range(count)])  29 us
    dynamic_slice x1, local copies, waits for them, and re-layouts, reduced(): lax.dynamic_index_in_dim(stack, index, 0, keepdims=False)  10.9 us
    unnamed x20, local copies, waits for them, and re-layouts  10.2 us
    ppermute x2, starting transfers between devices, passed_along(): lax.ppermute(value, axis, [(source, source + steps) for source in range(i...  6.99 us
    reshape x1, local copies, waits for them, and re-layouts, shards(): split = terms.reshape(tok, *sizes, chans).transpose(3, 2, 1, 0, 4)  6.08 us
  transfers between devices with their start and end apart: 16, of which 13 were waited for; matrix products, arithmetic and copies ran while one was open for 4% of the time, Pallas kernels for 0%

profile of v2, /device:TPU:3, one launch (start us, length us, event | category | flops | bytes accessed | tf_op | source)
XLA Modules:
  0.0 195.8 jit_solution(12565900330041448057)
XLA Ops:
  1.1 8.8 %collective-permute-start = (bf16[384,128]{0,1:T(8,128)(2,1)S(1)}, bf16[384,128]{0,1:T(8,128)(2,1)S(1)}, u32[]{:S(2)}, u32[]{:S(2)}) collective-permute-start(bf16[384,128]{0,1:T(8,128)(2,1)S(1)} %copy.11), channel_id=1, source_target_pairs={{0,8},{8,16},{16,24},{24,0},{1,9},{9,17},{17,25},{25,1},{2,10},{10... | collective-permute-start | bytes 294920 | tf_op jit(solution)/shard_map/ppermute | solution.py:26
  9.9 10.6 %collective-permute-start.1 = (bf16[384,128]{0,1:T(8,128)(2,1)S(1)}, bf16[384,128]{0,1:T(8,128)(2,1)S(1)}, u32[]{:S(2)}, u32[]{:S(2)}) collective-permute-start(bf16[384,128]{0,1:T(8,128)(2,1)S(1)} %copy.11), channel_id=1, source_target_pairs={{0,16},{8,24},{16,0},{24,8},{1,17},{9,25},{17,1},{25,9},{2,18},{10... | collective-permute-start | bytes 294920 | tf_op jit(solution)/shard_map/ppermute | solution.py:26
  20.6 5.2 %collective-permute-start.2 = (bf16[384,128]{0,1:T(8,128)(2,1)S(1)}, bf16[384,128]{0,1:T(8,128)(2,1)S(1)}, u32[]{:S(2)}, u32[]{:S(2)}) collective-permute-start(bf16[384,128]{0,1:T(8,128)(2,1)S(1)} %copy.11), channel_id=1, source_target_pairs={{0,24},{8,0},{16,8},{24,16},{1,25},{9,1},{17,9},{25,17},{2,26},{10... | collective-permute-start | bytes 294920 | tf_op jit(solution)/shard_map/ppermute | solution.py:26
  25.9 5.6 %collective-permute-done.1 = bf16[384,128]{0,1:T(8,128)(2,1)S(1)} collective-permute-done((bf16[384,128]{0,1:T(8,128)(2,1)S(1)}, bf16[384,128]{0,1:T(8,128)(2,1)S(1)}, u32[]{:S(2)}, u32[]{:S(2)}) %collective-permute-start.1) | collective-permute-done | bytes 98336 | tf_op jit(solution)/shard_map/ppermute | solution.py:26
  31.6 7.4 %collective-permute-done.2 = bf16[384,128]{0,1:T(8,128)(2,1)S(1)} collective-permute-done((bf16[384,128]{0,1:T(8,128)(2,1)S(1)}, bf16[384,128]{0,1:T(8,128)(2,1)S(1)}, u32[]{:S(2)}, u32[]{:S(2)}) %collective-permute-start.2) | collective-permute-done | bytes 98336 | tf_op jit(solution)/shard_map/ppermute | solution.py:26
  39.1 3.1 %collective-permute-start.3 = (bf16[4,384,128]{1,2,0:T(8,128)(2,1)S(1)}, bf16[4,384,128]{1,2,0:T(8,128)(2,1)S(1)}, u32[]{:S(2)}, u32[]{:S(2)}) collective-permute-start(bf16[4,384,128]{1,2,0:T(8,128)(2,1)S(1)} %bitcast_dynamic-update-slice_fusion.6), channel_id=1, source_target_pairs={{0,2},{2,4},{4,6},{6,0},{1,3},{3,5},{5,7},{7,1},{8,10},{10,12},{12... | collective-permute-start | bytes 1179656 | tf_op jit(solution)/shard_map/ppermute | solution.py:26
  42.2 2.7 %collective-permute-start.4 = (bf16[4,384,128]{1,2,0:T(8,128)(2,1)S(1)}, bf16[4,384,128]{1,2,0:T(8,128)(2,1)S(1)}, u32[]{:S(2)}, u32[]{:S(2)}) collective-permute-start(bf16[4,384,128]{1,2,0:T(8,128)(2,1)S(1)} %bitcast_dynamic-update-slice_fusion.6), channel_id=1, source_target_pairs={{0,4},{2,6},{4,0},{6,2},{1,5},{3,7},{5,1},{7,3},{8,12},{10,14},{12... | collective-permute-start | bytes 1179656 | tf_op jit(solution)/shard_map/ppermute | solution.py:26
  45.0 3.8 %collective-permute-start.5 = (bf16[4,384,128]{1,2,0:T(8,128)(2,1)S(1)}, bf16[4,384,128]{1,2,0:T(8,128)(2,1)S(1)}, u32[]{:S(2)}, u32[]{:S(2)}) collective-permute-start(bf16[4,384,128]{1,2,0:T(8,128)(2,1)S(1)} %bitcast_dynamic-update-slice_fusion.6), channel_id=1, source_target_pairs={{0,6},{2,0},{4,2},{6,4},{1,7},{3,1},{5,3},{7,5},{8,14},{10,8},{12,... | collective-permute-start | bytes 1179656 | tf_op jit(solution)/shard_map/ppermute | solution.py:26
  51.1 4.4 %collective-permute-done.4 = bf16[4,384,128]{1,2,0:T(8,128)(2,1)S(1)} collective-permute-done((bf16[4,384,128]{1,2,0:T(8,128)(2,1)S(1)}, bf16[4,384,128]{1,2,0:T(8,128)(2,1)S(1)}, u32[]{:S(2)}, u32[]{:S(2)}) %collective-permute-start.4) | collective-permute-done | bytes 393248 | tf_op jit(solution)/shard_map/ppermute | solution.py:26
  55.5 9.6 %collective-permute-done.5 = bf16[4,384,128]{1,2,0:T(8,128)(2,1)S(1)} collective-permute-done((bf16[4,384,128]{1,2,0:T(8,128)(2,1)S(1)}, bf16[4,384,128]{1,2,0:T(8,128)(2,1)S(1)}, u32[]{:S(2)}, u32[]{:S(2)}) %collective-permute-start.5) | collective-permute-done | bytes 393248 | tf_op jit(solution)/shard_map/ppermute | solution.py:26
  65.2 2.4 %collective-permute-start.6 = (bf16[4,4,384,128]{2,3,0,1:T(8,128)(2,1)S(1)}, bf16[4,4,384,128]{2,3,0,1:T(8,128)(2,1)}, u32[]{:S(2)}, u32[]{:S(2)}) collective-permute-start(bf16[4,4,384,128]{2,3,0,1:T(8,128)(2,1)S(1)} %bitcast_dynamic-update-slice_fusion.5), channel_id=1, source_target_pairs={{0,1},{1,0},{2,3},{3,2},{4,5},{5,4},{6,7},{7,6},{8,9},{9,8},{10,11... | collective-permute-start | bytes 4718600 | tf_op jit(solution)/shard_map/ppermute | solution.py:26
  67.6 4.7 %copy.19 = bf16[4096,3,128]{0,2,1:T(8,128)(2,1)} copy(bf16[4096,3,128]{2,0,1:T(8,128)(2,1)} %param.9) | data formatting | bytes 6291456 | tf_op args[2]
  80.3 3.2 %collective-permute-start.7 = (bf16[2,384]{1,0:T(2,128)(2,1)S(1)}, bf16[2,384]{1,0:T(2,128)(2,1)S(1)}, u32[]{:S(2)}, u32[]{:S(2)}) collective-permute-start(bf16[2,384]{1,0:T(2,128)(2,1)S(1)} %slice.48), channel_id=1, source_target_pairs={{0,32},{32,64},{64,96},{96,128},{128,160},{160,192},{192,224},{224... | collective-permute-start | bytes 4616 | tf_op jit(solution)/shard_map/ppermute | solution.py:18
  87.3 3.8 %collective-permute-start.8 = (bf16[127,128]{1,0:T(8,128)(2,1)S(1)}, bf16[127,128]{1,0:T(8,128)(2,1)S(1)}, u32[]{:S(2)}, u32[]{:S(2)}) collective-permute-start(bf16[127,128]{1,0:T(8,128)(2,1)S(1)} %slice_bitcast_fusion.1), channel_id=1, source_target_pairs={{0,32},{32,64},{64,96},{96,128},{128,160},{160,192},{192,224},{224... | collective-permute-start | bytes 97544 | tf_op jit(solution)/shard_map/ppermute | solution.py:18
  92.8 4.3 %shard_map.73 = f32[384,128]{1,0:T(8,128)} custom-call(f32[512,128]{1,0:T(8,128)} %maximum_convert_fusion.ext_ref, f32[128,128]{1,0:T(8,128)} %convert_bitcast_fusion.filt_ref), custom_call_target="tpu_custom_call" | custom-call | tf_op jit(solution)/shard_map/pallas_call | solution.py:79
  97.1 3.5 %convolution_convert_fusion = bf16[384,4096]{1,0:T(8,128)(2,1)} fusion(bf16[128,4096]{1,0:T(8,128)(2,1)S(1)} %copy-done, f32[384,3,128]{2,0,1:T(8,128)S(1)} %multiply_add_fusion, f32[384,128]{1,0:T(8,128)} %shard_map.73, f32[128]{0:T(128)S(1)} %copy-done.6, bf16[384,1,128]{2,0,1:T(8,128)(2,1)S(1)} %fusion.11), kind=kOutput, calls=%fused_computation.6 | convolution fusion | flops 404471808 | bytes 4686336 | tf_op jit(solution)/shard_map/dot_general | solution.py:111
  100.6 6.1 %reshape.51 = bf16[384,4,4,2,128]{4,3,2,1,0:T(2,128)(2,1)} reshape(bf16[384,4096]{1,0:T(8,128)(2,1)} %convolution_convert_fusion) | data formatting | bytes 6291456 | tf_op jit(solution)/shard_map/reshape | solution.py:113
  106.7 10.9 %constant_dynamic-slice_fusion.1 = (bf16[384,4,4,1,128]{4,3,2,1,0:T(2,128)(2,1)}, bf16[384,4,4,1,128]{4,3,2,1,0:T(2,128)(2,1)S(1)}) fusion(bf16[384,4,4,2,128]{4,3,2,1,0:T(2,128)(2,1)} %reshape.51, s32[]{:T(128)S(6)} %select_n.133, s32[]{:T(128)S(6)} %select_n.137), kind=kLoop, calls=%fused_computation.52 | loop fusion | bytes 6291464 | tf_op jit(solution)/shard_map/jit(dynamic_index_in_dim)/dynamic_slice | solution.py:33
  119.8 3.9 %collective-permute-start.9 = (bf16[4,4,384,128]{3,2,1,0:T(8,128)(2,1)}, bf16[4,4,384,128]{3,2,1,0:T(8,128)(2,1)S(1)}, u32[]{:S(2)}, u32[]{:S(2)}) collective-permute-start(bf16[4,4,384,128]{3,2,1,0:T(8,128)(2,1)} %bitcast.95), channel_id=1, source_target_pairs={{0,1},{1,0},{2,3},{3,2},{4,5},{5,4},{6,7},{7,6},{8,9},{9,8},{10,11... | collective-permute-start | bytes 4718600 | tf_op jit(solution)/shard_map/ppermute | solution.py:36
  123.8 3.2 %collective-permute-done.9 = bf16[4,4,384,128]{3,2,1,0:T(8,128)(2,1)S(1)} collective-permute-done((bf16[4,4,384,128]{3,2,1,0:T(8,128)(2,1)}, bf16[4,4,384,128]{3,2,1,0:T(8,128)(2,1)S(1)}, u32[]{:S(2)}, u32[]{:S(2)}) %collective-permute-start.9) | collective-permute-done | bytes 1572896 | tf_op jit(solution)/shard_map/ppermute | solution.py:36
  128.2 3.4 %fusion.4 = bf16[4,4,384,128]{3,2,1,0:T(8,128)(2,1)S(1)} fusion(bf16[4,4,384,128]{3,2,1,0:T(8,128)(2,1)} %copy-done.2, bf16[384,4,4,1,128]{4,3,2,1,0:T(2,128)(2,1)} %get-tuple-element.5), kind=kLoop, calls=%fused_computation.8 | loop fusion | flops 3145728 | bytes 4718592 | tf_op jit(solution)/shard_map/convert_element_type | solution.py:115
  132.4 2.2 %collective-permute-start.10 = (bf16[4,384,128]{2,1,0:T(8,128)(2,1)}, bf16[4,384,128]{2,1,0:T(8,128)(2,1)}, u32[]{:S(2)}, u32[]{:S(2)}) collective-permute-start(bf16[4,384,128]{2,1,0:T(8,128)(2,1)} %get-tuple-element.7), channel_id=1, source_target_pairs={{0,2},{2,4},{4,6},{6,0},{1,3},{3,5},{5,7},{7,1},{8,10},{10,12},{12... | collective-permute-start | bytes 1179656 | tf_op jit(solution)/shard_map/ppermute | solution.py:36
  134.7 2.7 %collective-permute-start.11 = (bf16[4,384,128]{2,1,0:T(8,128)(2,1)S(1)}, bf16[4,384,128]{2,1,0:T(8,128)(2,1)}, u32[]{:S(2)}, u32[]{:S(2)}) collective-permute-start(bf16[4,384,128]{2,1,0:T(8,128)(2,1)S(1)} %get-tuple-element.9), channel_id=1, source_target_pairs={{0,4},{2,6},{4,0},{6,2},{1,5},{3,7},{5,1},{7,3},{8,12},{10,14},{12... | collective-permute-start | bytes 1179656 | tf_op jit(solution)/shard_map/ppermute | solution.py:36
  137.4 3.7 %collective-permute-start.12 = (bf16[4,384,128]{2,1,0:T(8,128)(2,1)S(1)}, bf16[4,384,128]{2,1,0:T(8,128)(2,1)}, u32[]{:S(2)}, u32[]{:S(2)}) collective-permute-start(bf16[4,384,128]{2,1,0:T(8,128)(2,1)S(1)} %get-tuple-element.8), channel_id=1, source_target_pairs={{0,6},{2,0},{4,2},{6,4},{1,7},{3,1},{5,3},{7,5},{8,14},{10,8},{12,... | collective-permute-start | bytes 1179656 | tf_op jit(solution)/shard_map/ppermute | solution.py:36
  141.1 3.8 %collective-permute-done.10 = bf16[4,384,128]{2,1,0:T(8,128)(2,1)} collective-permute-done((bf16[4,384,128]{2,1,0:T(8,128)(2,1)}, bf16[4,384,128]{2,1,0:T(8,128)(2,1)}, u32[]{:S(2)}, u32[]{:S(2)}) %collective-permute-start.10) | collective-permute-done | bytes 393248 | tf_op jit(solution)/shard_map/ppermute | solution.py:36
  145.0 3.2 %collective-permute-done.11 = bf16[4,384,128]{2,1,0:T(8,128)(2,1)} collective-permute-done((bf16[4,384,128]{2,1,0:T(8,128)(2,1)S(1)}, bf16[4,384,128]{2,1,0:T(8,128)(2,1)}, u32[]{:S(2)}, u32[]{:S(2)}) %collective-permute-start.11) | collective-permute-done | bytes 393248 | tf_op jit(solution)/shard_map/ppermute | solution.py:36
  148.2 9.4 %collective-permute-done.12 = bf16[4,384,128]{2,1,0:T(8,128)(2,1)} collective-permute-done((bf16[4,384,128]{2,1,0:T(8,128)(2,1)S(1)}, bf16[4,384,128]{2,1,0:T(8,128)(2,1)}, u32[]{:S(2)}, u32[]{:S(2)}) %collective-permute-start.12) | collective-permute-done | bytes 393248 | tf_op jit(solution)/shard_map/ppermute | solution.py:36
  159.1 5.5 %collective-permute-start.13 = (bf16[384,128]{1,0:T(8,128)(2,1)S(1)}, bf16[384,128]{1,0:T(8,128)(2,1)S(1)}, u32[]{:S(2)}, u32[]{:S(2)}) collective-permute-start(bf16[384,128]{1,0:T(8,128)(2,1)S(1)} %get-tuple-element.10), channel_id=1, source_target_pairs={{0,8},{8,16},{16,24},{24,0},{1,9},{9,17},{17,25},{25,1},{2,10},{10... | collective-permute-start | bytes 294920 | tf_op jit(solution)/shard_map/ppermute | solution.py:36
  164.6 8.5 %collective-permute-start.14 = (bf16[384,128]{1,0:T(8,128)(2,1)S(1)}, bf16[384,128]{1,0:T(8,128)(2,1)S(1)}, u32[]{:S(2)}, u32[]{:S(2)}) collective-permute-start(bf16[384,128]{1,0:T(8,128)(2,1)S(1)} %get-tuple-element.12), channel_id=1, source_target_pairs={{0,16},{8,24},{16,0},{24,8},{1,17},{9,25},{17,1},{25,9},{2,18},{10... | collective-permute-start | bytes 294920 | tf_op jit(solution)/shard_map/ppermute | solution.py:36
  173.2 4.8 %collective-permute-start.15 = (bf16[384,128]{1,0:T(8,128)(2,1)S(1)}, bf16[384,128]{1,0:T(8,128)(2,1)S(1)}, u32[]{:S(2)}, u32[]{:S(2)}) collective-permute-start(bf16[384,128]{1,0:T(8,128)(2,1)S(1)} %get-tuple-element.11), channel_id=1, source_target_pairs={{0,24},{8,0},{16,8},{24,16},{1,25},{9,1},{17,9},{25,17},{2,26},{10... | collective-permute-start | bytes 294920 | tf_op jit(solution)/shard_map/ppermute | solution.py:36
  177.9 8.8 %collective-permute-done.14 = bf16[384,128]{1,0:T(8,128)(2,1)S(1)} collective-permute-done((bf16[384,128]{1,0:T(8,128)(2,1)S(1)}, bf16[384,128]{1,0:T(8,128)(2,1)S(1)}, u32[]{:S(2)}, u32[]{:S(2)}) %collective-permute-start.14) | collective-permute-done | bytes 98336 | tf_op jit(solution)/shard_map/ppermute | solution.py:36
  186.7 8.4 %collective-permute-done.15 = bf16[384,128]{1,0:T(8,128)(2,1)S(1)} collective-permute-done((bf16[384,128]{1,0:T(8,128)(2,1)S(1)}, bf16[384,128]{1,0:T(8,128)(2,1)S(1)}, u32[]{:S(2)}, u32[]{:S(2)}) %collective-permute-start.15) | collective-permute-done | bytes 98336 | tf_op jit(solution)/shard_map/ppermute | solution.py:36
  (62 shorter events, 23.3 us)
Async XLA Ops:
  0.0 97.1 %copy-start = (bf16[128,4096]{1,0:T(8,128)(2,1)S(1)}, bf16[128,4096]{1,0:T(8,128)(2,1)}, u32[]{:S(2)}) copy-start(bf16[128,4096]{1,0:T(8,128)(2,1)} %param.13) | copy-start | bytes 3145732
  1.1 24.8 %collective-permute-start = (bf16[384,128]{0,1:T(8,128)(2,1)S(1)}, bf16[384,128]{0,1:T(8,128)(2,1)S(1)}, u32[]{:S(2)}, u32[]{:S(2)}) collective-permute-start(bf16[384,128]{0,1:T(8,128)(2,1)S(1)} %copy.11), channel_id=1, source_target_pairs={{0,8},{8,16},{16,24},{24,0},{1,9},{9,17},{17,25},{25,1},{2,10},{10... | collective-permute-start | bytes 294920 | tf_op jit(solution)/shard_map/ppermute | solution.py:26
  9.9 21.6 %collective-permute-start.1 = (bf16[384,128]{0,1:T(8,128)(2,1)S(1)}, bf16[384,128]{0,1:T(8,128)(2,1)S(1)}, u32[]{:S(2)}, u32[]{:S(2)}) collective-permute-start(bf16[384,128]{0,1:T(8,128)(2,1)S(1)} %copy.11), channel_id=1, source_target_pairs={{0,16},{8,24},{16,0},{24,8},{1,17},{9,25},{17,1},{25,9},{2,18},{10... | collective-permute-start | bytes 294920 | tf_op jit(solution)/shard_map/ppermute | solution.py:26
  20.6 18.5 %collective-permute-start.2 = (bf16[384,128]{0,1:T(8,128)(2,1)S(1)}, bf16[384,128]{0,1:T(8,128)(2,1)S(1)}, u32[]{:S(2)}, u32[]{:S(2)}) collective-permute-start(bf16[384,128]{0,1:T(8,128)(2,1)S(1)} %copy.11), channel_id=1, source_target_pairs={{0,24},{8,0},{16,8},{24,16},{1,25},{9,1},{17,9},{25,17},{2,26},{10... | collective-permute-start | bytes 294920 | tf_op jit(solution)/shard_map/ppermute | solution.py:26
  39.1 12.0 %collective-permute-start.3 = (bf16[4,384,128]{1,2,0:T(8,128)(2,1)S(1)}, bf16[4,384,128]{1,2,0:T(8,128)(2,1)S(1)}, u32[]{:S(2)}, u32[]{:S(2)}) collective-permute-start(bf16[4,384,128]{1,2,0:T(8,128)(2,1)S(1)} %bitcast_dynamic-update-slice_fusion.6), channel_id=1, source_target_pairs={{0,2},{2,4},{4,6},{6,0},{1,3},{3,5},{5,7},{7,1},{8,10},{10,12},{12... | collective-permute-start | bytes 1179656 | tf_op jit(solution)/shard_map/ppermute | solution.py:26
  42.2 13.2 %collective-permute-start.4 = (bf16[4,384,128]{1,2,0:T(8,128)(2,1)S(1)}, bf16[4,384,128]{1,2,0:T(8,128)(2,1)S(1)}, u32[]{:S(2)}, u32[]{:S(2)}) collective-permute-start(bf16[4,384,128]{1,2,0:T(8,128)(2,1)S(1)} %bitcast_dynamic-update-slice_fusion.6), channel_id=1, source_target_pairs={{0,4},{2,6},{4,0},{6,2},{1,5},{3,7},{5,1},{7,3},{8,12},{10,14},{12... | collective-permute-start | bytes 1179656 | tf_op jit(solution)/shard_map/ppermute | solution.py:26
  45.0 20.1 %collective-permute-start.5 = (bf16[4,384,128]{1,2,0:T(8,128)(2,1)S(1)}, bf16[4,384,128]{1,2,0:T(8,128)(2,1)S(1)}, u32[]{:S(2)}, u32[]{:S(2)}) collective-permute-start(bf16[4,384,128]{1,2,0:T(8,128)(2,1)S(1)} %bitcast_dynamic-update-slice_fusion.6), channel_id=1, source_target_pairs={{0,6},{2,0},{4,2},{6,4},{1,7},{3,1},{5,3},{7,5},{8,14},{10,8},{12,... | collective-permute-start | bytes 1179656 | tf_op jit(solution)/shard_map/ppermute | solution.py:26
  65.2 8.8 %collective-permute-start.6 = (bf16[4,4,384,128]{2,3,0,1:T(8,128)(2,1)S(1)}, bf16[4,4,384,128]{2,3,0,1:T(8,128)(2,1)}, u32[]{:S(2)}, u32[]{:S(2)}) collective-permute-start(bf16[4,4,384,128]{2,3,0,1:T(8,128)(2,1)S(1)} %bitcast_dynamic-update-slice_fusion.5), channel_id=1, source_target_pairs={{0,1},{1,0},{2,3},{3,2},{4,5},{5,4},{6,7},{7,6},{8,9},{9,8},{10,11... | collective-permute-start | bytes 4718600 | tf_op jit(solution)/shard_map/ppermute | solution.py:26
  67.6 4.7 %copy-start.3 = (bf16[128,128]{1,0:T(8,128)(2,1)S(1)}, bf16[128,128]{1,0:T(8,128)(2,1)}, u32[]{:S(2)}) copy-start(bf16[128,128]{1,0:T(8,128)(2,1)} %param.11) | copy-start | bytes 98308
  67.6 4.8 %copy-start.5 = (f32[3,3,128]{2,1,0:T(4,128)S(1)}, f32[3,3,128]{2,1,0:T(4,128)}, u32[]{:S(2)}) copy-start(f32[3,3,128]{2,1,0:T(4,128)} %param.10) | copy-start | bytes 13828
  73.9 2.6 %copy-start.4 = (f32[4096]{0:T(1024)S(1)}, f32[4096]{0:T(1024)}, u32[]{:S(2)}) copy-start(f32[4096]{0:T(1024)} %param.8) | copy-start | bytes 49156
  76.5 1.9 copy-start.1
  80.3 3.9 %collective-permute-start.7 = (bf16[2,384]{1,0:T(2,128)(2,1)S(1)}, bf16[2,384]{1,0:T(2,128)(2,1)S(1)}, u32[]{:S(2)}, u32[]{:S(2)}) collective-permute-start(bf16[2,384]{1,0:T(2,128)(2,1)S(1)} %slice.48), channel_id=1, source_target_pairs={{0,32},{32,64},{64,96},{96,128},{128,160},{160,192},{192,224},{224... | collective-permute-start | bytes 4616 | tf_op jit(solution)/shard_map/ppermute | solution.py:18
  85.6 11.5 %copy-start.6 = (f32[128]{0:T(128)S(1)}, f32[128]{0:T(128)}, u32[]{:S(2)}) copy-start(f32[128]{0:T(128)} %param.12) | copy-start | bytes 1540
  87.3 4.6 %collective-permute-start.8 = (bf16[127,128]{1,0:T(8,128)(2,1)S(1)}, bf16[127,128]{1,0:T(8,128)(2,1)S(1)}, u32[]{:S(2)}, u32[]{:S(2)}) collective-permute-start(bf16[127,128]{1,0:T(8,128)(2,1)S(1)} %slice_bitcast_fusion.1), channel_id=1, source_target_pairs={{0,32},{32,64},{64,96},{96,128},{128,160},{160,192},{192,224},{224... | collective-permute-start | bytes 97544 | tf_op jit(solution)/shard_map/ppermute | solution.py:18
  119.8 7.1 %collective-permute-start.9 = (bf16[4,4,384,128]{3,2,1,0:T(8,128)(2,1)}, bf16[4,4,384,128]{3,2,1,0:T(8,128)(2,1)S(1)}, u32[]{:S(2)}, u32[]{:S(2)}) collective-permute-start(bf16[4,4,384,128]{3,2,1,0:T(8,128)(2,1)} %bitcast.95), channel_id=1, source_target_pairs={{0,1},{1,0},{2,3},{3,2},{4,5},{5,4},{6,7},{7,6},{8,9},{9,8},{10,11... | collective-permute-start | bytes 4718600 | tf_op jit(solution)/shard_map/ppermute | solution.py:36
  127.0 1.2 copy-start.2
  132.4 12.5 %collective-permute-start.10 = (bf16[4,384,128]{2,1,0:T(8,128)(2,1)}, bf16[4,384,128]{2,1,0:T(8,128)(2,1)}, u32[]{:S(2)}, u32[]{:S(2)}) collective-permute-start(bf16[4,384,128]{2,1,0:T(8,128)(2,1)} %get-tuple-element.7), channel_id=1, source_target_pairs={{0,2},{2,4},{4,6},{6,0},{1,3},{3,5},{5,7},{7,1},{8,10},{10,12},{12... | collective-permute-start | bytes 1179656 | tf_op jit(solution)/shard_map/ppermute | solution.py:36
  134.7 13.6 %collective-permute-start.11 = (bf16[4,384,128]{2,1,0:T(8,128)(2,1)S(1)}, bf16[4,384,128]{2,1,0:T(8,128)(2,1)}, u32[]{:S(2)}, u32[]{:S(2)}) collective-permute-start(bf16[4,384,128]{2,1,0:T(8,128)(2,1)S(1)} %get-tuple-element.9), channel_id=1, source_target_pairs={{0,4},{2,6},{4,0},{6,2},{1,5},{3,7},{5,1},{7,3},{8,12},{10,14},{12... | collective-permute-start | bytes 1179656 | tf_op jit(solution)/shard_map/ppermute | solution.py:36
  137.4 20.2 %collective-permute-start.12 = (bf16[4,384,128]{2,1,0:T(8,128)(2,1)S(1)}, bf16[4,384,128]{2,1,0:T(8,128)(2,1)}, u32[]{:S(2)}, u32[]{:S(2)}) collective-permute-start(bf16[4,384,128]{2,1,0:T(8,128)(2,1)S(1)} %get-tuple-element.8), channel_id=1, source_target_pairs={{0,6},{2,0},{4,2},{6,4},{1,7},{3,1},{5,3},{7,5},{8,14},{10,8},{12,... | collective-permute-start | bytes 1179656 | tf_op jit(solution)/shard_map/ppermute | solution.py:36
  159.1 18.8 %collective-permute-start.13 = (bf16[384,128]{1,0:T(8,128)(2,1)S(1)}, bf16[384,128]{1,0:T(8,128)(2,1)S(1)}, u32[]{:S(2)}, u32[]{:S(2)}) collective-permute-start(bf16[384,128]{1,0:T(8,128)(2,1)S(1)} %get-tuple-element.10), channel_id=1, source_target_pairs={{0,8},{8,16},{16,24},{24,0},{1,9},{9,17},{17,25},{25,1},{2,10},{10... | collective-permute-start | bytes 294920 | tf_op jit(solution)/shard_map/ppermute | solution.py:36
  164.6 22.1 %collective-permute-start.14 = (bf16[384,128]{1,0:T(8,128)(2,1)S(1)}, bf16[384,128]{1,0:T(8,128)(2,1)S(1)}, u32[]{:S(2)}, u32[]{:S(2)}) collective-permute-start(bf16[384,128]{1,0:T(8,128)(2,1)S(1)} %get-tuple-element.12), channel_id=1, source_target_pairs={{0,16},{8,24},{16,0},{24,8},{1,17},{9,25},{17,1},{25,9},{2,18},{10... | collective-permute-start | bytes 294920 | tf_op jit(solution)/shard_map/ppermute | solution.py:36
  173.2 22.0 %collective-permute-start.15 = (bf16[384,128]{1,0:T(8,128)(2,1)S(1)}, bf16[384,128]{1,0:T(8,128)(2,1)S(1)}, u32[]{:S(2)}, u32[]{:S(2)}) collective-permute-start(bf16[384,128]{1,0:T(8,128)(2,1)S(1)} %get-tuple-element.11), channel_id=1, source_target_pairs={{0,24},{8,0},{16,8},{24,16},{1,25},{9,1},{17,9},{25,17},{2,26},{10... | collective-permute-start | bytes 294920 | tf_op jit(solution)/shard_map/ppermute | solution.py:36

commit v3 on v2

--- a/solution.py
+++ b/solution.py
@@ -18,24 +18,44 @@
     return lax.ppermute(value, axis, [(source, source + steps) for source in range(initial, last)])
 
 
+def shifted(value, name, count, steps):
+    return lax.ppermute(value, name, [(k, (k + steps) % count) for k in range(count)])
+
+
+def halves(value):
+    half = value.shape[-2] // 2
+    return value[..., :half, :], value[..., half:, :]
+
+
 def gathered(block, name, count):
     index = lax.axis_index(name)
     out = jnp.zeros((count,) + block.shape, block.dtype)
     out = lax.dynamic_update_index_in_dim(out, block, index, 0)
-    for shift in range(1, count):
-        got = lax.ppermute(block, name, [(k, (k + shift) % count) for k in range(count)])
-        out = lax.dynamic_update_index_in_dim(out, got, (index - shift) % count, 0)
-    return out
+    if count == 2:
+        return lax.dynamic_update_index_in_dim(out, shifted(block, name, 2, 1), 1 - index, 0)
+    left = shifted(block, name, count, 1)
+    right = shifted(block, name, count, -1)
+    far = jnp.concatenate(
+        [shifted(halves(left)[0], name, count, 1), shifted(halves(right)[1], name, count, -1)], axis=-2
+    )
+    out = lax.dynamic_update_index_in_dim(out, left, (index - 1) % count, 0)
+    out = lax.dynamic_update_index_in_dim(out, right, (index + 1) % count, 0)
+    return lax.dynamic_update_index_in_dim(out, far, (index + 2) % count, 0)
 
 
 def reduced(stack, name, count):
-    index = lax.axis_index(name)
-    total = lax.dynamic_index_in_dim(stack, index, 0, keepdims=False).astype(jnp.float32)
-    for shift in range(1, count):
-        part = lax.dynamic_index_in_dim(stack, (index + shift) % count, 0, keepdims=False)
-        got = lax.ppermute(part, name, [(k, (k + shift) % count) for k in range(count)])
-        total = total + got.astype(jnp.float32)
-    return total
+    own = stack[0].astype(jnp.float32)
+    if count == 2:
+        return own + shifted(stack[1], name, 2, 1).astype(jnp.float32)
+    far_a, far_b = halves(stack[2])
+    from_left = shifted(far_a, name, count, 1).astype(jnp.float32)
+    from_right = shifted(far_b, name, count, -1).astype(jnp.float32)
+    next_a, next_b = halves(stack[1])
+    prev_a, prev_b = halves(stack[3])
+    to_next = jnp.concatenate([(next_a.astype(jnp.float32) + from_left).astype(jnp.bfloat16), next_b], axis=-2)
+    to_prev = jnp.concatenate([prev_a, (prev_b.astype(jnp.float32) + from_right).astype(jnp.bfloat16)], axis=-2)
+    total = own + shifted(to_next, name, count, 1).astype(jnp.float32)
+    return total + shifted(to_prev, name, count, -1).astype(jnp.float32)
 
 
 def featurize(extended, feat_taps, count):
@@ -108,9 +128,14 @@
     ).astype(jnp.float32)
     filtered = causal_filter(extended, long_filter.astype(jnp.float32).T)
     gated = (query * (filtered + skip_gain * product.astype(jnp.float32))).astype(jnp.bfloat16)
-    terms = jnp.dot(gated, w_out, preferred_element_type=jnp.float32).astype(jnp.bfloat16)
     sizes = [size for _, size in CH_PARTS]
-    split = terms.reshape(tok, *sizes, chans).transpose(3, 2, 1, 0, 4)
+    blocks = w_out.reshape(chans, *sizes, chans)
+    for axis, (name, _) in enumerate(CH_PARTS):
+        blocks = jnp.roll(blocks, -lax.axis_index(name), axis=axis + 1)
+    blocks = blocks.transpose(3, 2, 1, 0, 4)
+    split = jnp.einsum(
+        "tk,cxzki->cxzti", gated, blocks, preferred_element_type=jnp.float32
+    ).astype(jnp.bfloat16)
     for name, size in CH_PARTS[::-1]:
         split = reduced(split, name, size).astype(jnp.bfloat16)
     return split

time: 197 us -> 174 us (0.88)
  the two profiles are of different devices: /device:TPU:3 before, /device:TPU:102 now
where the time goes in v3:
time: 174 us
  starting transfers between devices  74.9 us (43%)
  waiting for transfers between devices  67.9 us (39%)
  local copies, waits for them, and re-layouts  14.6 us (8%)
  other arithmetic  6.58 us (4%)
  matrix products  4.39 us (3%)
  Pallas kernels  4.33 us (2%)
    ppermute x18, starting transfers between devices, shifted(): lax.ppermute(value, name, [(k, (k + steps) % count) for k in range(count)])  69.5 us
    ppermute x18, waiting for transfers between devices, shifted(): lax.ppermute(value, name, [(k, (k + steps) % count) for k in range(count)])  58.3 us
    ppermute x2, waiting for transfers between devices, passed_along(): lax.ppermute(value, axis, [(source, source + steps) for source in range(i...  9.55 us
    unnamed x16, local copies, waits for them, and re-layouts  8.46 us
    ppermute x2, starting transfers between devices, passed_along(): lax.ppermute(value, axis, [(source, source + steps) for source in range(i...  5.41 us
    pallas_call x1, Pallas kernels, causal_filter(): pl.pallas_call(filter_kernel, out_shape=jax.ShapeDtypeStruct((count, chan...  4.33 us
  transfers between devices with their start and end apart: 20, of which 16 were waited for; matrix products, arithmetic and copies ran while one was open for 6% of the time, Pallas kernels for 0%

profile of v3, /device:TPU:102, one launch (start us, length us, event | category | flops | bytes accessed | tf_op | source)
XLA Modules:
  0.0 173.5 jit_solution(16310853066732865291)
XLA Ops:
  1.0 9.1 %collective-permute-start = (bf16[384,128]{0,1:T(8,128)(2,1)S(1)}, bf16[384,128]{0,1:T(8,128)(2,1)S(1)}, u32[]{:S(2)}, u32[]{:S(2)}) collective-permute-start(bf16[384,128]{0,1:T(8,128)(2,1)S(1)} %copy.13), channel_id=1, source_target_pairs={{0,8},{8,16},{16,24},{24,0},{1,9},{9,17},{17,25},{25,1},{2,10},{10... | collective-permute-start | bytes 294920 | tf_op jit(solution)/shard_map/ppermute | solution.py:22
  10.1 2.9 %collective-permute-start.1 = (bf16[384,128]{0,1:T(8,128)(2,1)S(1)}, bf16[384,128]{0,1:T(8,128)(2,1)S(1)}, u32[]{:S(2)}, u32[]{:S(2)}) collective-permute-start(bf16[384,128]{0,1:T(8,128)(2,1)S(1)} %copy.13), channel_id=1, source_target_pairs={{0,24},{8,0},{16,8},{24,16},{1,25},{9,1},{17,9},{25,17},{2,26},{10... | collective-permute-start | bytes 294920 | tf_op jit(solution)/shard_map/ppermute | solution.py:22
  13.1 7.0 %collective-permute-done = bf16[384,128]{0,1:T(8,128)(2,1)S(1)} collective-permute-done((bf16[384,128]{0,1:T(8,128)(2,1)S(1)}, bf16[384,128]{0,1:T(8,128)(2,1)S(1)}, u32[]{:S(2)}, u32[]{:S(2)}) %collective-permute-start) | collective-permute-done | bytes 98336 | tf_op jit(solution)/shard_map/ppermute | solution.py:22
  20.2 5.3 %collective-permute-start.2 = (bf16[192,128]{0,1:T(8,128)(2,1)S(1)}, bf16[192,128]{0,1:T(8,128)(2,1)S(1)}, u32[]{:S(2)}, u32[]{:S(2)}) collective-permute-start(bf16[192,128]{0,1:T(8,128)(2,1)S(1)} %slice.167), channel_id=1, source_target_pairs={{0,8},{8,16},{16,24},{24,0},{1,9},{9,17},{17,25},{25,1},{2,10},{10... | collective-permute-start | bytes 147464 | tf_op jit(solution)/shard_map/ppermute | solution.py:22
  25.6 4.5 %collective-permute-start.3 = (bf16[192,128]{0,1:T(8,128)(2,1)S(1)}, bf16[192,128]{0,1:T(8,128)(2,1)S(1)}, u32[]{:S(2)}, u32[]{:S(2)}) collective-permute-start(bf16[192,128]{0,1:T(8,128)(2,1)S(1)} %slice.168), channel_id=1, source_target_pairs={{0,24},{8,0},{16,8},{24,16},{1,25},{9,1},{17,9},{25,17},{2,26},{10... | collective-permute-start | bytes 147464 | tf_op jit(solution)/shard_map/ppermute | solution.py:22
  31.2 6.0 %collective-permute-done.3 = bf16[192,128]{0,1:T(8,128)(2,1)S(1)} collective-permute-done((bf16[192,128]{0,1:T(8,128)(2,1)S(1)}, bf16[192,128]{0,1:T(8,128)(2,1)S(1)}, u32[]{:S(2)}, u32[]{:S(2)}) %collective-permute-start.3) | collective-permute-done | bytes 49184 | tf_op jit(solution)/shard_map/ppermute | solution.py:22
  37.3 2.4 %collective-permute-start.4 = (bf16[4,384,128]{1,2,0:T(8,128)(2,1)S(1)}, bf16[4,384,128]{1,2,0:T(8,128)(2,1)S(1)}, u32[]{:S(2)}, u32[]{:S(2)}) collective-permute-start(bf16[4,384,128]{1,2,0:T(8,128)(2,1)S(1)} %fusion.25), channel_id=1, source_target_pairs={{0,2},{2,4},{4,6},{6,0},{1,3},{3,5},{5,7},{7,1},{8,10},{10,12},{12... | collective-permute-start | bytes 1179656 | tf_op jit(solution)/shard_map/ppermute | solution.py:22
  39.7 3.5 %collective-permute-start.5 = (bf16[4,384,128]{1,2,0:T(8,128)(2,1)S(1)}, bf16[4,384,128]{1,2,0:T(8,128)(2,1)S(1)}, u32[]{:S(2)}, u32[]{:S(2)}) collective-permute-start(bf16[4,384,128]{1,2,0:T(8,128)(2,1)S(1)} %fusion.25), channel_id=1, source_target_pairs={{0,6},{2,0},{4,2},{6,4},{1,7},{3,1},{5,3},{7,5},{8,14},{10,8},{12,... | collective-permute-start | bytes 1179656 | tf_op jit(solution)/shard_map/ppermute | solution.py:22
  43.5 3.6 %collective-permute-done.4 = bf16[4,384,128]{1,2,0:T(8,128)(2,1)S(1)} collective-permute-done((bf16[4,384,128]{1,2,0:T(8,128)(2,1)S(1)}, bf16[4,384,128]{1,2,0:T(8,128)(2,1)S(1)}, u32[]{:S(2)}, u32[]{:S(2)}) %collective-permute-start.4) | collective-permute-done | bytes 393248 | tf_op jit(solution)/shard_map/ppermute | solution.py:22
  47.1 3.6 %collective-permute-start.6 = (bf16[4,192,128]{1,2,0:T(8,128)(2,1)S(1)}, bf16[4,192,128]{1,2,0:T(8,128)(2,1)S(1)}, u32[]{:S(2)}, u32[]{:S(2)}) collective-permute-start(bf16[4,192,128]{1,2,0:T(8,128)(2,1)S(1)} %slice.169), channel_id=1, source_target_pairs={{0,2},{2,4},{4,6},{6,0},{1,3},{3,5},{5,7},{7,1},{8,10},{10,12},{12... | collective-permute-start | bytes 589832 | tf_op jit(solution)/shard_map/ppermute | solution.py:22
  50.9 2.2 %collective-permute-start.7 = (bf16[4,192,128]{1,2,0:T(8,128)(2,1)S(1)}, bf16[4,192,128]{1,2,0:T(8,128)(2,1)S(1)}, u32[]{:S(2)}, u32[]{:S(2)}) collective-permute-start(bf16[4,192,128]{1,2,0:T(8,128)(2,1)S(1)} %slice.170), channel_id=1, source_target_pairs={{0,6},{2,0},{4,2},{6,4},{1,7},{3,1},{5,3},{7,5},{8,14},{10,8},{12,... | collective-permute-start | bytes 589832 | tf_op jit(solution)/shard_map/ppermute | solution.py:22
  53.3 2.1 %collective-permute-done.6 = bf16[4,192,128]{1,2,0:T(8,128)(2,1)S(1)} collective-permute-done((bf16[4,192,128]{1,2,0:T(8,128)(2,1)S(1)}, bf16[4,192,128]{1,2,0:T(8,128)(2,1)S(1)}, u32[]{:S(2)}, u32[]{:S(2)}) %collective-permute-start.6) | collective-permute-done | bytes 196640 | tf_op jit(solution)/shard_map/ppermute | solution.py:22
  55.4 5.0 %collective-permute-done.7 = bf16[4,192,128]{1,2,0:T(8,128)(2,1)S(1)} collective-permute-done((bf16[4,192,128]{1,2,0:T(8,128)(2,1)S(1)}, bf16[4,192,128]{1,2,0:T(8,128)(2,1)S(1)}, u32[]{:S(2)}, u32[]{:S(2)}) %collective-permute-start.7) | collective-permute-done | bytes 196640 | tf_op jit(solution)/shard_map/ppermute | solution.py:22
  60.5 1.9 %collective-permute-start.8 = (bf16[4,4,384,128]{2,3,0,1:T(8,128)(2,1)S(1)}, bf16[4,4,384,128]{2,3,0,1:T(8,128)(2,1)}, u32[]{:S(2)}, u32[]{:S(2)}) collective-permute-start(bf16[4,4,384,128]{2,3,0,1:T(8,128)(2,1)S(1)} %fusion.12), channel_id=1, source_target_pairs={{0,1},{1,0},{2,3},{3,2},{4,5},{5,4},{6,7},{7,6},{8,9},{9,8},{10,11... | collective-permute-start | bytes 4718600 | tf_op jit(solution)/shard_map/ppermute | solution.py:22
  62.5 4.7 %copy.20 = bf16[4096,3,128]{0,2,1:T(8,128)(2,1)} copy(bf16[4096,3,128]{2,0,1:T(8,128)(2,1)} %param.9) | data formatting | bytes 6291456 | tf_op args[2]
  78.2 3.5 %collective-permute-start.9 = (bf16[2,384]{1,0:T(2,128)(2,1)S(1)}, bf16[2,384]{1,0:T(2,128)(2,1)S(1)}, u32[]{:S(2)}, u32[]{:S(2)}) collective-permute-start(bf16[2,384]{1,0:T(2,128)(2,1)S(1)} %slice.171), channel_id=1, source_target_pairs={{0,32},{32,64},{64,96},{96,128},{128,160},{160,192},{192,224},{224... | collective-permute-start | bytes 4616 | tf_op jit(solution)/shard_map/ppermute | solution.py:18
  82.2 3.6 %collective-permute-done.9 = bf16[2,384]{1,0:T(2,128)(2,1)S(1)} collective-permute-done((bf16[2,384]{1,0:T(2,128)(2,1)S(1)}, bf16[2,384]{1,0:T(2,128)(2,1)S(1)}, u32[]{:S(2)}, u32[]{:S(2)}) %collective-permute-start.9) | collective-permute-done | bytes 1568 | tf_op jit(solution)/shard_map/ppermute | solution.py:18
  89.0 6.0 %collective-permute-done.10 = bf16[127,128]{1,0:T(8,128)(2,1)S(1)} collective-permute-done((bf16[127,128]{1,0:T(8,128)(2,1)S(1)}, bf16[127,128]{1,0:T(8,128)(2,1)S(1)}, u32[]{:S(2)}, u32[]{:S(2)}) %collective-permute-start.10) | collective-permute-done | bytes 32544 | tf_op jit(solution)/shard_map/ppermute | solution.py:18
  95.8 4.3 %shard_map.73 = f32[384,128]{1,0:T(8,128)} custom-call(f32[512,128]{1,0:T(8,128)} %maximum_convert_fusion.ext_ref, f32[128,128]{1,0:T(8,128)} %convert_bitcast_fusion.1.filt_ref), custom_call_target="tpu_custom_call" | custom-call | tf_op jit(solution)/shard_map/pallas_call | solution.py:99
  100.1 2.6 %convert_bitcast_fusion = bf16[2,4,4,384,128]{3,4,2,1,0:T(8,128)(2,1)S(1)} fusion(s32[]{:T(128)S(6)} %select_n.97, f32[384,128]{1,0:T(8,128)} %shard_map.73, f32[384,3,128]{2,0,1:T(8,128)S(1)} %multiply_add_fusion, f32[128]{0:T(128)S(1)} %copy-done.4, bf16[384,1,128]{2,0,1:T(8,128)(2,1)S(1)} %fusion.16, s32[]{:T(128)S(6)} %select_n.95, ...), kind=kOutput, calls=%fused_computation.8 | convolution fusion | flops 407093248 | bytes 4686344 | tf_op jit(solution)/shard_map/tk,cxzki->cxzti/dot_general | solution.py:136
  104.8 3.4 %collective-permute-done.11 = bf16[4,4,384,128]{2,3,1,0:T(8,128)(2,1)S(1)} collective-permute-done((bf16[4,4,384,128]{2,3,1,0:T(8,128)(2,1)S(1)}, bf16[4,4,384,128]{2,3,1,0:T(8,128)(2,1)S(1)}, u32[]{:S(2)}, u32[]{:S(2)}) %collective-permute-start.11) | collective-permute-done | bytes 1572896 | tf_op jit(solution)/shard_map/ppermute | solution.py:22
  111.0 3.9 %collective-permute-start.14 = (bf16[4,192,128]{1,2,0:T(8,128)(2,1)S(1)}, bf16[4,192,128]{1,2,0:T(8,128)(2,1)S(1)}, u32[]{:S(2)}, u32[]{:S(2)}) collective-permute-start(bf16[4,192,128]{1,2,0:T(8,128)(2,1)S(1)} %get-tuple-element.15), channel_id=1, source_target_pairs={{0,6},{2,0},{4,2},{6,4},{1,7},{3,1},{5,3},{7,5},{8,14},{10,8},{12,... | collective-permute-start | bytes 589832 | tf_op jit(solution)/shard_map/ppermute | solution.py:22
  115.0 4.2 %collective-permute-done.12 = bf16[4,192,128]{1,2,0:T(8,128)(2,1)S(1)} collective-permute-done((bf16[4,192,128]{1,2,0:T(8,128)(2,1)S(1)}, bf16[4,192,128]{1,2,0:T(8,128)(2,1)S(1)}, u32[]{:S(2)}, u32[]{:S(2)}) %collective-permute-start.12) | collective-permute-done | bytes 196640 | tf_op jit(solution)/shard_map/ppermute | solution.py:22
  119.4 3.4 %collective-permute-start.13 = (bf16[4,384,128]{1,2,0:T(8,128)(2,1)S(1)}, bf16[4,384,128]{1,2,0:T(8,128)(2,1)S(1)}, u32[]{:S(2)}, u32[]{:S(2)}) collective-permute-start(bf16[4,384,128]{1,2,0:T(8,128)(2,1)S(1)} %pad_maximum_fusion), channel_id=1, source_target_pairs={{0,2},{2,4},{4,6},{6,0},{1,3},{3,5},{5,7},{7,1},{8,10},{10,12},{12... | collective-permute-start | bytes 1179656 | tf_op jit(solution)/shard_map/ppermute | solution.py:22
  123.2 2.4 %collective-permute-start.15 = (bf16[4,384,128]{1,2,0:T(8,128)(2,1)S(1)}, bf16[4,384,128]{1,2,0:T(8,128)(2,1)S(1)}, u32[]{:S(2)}, u32[]{:S(2)}) collective-permute-start(bf16[4,384,128]{1,2,0:T(8,128)(2,1)S(1)} %pad_maximum_fusion.1), channel_id=1, source_target_pairs={{0,6},{2,0},{4,2},{6,4},{1,7},{3,1},{5,3},{7,5},{8,14},{10,8},{12,... | collective-permute-start | bytes 1179656 | tf_op jit(solution)/shard_map/ppermute | solution.py:22
  125.6 6.0 %collective-permute-done.13 = bf16[4,384,128]{1,2,0:T(8,128)(2,1)S(1)} collective-permute-done((bf16[4,384,128]{1,2,0:T(8,128)(2,1)S(1)}, bf16[4,384,128]{1,2,0:T(8,128)(2,1)S(1)}, u32[]{:S(2)}, u32[]{:S(2)}) %collective-permute-start.13) | collective-permute-done | bytes 393248 | tf_op jit(solution)/shard_map/ppermute | solution.py:22
  131.7 5.0 %collective-permute-done.15 = bf16[4,384,128]{1,2,0:T(8,128)(2,1)S(1)} collective-permute-done((bf16[4,384,128]{1,2,0:T(8,128)(2,1)S(1)}, bf16[4,384,128]{1,2,0:T(8,128)(2,1)S(1)}, u32[]{:S(2)}, u32[]{:S(2)}) %collective-permute-start.15) | collective-permute-done | bytes 393248 | tf_op jit(solution)/shard_map/ppermute | solution.py:22
  136.9 8.9 %collective-permute-start.16 = (bf16[192,128]{0,1:T(8,128)(2,1)S(1)}, bf16[192,128]{0,1:T(8,128)(2,1)S(1)}, u32[]{:S(2)}, u32[]{:S(2)}) collective-permute-start(bf16[192,128]{0,1:T(8,128)(2,1)S(1)} %get-tuple-element.10), channel_id=1, source_target_pairs={{0,8},{8,16},{16,24},{24,0},{1,9},{9,17},{17,25},{25,1},{2,10},{10... | collective-permute-start | bytes 147464 | tf_op jit(solution)/shard_map/ppermute | solution.py:22
  148.2 8.4 %collective-permute-done.18 = bf16[192,128]{0,1:T(8,128)(2,1)S(1)} collective-permute-done((bf16[192,128]{0,1:T(8,128)(2,1)S(1)}, bf16[192,128]{0,1:T(8,128)(2,1)S(1)}, u32[]{:S(2)}, u32[]{:S(2)}) %collective-permute-start.18) | collective-permute-done | bytes 49184 | tf_op jit(solution)/shard_map/ppermute | solution.py:22
  156.8 4.5 %collective-permute-start.17 = (bf16[384,128]{0,1:T(8,128)(2,1)S(1)}, bf16[384,128]{0,1:T(8,128)(2,1)S(1)}, u32[]{:S(2)}, u32[]{:S(2)}) collective-permute-start(bf16[384,128]{0,1:T(8,128)(2,1)S(1)} %pad_maximum_fusion.3), channel_id=1, source_target_pairs={{0,8},{8,16},{16,24},{24,0},{1,9},{9,17},{17,25},{25,1},{2,10},{10... | collective-permute-start | bytes 294920 | tf_op jit(solution)/shard_map/ppermute | solution.py:22
  161.4 5.3 %collective-permute-start.19 = (bf16[384,128]{0,1:T(8,128)(2,1)S(1)}, bf16[384,128]{0,1:T(8,128)(2,1)S(1)}, u32[]{:S(2)}, u32[]{:S(2)}) collective-permute-start(bf16[384,128]{0,1:T(8,128)(2,1)S(1)} %pad_maximum_fusion.4), channel_id=1, source_target_pairs={{0,24},{8,0},{16,8},{24,16},{1,25},{9,1},{17,9},{25,17},{2,26},{10... | collective-permute-start | bytes 294920 | tf_op jit(solution)/shard_map/ppermute | solution.py:22
  167.5 5.2 %collective-permute-done.19 = bf16[384,128]{0,1:T(8,128)(2,1)S(1)} collective-permute-done((bf16[384,128]{0,1:T(8,128)(2,1)S(1)}, bf16[384,128]{0,1:T(8,128)(2,1)S(1)}, u32[]{:S(2)}, u32[]{:S(2)}) %collective-permute-start.19) | collective-permute-done | bytes 98336 | tf_op jit(solution)/shard_map/ppermute | solution.py:22
  (81 shorter events, 28.4 us)
Async XLA Ops:
  1.0 19.1 %collective-permute-start = (bf16[384,128]{0,1:T(8,128)(2,1)S(1)}, bf16[384,128]{0,1:T(8,128)(2,1)S(1)}, u32[]{:S(2)}, u32[]{:S(2)}) collective-permute-start(bf16[384,128]{0,1:T(8,128)(2,1)S(1)} %copy.13), channel_id=1, source_target_pairs={{0,8},{8,16},{16,24},{24,0},{1,9},{9,17},{17,25},{25,1},{2,10},{10... | collective-permute-start | bytes 294920 | tf_op jit(solution)/shard_map/ppermute | solution.py:22
  10.1 15.3 %collective-permute-start.1 = (bf16[384,128]{0,1:T(8,128)(2,1)S(1)}, bf16[384,128]{0,1:T(8,128)(2,1)S(1)}, u32[]{:S(2)}, u32[]{:S(2)}) collective-permute-start(bf16[384,128]{0,1:T(8,128)(2,1)S(1)} %copy.13), channel_id=1, source_target_pairs={{0,24},{8,0},{16,8},{24,16},{1,25},{9,1},{17,9},{25,17},{2,26},{10... | collective-permute-start | bytes 294920 | tf_op jit(solution)/shard_map/ppermute | solution.py:22
  20.2 11.1 %collective-permute-start.2 = (bf16[192,128]{0,1:T(8,128)(2,1)S(1)}, bf16[192,128]{0,1:T(8,128)(2,1)S(1)}, u32[]{:S(2)}, u32[]{:S(2)}) collective-permute-start(bf16[192,128]{0,1:T(8,128)(2,1)S(1)} %slice.167), channel_id=1, source_target_pairs={{0,8},{8,16},{16,24},{24,0},{1,9},{9,17},{17,25},{25,1},{2,10},{10... | collective-permute-start | bytes 147464 | tf_op jit(solution)/shard_map/ppermute | solution.py:22
  25.6 11.6 %collective-permute-start.3 = (bf16[192,128]{0,1:T(8,128)(2,1)S(1)}, bf16[192,128]{0,1:T(8,128)(2,1)S(1)}, u32[]{:S(2)}, u32[]{:S(2)}) collective-permute-start(bf16[192,128]{0,1:T(8,128)(2,1)S(1)} %slice.168), channel_id=1, source_target_pairs={{0,24},{8,0},{16,8},{24,16},{1,25},{9,1},{17,9},{25,17},{2,26},{10... | collective-permute-start | bytes 147464 | tf_op jit(solution)/shard_map/ppermute | solution.py:22
  37.3 9.8 %collective-permute-start.4 = (bf16[4,384,128]{1,2,0:T(8,128)(2,1)S(1)}, bf16[4,384,128]{1,2,0:T(8,128)(2,1)S(1)}, u32[]{:S(2)}, u32[]{:S(2)}) collective-permute-start(bf16[4,384,128]{1,2,0:T(8,128)(2,1)S(1)} %fusion.25), channel_id=1, source_target_pairs={{0,2},{2,4},{4,6},{6,0},{1,3},{3,5},{5,7},{7,1},{8,10},{10,12},{12... | collective-permute-start | bytes 1179656 | tf_op jit(solution)/shard_map/ppermute | solution.py:22
  39.7 11.0 %collective-permute-start.5 = (bf16[4,384,128]{1,2,0:T(8,128)(2,1)S(1)}, bf16[4,384,128]{1,2,0:T(8,128)(2,1)S(1)}, u32[]{:S(2)}, u32[]{:S(2)}) collective-permute-start(bf16[4,384,128]{1,2,0:T(8,128)(2,1)S(1)} %fusion.25), channel_id=1, source_target_pairs={{0,6},{2,0},{4,2},{6,4},{1,7},{3,1},{5,3},{7,5},{8,14},{10,8},{12,... | collective-permute-start | bytes 1179656 | tf_op jit(solution)/shard_map/ppermute | solution.py:22
  47.1 8.3 %collective-permute-start.6 = (bf16[4,192,128]{1,2,0:T(8,128)(2,1)S(1)}, bf16[4,192,128]{1,2,0:T(8,128)(2,1)S(1)}, u32[]{:S(2)}, u32[]{:S(2)}) collective-permute-start(bf16[4,192,128]{1,2,0:T(8,128)(2,1)S(1)} %slice.169), channel_id=1, source_target_pairs={{0,2},{2,4},{4,6},{6,0},{1,3},{3,5},{5,7},{7,1},{8,10},{10,12},{12... | collective-permute-start | bytes 589832 | tf_op jit(solution)/shard_map/ppermute | solution.py:22
  50.9 9.5 %collective-permute-start.7 = (bf16[4,192,128]{1,2,0:T(8,128)(2,1)S(1)}, bf16[4,192,128]{1,2,0:T(8,128)(2,1)S(1)}, u32[]{:S(2)}, u32[]{:S(2)}) collective-permute-start(bf16[4,192,128]{1,2,0:T(8,128)(2,1)S(1)} %slice.170), channel_id=1, source_target_pairs={{0,6},{2,0},{4,2},{6,4},{1,7},{3,1},{5,3},{7,5},{8,14},{10,8},{12,... | collective-permute-start | bytes 589832 | tf_op jit(solution)/shard_map/ppermute | solution.py:22
  60.5 11.4 %collective-permute-start.8 = (bf16[4,4,384,128]{2,3,0,1:T(8,128)(2,1)S(1)}, bf16[4,4,384,128]{2,3,0,1:T(8,128)(2,1)}, u32[]{:S(2)}, u32[]{:S(2)}) collective-permute-start(bf16[4,4,384,128]{2,3,0,1:T(8,128)(2,1)S(1)} %fusion.12), channel_id=1, source_target_pairs={{0,1},{1,0},{2,3},{3,2},{4,5},{5,4},{6,7},{7,6},{8,9},{9,8},{10,11... | collective-permute-start | bytes 4718600 | tf_op jit(solution)/shard_map/ppermute | solution.py:22
  62.5 4.7 %copy-start.1 = (bf16[128,128]{1,0:T(8,128)(2,1)S(1)}, bf16[128,128]{1,0:T(8,128)(2,1)}, u32[]{:S(2)}) copy-start(bf16[128,128]{1,0:T(8,128)(2,1)} %param.11) | copy-start | bytes 98308
  67.2 3.2 %copy-start.3 = (f32[3,3,128]{2,1,0:T(4,128)S(1)}, f32[3,3,128]{2,1,0:T(4,128)}, u32[]{:S(2)}) copy-start(f32[3,3,128]{2,1,0:T(4,128)} %param.10) | copy-start | bytes 13828
  71.9 2.6 %copy-start.2 = (f32[4096]{0:T(1024)S(1)}, f32[4096]{0:T(1024)}, u32[]{:S(2)}) copy-start(f32[4096]{0:T(1024)} %param.8) | copy-start | bytes 49156
  74.5 1.9 %copy-start = (bf16[4096,3,128]{0,2,1:T(8,128)(2,1)S(1)}, bf16[4096,3,128]{0,2,1:T(8,128)(2,1)}, u32[]{:S(2)}) copy-start(bf16[4096,3,128]{0,2,1:T(8,128)(2,1)} %copy.20) | copy-start | bytes 9437188
  78.2 7.6 %collective-permute-start.9 = (bf16[2,384]{1,0:T(2,128)(2,1)S(1)}, bf16[2,384]{1,0:T(2,128)(2,1)S(1)}, u32[]{:S(2)}, u32[]{:S(2)}) collective-permute-start(bf16[2,384]{1,0:T(2,128)(2,1)S(1)} %slice.171), channel_id=1, source_target_pairs={{0,32},{32,64},{64,96},{96,128},{128,160},{160,192},{192,224},{224... | collective-permute-start | bytes 4616 | tf_op jit(solution)/shard_map/ppermute | solution.py:18
  86.4 13.7 %copy-start.4 = (f32[128]{0:T(128)S(1)}, f32[128]{0:T(128)}, u32[]{:S(2)}) copy-start(f32[128]{0:T(128)} %param.12) | copy-start | bytes 1540
  87.0 7.9 %collective-permute-start.10 = (bf16[127,128]{1,0:T(8,128)(2,1)S(1)}, bf16[127,128]{1,0:T(8,128)(2,1)S(1)}, u32[]{:S(2)}, u32[]{:S(2)}) collective-permute-start(bf16[127,128]{1,0:T(8,128)(2,1)S(1)} %slice_bitcast_fusion.14), channel_id=1, source_target_pairs={{0,32},{32,64},{64,96},{96,128},{128,160},{160,192},{192,224},{224... | collective-permute-start | bytes 97544 | tf_op jit(solution)/shard_map/ppermute | solution.py:18
  102.9 5.3 %collective-permute-start.11 = (bf16[4,4,384,128]{2,3,1,0:T(8,128)(2,1)S(1)}, bf16[4,4,384,128]{2,3,1,0:T(8,128)(2,1)S(1)}, u32[]{:S(2)}, u32[]{:S(2)}) collective-permute-start(bf16[4,4,384,128]{2,3,1,0:T(8,128)(2,1)S(1)} %slice_bitcast_fusion), channel_id=1, source_target_pairs={{0,1},{1,0},{2,3},{3,2},{4,5},{5,4},{6,7},{7,6},{8,9},{9,8},{10,11... | collective-permute-start | bytes 4718600 | tf_op jit(solution)/shard_map/ppermute | solution.py:22
  109.0 10.2 %collective-permute-start.12 = (bf16[4,192,128]{1,2,0:T(8,128)(2,1)S(1)}, bf16[4,192,128]{1,2,0:T(8,128)(2,1)S(1)}, u32[]{:S(2)}, u32[]{:S(2)}) collective-permute-start(bf16[4,192,128]{1,2,0:T(8,128)(2,1)S(1)} %get-tuple-element.14), channel_id=1, source_target_pairs={{0,2},{2,4},{4,6},{6,0},{1,3},{3,5},{5,7},{7,1},{8,10},{10,12},{12... | collective-permute-start | bytes 589832 | tf_op jit(solution)/shard_map/ppermute | solution.py:22
  111.0 11.8 %collective-permute-start.14 = (bf16[4,192,128]{1,2,0:T(8,128)(2,1)S(1)}, bf16[4,192,128]{1,2,0:T(8,128)(2,1)S(1)}, u32[]{:S(2)}, u32[]{:S(2)}) collective-permute-start(bf16[4,192,128]{1,2,0:T(8,128)(2,1)S(1)} %get-tuple-element.15), channel_id=1, source_target_pairs={{0,6},{2,0},{4,2},{6,4},{1,7},{3,1},{5,3},{7,5},{8,14},{10,8},{12,... | collective-permute-start | bytes 589832 | tf_op jit(solution)/shard_map/ppermute | solution.py:22
  119.4 12.2 %collective-permute-start.13 = (bf16[4,384,128]{1,2,0:T(8,128)(2,1)S(1)}, bf16[4,384,128]{1,2,0:T(8,128)(2,1)S(1)}, u32[]{:S(2)}, u32[]{:S(2)}) collective-permute-start(bf16[4,384,128]{1,2,0:T(8,128)(2,1)S(1)} %pad_maximum_fusion), channel_id=1, source_target_pairs={{0,2},{2,4},{4,6},{6,0},{1,3},{3,5},{5,7},{7,1},{8,10},{10,12},{12... | collective-permute-start | bytes 1179656 | tf_op jit(solution)/shard_map/ppermute | solution.py:22
  123.2 13.5 %collective-permute-start.15 = (bf16[4,384,128]{1,2,0:T(8,128)(2,1)S(1)}, bf16[4,384,128]{1,2,0:T(8,128)(2,1)S(1)}, u32[]{:S(2)}, u32[]{:S(2)}) collective-permute-start(bf16[4,384,128]{1,2,0:T(8,128)(2,1)S(1)} %pad_maximum_fusion.1), channel_id=1, source_target_pairs={{0,6},{2,0},{4,2},{6,4},{1,7},{3,1},{5,3},{7,5},{8,14},{10,8},{12,... | collective-permute-start | bytes 1179656 | tf_op jit(solution)/shard_map/ppermute | solution.py:22
  136.9 11.3 %collective-permute-start.16 = (bf16[192,128]{0,1:T(8,128)(2,1)S(1)}, bf16[192,128]{0,1:T(8,128)(2,1)S(1)}, u32[]{:S(2)}, u32[]{:S(2)}) collective-permute-start(bf16[192,128]{0,1:T(8,128)(2,1)S(1)} %get-tuple-element.10), channel_id=1, source_target_pairs={{0,8},{8,16},{16,24},{24,0},{1,9},{9,17},{17,25},{25,1},{2,10},{10... | collective-permute-start | bytes 147464 | tf_op jit(solution)/shard_map/ppermute | solution.py:22
  145.8 10.8 %collective-permute-start.18 = (bf16[192,128]{0,1:T(8,128)(2,1)S(1)}, bf16[192,128]{0,1:T(8,128)(2,1)S(1)}, u32[]{:S(2)}, u32[]{:S(2)}) collective-permute-start(bf16[192,128]{0,1:T(8,128)(2,1)S(1)} %get-tuple-element.11), channel_id=1, source_target_pairs={{0,24},{8,0},{16,8},{24,16},{1,25},{9,1},{17,9},{25,17},{2,26},{10... | collective-permute-start | bytes 147464 | tf_op jit(solution)/shard_map/ppermute | solution.py:22
  156.8 10.7 %collective-permute-start.17 = (bf16[384,128]{0,1:T(8,128)(2,1)S(1)}, bf16[384,128]{0,1:T(8,128)(2,1)S(1)}, u32[]{:S(2)}, u32[]{:S(2)}) collective-permute-start(bf16[384,128]{0,1:T(8,128)(2,1)S(1)} %pad_maximum_fusion.3), channel_id=1, source_target_pairs={{0,8},{8,16},{16,24},{24,0},{1,9},{9,17},{17,25},{25,1},{2,10},{10... | collective-permute-start | bytes 294920 | tf_op jit(solution)/shard_map/ppermute | solution.py:22
  161.4 11.3 %collective-permute-start.19 = (bf16[384,128]{0,1:T(8,128)(2,1)S(1)}, bf16[384,128]{0,1:T(8,128)(2,1)S(1)}, u32[]{:S(2)}, u32[]{:S(2)}) collective-permute-start(bf16[384,128]{0,1:T(8,128)(2,1)S(1)} %pad_maximum_fusion.4), channel_id=1, source_target_pairs={{0,24},{8,0},{16,8},{24,16},{1,25},{9,1},{17,9},{25,17},{2,26},{10... | collective-permute-start | bytes 294920 | tf_op jit(solution)/shard_map/ppermute | solution.py:22

commit v4 on v1

--- a/solution.py
+++ b/solution.py
@@ -16,6 +16,19 @@
 def passed_along(value, axis, count, steps):
     initial, last = (max(0, -steps), min(count, count - steps))
     return lax.ppermute(value, axis, [(source, source + steps) for source in range(initial, last)])
+
+
+def gathered(block, name, count):
+    copies = jnp.broadcast_to(block[None], (count,) + block.shape)
+    return lax.all_to_all(copies, name, 0, 0)
+
+
+def reduced(stack, name, count):
+    parts = lax.all_to_all(stack, name, 0, 0)
+    total = parts[0].astype(jnp.float32)
+    for member in range(1, count):
+        total = total + parts[member].astype(jnp.float32)
+    return total
 
 
 def featurize(extended, feat_taps, count):
@@ -70,8 +83,8 @@
     feat_len = feat_taps.shape[1]
     w_flat = w_in.reshape(width, 3 * chans)
     stacked = bases_in
-    for name, _ in CH_PARTS:
-        stacked = lax.all_gather(stacked, name, axis=0)
+    for name, size in CH_PARTS:
+        stacked = gathered(stacked, name, size)
     whole = stacked.transpose(3, 2, 1, 0, 4).reshape(tok, width)
     wide = whole.astype(jnp.float32)
     inverse = lax.rsqrt(jnp.mean(wide * wide, axis=1, keepdims=True) + 1e-05)
@@ -88,11 +101,13 @@
     ).astype(jnp.float32)
     filtered = causal_filter(extended, long_filter.astype(jnp.float32).T)
     gated = (query * (filtered + skip_gain * product.astype(jnp.float32))).astype(jnp.bfloat16)
-    terms = jnp.dot(gated, w_out, preferred_element_type=jnp.float32).astype(jnp.bfloat16)
     sizes = [size for _, size in CH_PARTS]
-    split = terms.reshape(tok, *sizes, chans).transpose(3, 2, 1, 0, 4)
-    for name, _ in CH_PARTS[::-1]:
-        split = lax.psum_scatter(split, name, scatter_dimension=0)
+    blocks = w_out.reshape(chans, *sizes, chans).transpose(3, 2, 1, 0, 4)
+    split = jnp.einsum(
+        "tk,cxzki->cxzti", gated, blocks, preferred_element_type=jnp.float32
+    ).astype(jnp.bfloat16)
+    for name, size in CH_PARTS[::-1]:
+        split = reduced(split, name, size).astype(jnp.bfloat16)
     return split
 
 

time: 254 us -> 165 us (0.65)
  the two profiles are of different devices: /device:TPU:2 before, /device:TPU:32 now
where the time goes in v4:
time: 165 us; the launch traced here: 164 us
  blocking collectives  105 us (64%)
  waiting for transfers between devices  23.1 us (14%)
  local copies, waits for them, and re-layouts  11.8 us (7%)
  starting transfers between devices  9.7 us (6%)
  other arithmetic  5.85 us (4%)
  Pallas kernels  4.33 us (3%)
  matrix products  3.92 us (2%)
    all_to_all x3, blocking collectives, reduced(): parts = lax.all_to_all(stack, name, 0, 0)  57.9 us
    all_to_all x2, blocking collectives, gathered(): return lax.all_to_all(copies, name, 0, 0)  47.2 us
    all_to_all x1, waiting for transfers between devices, gathered(): return lax.all_to_all(copies, name, 0, 0)  14.3 us
    ppermute x2, waiting for transfers between devices, passed_along(): lax.ppermute(value, axis, [(source, source + steps) for source in range(i...  8.82 us
    unnamed x17, local copies, waits for them, and re-layouts  6.8 us
    ppermute x2, starting transfers between devices, passed_along(): lax.ppermute(value, axis, [(source, source + steps) for source in range(i...  5.4 us
    pallas_call x1, Pallas kernels, causal_filter(): pl.pallas_call(filter_kernel, out_shape=jax.ShapeDtypeStruct((count, chan...  4.33 us
    all_to_all x1, starting transfers between devices, gathered(): return lax.all_to_all(copies, name, 0, 0)  4.29 us
  transfers between devices with their start and end apart: 3, of which 3 were waited for; matrix products, arithmetic and copies ran while one was open for 4% of the time, Pallas kernels for 0%

profile of v4, /device:TPU:32, one launch (start us, length us, event | category | flops | bytes accessed | tf_op | source)
XLA Modules:
  0.0 164.1 jit_solution(1276065037336766311)
XLA Ops:
  0.0 1.0 copy.20
  1.1 41.0 %all_to_all.30 = bf16[4,384,128]{1,2,0:T(8,128)(2,1)S(1)} all-to-all(bf16[4,384,128]{1,2,0:T(8,128)(2,1)S(1)} %broadcast_in_dim.8), channel_id=1, replica_groups=mesh['z_lo'=4,'y'=4,'z_hi'=4,'x'=4,'core'=2] {'z_hi'}, dimensions={0} | all-to-all | bytes 786432 | tf_op jit(solution)/shard_map/all_to_all | solution.py:23
  42.0 1.4 broadcast_in_dim.9
  43.4 4.3 %all-to-all-start.1 = ((bf16[4,4,384,128]{2,3,1,0:T(8,128)(2,1)}), bf16[4,4,384,128]{2,3,1,0:T(8,128)(2,1)S(1)}, u32[]{:S(2)}, u32[]{:S(2)}) async-start(bf16[4,4,384,128]{2,3,1,0:T(8,128)(2,1)} %broadcast_in_dim.9), calls=%async_computation.1 | async-start | bytes 3145728 | tf_op jit(solution)/shard_map/all_to_all | solution.py:23
  47.7 4.7 %copy.23 = bf16[4096,3,128]{0,2,1:T(8,128)(2,1)} copy(bf16[4096,3,128]{2,0,1:T(8,128)(2,1)} %param.9) | data formatting | bytes 6291456 | tf_op args[2]
  52.5 0.6 convert_bitcast_fusion.1.filt_ref
  53.2 14.3 %all-to-all-done.1 = bf16[4,4,384,128]{2,3,1,0:T(8,128)(2,1)S(1)} async-done(((bf16[4,4,384,128]{2,3,1,0:T(8,128)(2,1)}), bf16[4,4,384,128]{2,3,1,0:T(8,128)(2,1)S(1)}, u32[]{:S(2)}, u32[]{:S(2)}) %all-to-all-start.1) | async-done | bytes 1572896 | tf_op jit(solution)/shard_map/all_to_all | solution.py:23
  67.7 0.5 broadcast_in_dim.10
  68.2 6.3 %all_to_all.31 = bf16[2,4,4,384,128]{3,4,1,2,0:T(8,128)(2,1)S(1)} all-to-all(bf16[2,4,4,384,128]{3,4,1,2,0:T(8,128)(2,1)S(1)} %broadcast_in_dim.10), channel_id=1, replica_groups=mesh['z_lo'=4,'y'=4,'z_hi'=4,'x'=4,'core'=2] {'core'}, dimensions={0} | all-to-all | bytes 6291456 | tf_op jit(solution)/shard_map/all_to_all | solution.py:23
  74.4 0.8 fusion
  75.3 0.9 fusion.3
  76.2 1.0 copy-done
  77.2 1.8 %convolution_convert_fusion = bf16[384,384]{1,0:T(8,128)(2,1)S(1)} fusion(bf16[384,4096]{0,1:T(8,128)(2,1)S(1)} %bitcast.58, bf16[4096,384]{0,1:T(8,128)(2,1)S(1)} %bitcast.57), kind=kOutput, calls=%fused_computation.9 | convolution fusion | flops 1208107008 | bytes 6586368 | tf_op jit(solution)/shard_map/dot_general | solution.py:92
  79.0 3.5 %collective-permute-start = (bf16[2,384]{1,0:T(2,128)(2,1)S(1)}, bf16[2,384]{1,0:T(2,128)(2,1)S(1)}, u32[]{:S(2)}, u32[]{:S(2)}) collective-permute-start(bf16[2,384]{1,0:T(2,128)(2,1)S(1)} %slice.88), channel_id=1, source_target_pairs={{0,32},{32,64},{64,96},{96,128},{128,160},{160,192},{192,224},{224... | collective-permute-start | bytes 4616 | tf_op jit(solution)/shard_map/ppermute | solution.py:18
  82.5 0.8 reshape.68
  83.5 0.2 copy.25
  83.7 2.9 %collective-permute-done = bf16[2,384]{1,0:T(2,128)(2,1)S(1)} collective-permute-done((bf16[2,384]{1,0:T(2,128)(2,1)S(1)}, bf16[2,384]{1,0:T(2,128)(2,1)S(1)}, u32[]{:S(2)}, u32[]{:S(2)}) %collective-permute-start) | collective-permute-done | bytes 1568 | tf_op jit(solution)/shard_map/ppermute | solution.py:18
  86.7 0.2 copy.26
  86.9 1.1 copy.27
  88.0 0.2 copy.28
  88.2 0.2 copy.29
  88.4 1.2 multiply_add_fusion
  89.7 1.9 %collective-permute-start.1 = (bf16[127,128]{1,0:T(8,128)(2,1)S(1)}, bf16[127,128]{1,0:T(8,128)(2,1)S(1)}, u32[]{:S(2)}, u32[]{:S(2)}) collective-permute-start(bf16[127,128]{1,0:T(8,128)(2,1)S(1)} %slice_bitcast_fusion.1), channel_id=1, source_target_pairs={{0,32},{32,64},{64,96},{96,128},{128,160},{160,192},{192,224},{224... | collective-permute-start | bytes 97544 | tf_op jit(solution)/shard_map/ppermute | solution.py:18
  91.6 6.0 %collective-permute-done.1 = bf16[127,128]{1,0:T(8,128)(2,1)S(1)} collective-permute-done((bf16[127,128]{1,0:T(8,128)(2,1)S(1)}, bf16[127,128]{1,0:T(8,128)(2,1)S(1)}, u32[]{:S(2)}, u32[]{:S(2)}) %collective-permute-start.1) | collective-permute-done | bytes 32544 | tf_op jit(solution)/shard_map/ppermute | solution.py:18
  97.6 0.8 maximum_convert_fusion.ext_ref
  98.4 4.3 %shard_map.73 = f32[384,128]{1,0:T(8,128)} custom-call(f32[512,128]{1,0:T(8,128)} %maximum_convert_fusion.ext_ref, f32[128,128]{1,0:T(8,128)} %convert_bitcast_fusion.1.filt_ref), custom_call_target="tpu_custom_call" | custom-call | tf_op jit(solution)/shard_map/pallas_call | solution.py:72
  102.8 2.1 %convert_bitcast_fusion = bf16[2,4,4,384,128]{4,3,2,1,0:T(8,128)(2,1)S(1)} fusion(bf16[128,4,4,2,128]{4,3,2,1,0:T(2,128)(2,1)S(1)} %reshape.68, f32[384,128]{1,0:T(8,128)} %shard_map.73, f32[384,3,128]{2,0,1:T(8,128)S(1)} %multiply_add_fusion, f32[128]{0:T(128)S(1)} %copy-done.5, bf16[384,1,128]{2,0,1:T(8,128)(2,1)S(1)} %fusion.11), kind=kOutput, calls=%fused_computation.7 | convolution fusion | flops 404471808 | bytes 4686336 | tf_op jit(solution)/shard_map/tk,cxzki->cxzti/dot_general | solution.py:106
  104.9 6.3 %all_to_all.32 = bf16[2,4,4,384,128]{4,3,2,1,0:T(8,128)(2,1)S(1)} all-to-all(bf16[2,4,4,384,128]{4,3,2,1,0:T(8,128)(2,1)S(1)} %convert_bitcast_fusion), channel_id=1, replica_groups=mesh['z_lo'=4,'y'=4,'z_hi'=4,'x'=4,'core'=2] {'core'}, dimensions={0} | all-to-all | bytes 6291456 | tf_op jit(solution)/shard_map/all_to_all | solution.py:27
  111.1 0.4 fusion.4
  111.6 23.7 %all_to_all.33 = bf16[4,4,384,128]{3,2,1,0:T(8,128)(2,1)S(1)} all-to-all(bf16[4,4,384,128]{3,2,1,0:T(8,128)(2,1)S(1)} %fusion.4), channel_id=1, replica_groups=mesh['z_lo'=4,'y'=4,'z_hi'=4,'x'=4,'core'=2] {'x'}, dimensions={0} | all-to-all | bytes 3145728 | tf_op jit(solution)/shard_map/all_to_all | solution.py:27
  135.5 27.9 %all_to_all.34 = bf16[4,384,128]{2,1,0:T(8,128)(2,1)S(1)} all-to-all(bf16[4,384,128]{2,1,0:T(8,128)(2,1)S(1)} %fusion.7), channel_id=1, replica_groups=mesh['z_lo'=4,'y'=4,'z_hi'=4,'x'=4,'core'=2] {'z_hi'}, dimensions={0} | all-to-all | bytes 786432 | tf_op jit(solution)/shard_map/all_to_all | solution.py:27
  163.4 0.7 fusion.14
  (26 shorter events, 0.9 us)
Async XLA Ops:
  43.4 24.1 %all-to-all-start.1 = ((bf16[4,4,384,128]{2,3,1,0:T(8,128)(2,1)}), bf16[4,4,384,128]{2,3,1,0:T(8,128)(2,1)S(1)}, u32[]{:S(2)}, u32[]{:S(2)}) async-start(bf16[4,4,384,128]{2,3,1,0:T(8,128)(2,1)} %broadcast_in_dim.9), calls=%async_computation.1 | async-start | bytes 3145728 | tf_op jit(solution)/shard_map/all_to_all | solution.py:23
  47.7 4.7 %copy-start.2 = (bf16[128,128]{1,0:T(8,128)(2,1)S(1)}, bf16[128,128]{1,0:T(8,128)(2,1)}, u32[]{:S(2)}) copy-start(bf16[128,128]{1,0:T(8,128)(2,1)} %param.11) | copy-start | bytes 98308
  47.7 4.8 %copy-start.4 = (f32[3,3,128]{2,1,0:T(4,128)S(1)}, f32[3,3,128]{2,1,0:T(4,128)}, u32[]{:S(2)}) copy-start(f32[3,3,128]{2,1,0:T(4,128)} %param.10) | copy-start | bytes 13828
  74.4 0.8 copy-start.3
  75.3 1.9 %copy-start = (bf16[4096,3,128]{0,2,1:T(8,128)(2,1)S(1)}, bf16[4096,3,128]{0,2,1:T(8,128)(2,1)}, u32[]{:S(2)}) copy-start(bf16[4096,3,128]{0,2,1:T(8,128)(2,1)} %copy.23) | copy-start | bytes 9437188
  77.2 5.4 %copy-start.1 = (bf16[128,4096]{1,0:T(8,128)(2,1)S(1)}, bf16[128,4096]{1,0:T(8,128)(2,1)}, u32[]{:S(2)}) copy-start(bf16[128,4096]{1,0:T(8,128)(2,1)} %param.13) | copy-start | bytes 3145732
  79.0 7.6 %collective-permute-start = (bf16[2,384]{1,0:T(2,128)(2,1)S(1)}, bf16[2,384]{1,0:T(2,128)(2,1)S(1)}, u32[]{:S(2)}, u32[]{:S(2)}) collective-permute-start(bf16[2,384]{1,0:T(2,128)(2,1)S(1)} %slice.88), channel_id=1, source_target_pairs={{0,32},{32,64},{64,96},{96,128},{128,160},{160,192},{192,224},{224... | collective-permute-start | bytes 4616 | tf_op jit(solution)/shard_map/ppermute | solution.py:18
  88.0 14.8 %copy-start.5 = (f32[128]{0:T(128)S(1)}, f32[128]{0:T(128)}, u32[]{:S(2)}) copy-start(f32[128]{0:T(128)} %param.12) | copy-start | bytes 1540
  89.7 7.9 %collective-permute-start.1 = (bf16[127,128]{1,0:T(8,128)(2,1)S(1)}, bf16[127,128]{1,0:T(8,128)(2,1)S(1)}, u32[]{:S(2)}, u32[]{:S(2)}) collective-permute-start(bf16[127,128]{1,0:T(8,128)(2,1)S(1)} %slice_bitcast_fusion.1), channel_id=1, source_target_pairs={{0,32},{32,64},{64,96},{96,128},{128,160},{160,192},{192,224},{224... | collective-permute-start | bytes 97544 | tf_op jit(solution)/shard_map/ppermute | solution.py:18

commit v5 on v4

--- a/solution.py
+++ b/solution.py
@@ -91,11 +91,14 @@
     normed = (wide * inverse * norm_gain).astype(jnp.bfloat16)
     mixed_in = jnp.dot(normed, w_flat, preferred_element_type=jnp.float32)
     projected = mixed_in.astype(jnp.bfloat16)
-    earlier = passed_along(projected[tok - (feat_len - 1) :], CTX, CTX_COUNT, 1)
-    feats = featurize(jnp.concatenate([earlier, projected], axis=0), feat_taps, tok)
+    earlier = passed_along(projected[tok - (taps - 1) - (feat_len - 1) :], CTX, CTX_COUNT, 1)
+    early_feats = featurize(earlier, feat_taps, taps - 1)
+    before = (early_feats[:, 1, :] * early_feats[:, 2, :]).astype(jnp.bfloat16)
+    feats = featurize(
+        jnp.concatenate([earlier[earlier.shape[0] - (feat_len - 1) :], projected], axis=0), feat_taps, tok
+    )
     query = feats[:, 0, :]
     product = (feats[:, 1, :] * feats[:, 2, :]).astype(jnp.bfloat16)
-    before = passed_along(product[tok - (taps - 1) :], CTX, CTX_COUNT, 1)
     extended = jnp.concatenate(
         [jnp.zeros((1, chans), jnp.bfloat16), before, product], axis=0
     ).astype(jnp.float32)

time: 165 us -> 159 us (0.964)
  waiting for transfers between devices: 23.1 us -> 18.6 us
  starting transfers between devices: 9.7 us -> 7.78 us
    ppermute x2 -> x1, waiting for transfers between devices: 8.82 us -> 4.25 us  [passed_along(): lax.ppermute(value, axis, [(source, source + steps) for source in range(i...]
    ppermute x2 -> x1, starting transfers between devices: 5.4 us -> 3.48 us  [passed_along(): lax.ppermute(value, axis, [(source, source + steps) for source in range(i...]
  transfers between devices with their start and end apart: 3 -> 2, of which waited for: 3 -> 2; matrix products, arithmetic and copies ran while one was open for 4% -> 4% of each run, Pallas kernels for 0% -> 0%
where the time goes in v5:
time: 159 us; the launch traced here: 158 us
  blocking collectives  105 us (66%)
  waiting for transfers between devices  18.6 us (12%)
  local copies, waits for them, and re-layouts  12.7 us (8%)
  starting transfers between devices  7.78 us (5%)
  other arithmetic  5.94 us (4%)
  Pallas kernels  4.33 us (3%)
  matrix products  3.95 us (2%)
    all_to_all x3, blocking collectives, reduced(): parts = lax.all_to_all(stack, name, 0, 0)  57.7 us
    all_to_all x2, blocking collectives, gathered(): return lax.all_to_all(copies, name, 0, 0)  47.2 us
    all_to_all x1, waiting for transfers between devices, gathered(): return lax.all_to_all(copies, name, 0, 0)  14.3 us
    unnamed x17, local copies, waits for them, and re-layouts  6.81 us
    pallas_call x1, Pallas kernels, causal_filter(): pl.pallas_call(filter_kernel, out_shape=jax.ShapeDtypeStruct((count, chan...  4.33 us
    all_to_all x1, starting transfers between devices, gathered(): return lax.all_to_all(copies, name, 0, 0)  4.29 us
    ppermute x1, waiting for transfers between devices, passed_along(): lax.ppermute(value, axis, [(source, source + steps) for source in range(i...  4.25 us
    ppermute x1, starting transfers between devices, passed_along(): lax.ppermute(value, axis, [(source, source + steps) for source in range(i...  3.48 us
  transfers between devices with their start and end apart: 2, of which 2 were waited for; matrix products, arithmetic and copies ran while one was open for 4% of the time, Pallas kernels for 0%

profile of v5, /device:TPU:32, one launch (start us, length us, event | category | flops | bytes accessed | tf_op | source)
XLA Modules:
  0.0 158.4 jit_solution(1119831399685514676)
XLA Ops:
  0.0 1.0 copy.26
  1.1 41.0 %all_to_all.30 = bf16[4,384,128]{1,2,0:T(8,128)(2,1)S(1)} all-to-all(bf16[4,384,128]{1,2,0:T(8,128)(2,1)S(1)} %broadcast_in_dim.8), channel_id=1, replica_groups=mesh['z_lo'=4,'y'=4,'z_hi'=4,'x'=4,'core'=2] {'z_hi'}, dimensions={0} | all-to-all | bytes 786432 | tf_op jit(solution)/shard_map/all_to_all | solution.py:23
  42.0 1.4 broadcast_in_dim.9
  43.4 4.3 %all-to-all-start.1 = ((bf16[4,4,384,128]{2,3,1,0:T(8,128)(2,1)}), bf16[4,4,384,128]{2,3,1,0:T(8,128)(2,1)S(1)}, u32[]{:S(2)}, u32[]{:S(2)}) async-start(bf16[4,4,384,128]{2,3,1,0:T(8,128)(2,1)} %broadcast_in_dim.9), calls=%async_computation.1 | async-start | bytes 3145728 | tf_op jit(solution)/shard_map/all_to_all | solution.py:23
  47.7 4.7 %copy.29 = bf16[4096,3,128]{0,2,1:T(8,128)(2,1)} copy(bf16[4096,3,128]{2,0,1:T(8,128)(2,1)} %param.9) | data formatting | bytes 6291456 | tf_op args[2]
  52.5 0.6 convert_bitcast_fusion.1.filt_ref
  53.2 14.3 %all-to-all-done.1 = bf16[4,4,384,128]{2,3,1,0:T(8,128)(2,1)S(1)} async-done(((bf16[4,4,384,128]{2,3,1,0:T(8,128)(2,1)}), bf16[4,4,384,128]{2,3,1,0:T(8,128)(2,1)S(1)}, u32[]{:S(2)}, u32[]{:S(2)}) %all-to-all-start.1) | async-done | bytes 1572896 | tf_op jit(solution)/shard_map/all_to_all | solution.py:23
  67.5 0.2 copy.27
  67.7 0.5 broadcast_in_dim.10
  68.2 6.3 %all_to_all.31 = bf16[2,4,4,384,128]{3,4,1,2,0:T(8,128)(2,1)S(1)} all-to-all(bf16[2,4,4,384,128]{3,4,1,2,0:T(8,128)(2,1)S(1)} %broadcast_in_dim.10), channel_id=1, replica_groups=mesh['z_lo'=4,'y'=4,'z_hi'=4,'x'=4,'core'=2] {'core'}, dimensions={0} | all-to-all | bytes 6291456 | tf_op jit(solution)/shard_map/all_to_all | solution.py:23
  74.4 0.8 fusion
  75.3 0.9 fusion.3
  76.2 1.0 copy-done
  77.2 1.8 %convolution_convert_fusion = bf16[384,384]{1,0:T(8,128)(2,1)S(1)} fusion(bf16[384,4096]{0,1:T(8,128)(2,1)S(1)} %bitcast.57, bf16[4096,384]{0,1:T(8,128)(2,1)S(1)} %bitcast.56), kind=kOutput, calls=%fused_computation.9 | convolution fusion | flops 1208107008 | bytes 6586368 | tf_op jit(solution)/shard_map/dot_general | solution.py:92
  79.0 3.5 %collective-permute-start = (bf16[129,384]{1,0:T(8,128)(2,1)S(1)}, bf16[129,384]{1,0:T(8,128)(2,1)S(1)}, u32[]{:S(2)}, u32[]{:S(2)}) collective-permute-start(bf16[129,384]{1,0:T(8,128)(2,1)S(1)} %slice.110), channel_id=1, source_target_pairs={{0,32},{32,64},{64,96},{96,128},{128,160},{160,192},{192,224},{224... | collective-permute-start | bytes 297224 | tf_op jit(solution)/shard_map/ppermute | solution.py:18
  82.5 0.8 reshape.79
  83.5 0.2 copy.31
  83.7 4.2 %collective-permute-done = bf16[129,384]{1,0:T(8,128)(2,1)S(1)} collective-permute-done((bf16[129,384]{1,0:T(8,128)(2,1)S(1)}, bf16[129,384]{1,0:T(8,128)(2,1)S(1)}, u32[]{:S(2)}, u32[]{:S(2)}) %collective-permute-start) | collective-permute-done | bytes 99104 | tf_op jit(solution)/shard_map/ppermute | solution.py:18
  88.1 0.2 copy.32
  88.3 1.1 copy.33
  89.4 0.2 copy.34
  89.6 0.2 copy.35
  89.9 1.2 multiply_add_fusion
  92.1 0.8 maximum_convert_fusion.ext_ref
  92.9 4.3 %shard_map.73 = f32[384,128]{1,0:T(8,128)} custom-call(f32[512,128]{1,0:T(8,128)} %maximum_convert_fusion.ext_ref, f32[128,128]{1,0:T(8,128)} %convert_bitcast_fusion.1.filt_ref), custom_call_target="tpu_custom_call" | custom-call | tf_op jit(solution)/shard_map/pallas_call | solution.py:72
  97.3 2.1 %convert_bitcast_fusion = bf16[2,4,4,384,128]{4,3,2,1,0:T(8,128)(2,1)S(1)} fusion(bf16[128,4,4,2,128]{4,3,2,1,0:T(2,128)(2,1)S(1)} %reshape.79, f32[384,128]{1,0:T(8,128)} %shard_map.73, bf16[384,128]{1,0:T(8,128)(2,1)S(1)} %fusion.17, f32[384,3,128]{2,0,1:T(8,128)S(1)} %multiply_add_fusion, f32[128]{0:T(128)S(1)} %copy-done.5), kind=kOutput, calls=%fused_computation.7 | convolution fusion | flops 404471808 | bytes 4686336 | tf_op jit(solution)/shard_map/tk,cxzki->cxzti/dot_general | solution.py:109
  99.4 6.3 %all_to_all.32 = bf16[2,4,4,384,128]{4,3,2,1,0:T(8,128)(2,1)S(1)} all-to-all(bf16[2,4,4,384,128]{4,3,2,1,0:T(8,128)(2,1)S(1)} %convert_bitcast_fusion), channel_id=1, replica_groups=mesh['z_lo'=4,'y'=4,'z_hi'=4,'x'=4,'core'=2] {'core'}, dimensions={0} | all-to-all | bytes 6291456 | tf_op jit(solution)/shard_map/all_to_all | solution.py:27
  105.7 0.4 fusion.4
  106.1 23.7 %all_to_all.33 = bf16[4,4,384,128]{3,2,1,0:T(8,128)(2,1)S(1)} all-to-all(bf16[4,4,384,128]{3,2,1,0:T(8,128)(2,1)S(1)} %fusion.4), channel_id=1, replica_groups=mesh['z_lo'=4,'y'=4,'z_hi'=4,'x'=4,'core'=2] {'x'}, dimensions={0} | all-to-all | bytes 3145728 | tf_op jit(solution)/shard_map/all_to_all | solution.py:27
  129.8 0.2 fusion.7
  130.0 27.7 %all_to_all.34 = bf16[4,384,128]{2,1,0:T(8,128)(2,1)S(1)} all-to-all(bf16[4,384,128]{2,1,0:T(8,128)(2,1)S(1)} %fusion.7), channel_id=1, replica_groups=mesh['z_lo'=4,'y'=4,'z_hi'=4,'x'=4,'core'=2] {'z_hi'}, dimensions={0} | all-to-all | bytes 786432 | tf_op jit(solution)/shard_map/all_to_all | solution.py:27
  157.8 0.7 fusion.14
  (32 shorter events, 1.5 us)
Async XLA Ops:
  43.4 24.1 %all-to-all-start.1 = ((bf16[4,4,384,128]{2,3,1,0:T(8,128)(2,1)}), bf16[4,4,384,128]{2,3,1,0:T(8,128)(2,1)S(1)}, u32[]{:S(2)}, u32[]{:S(2)}) async-start(bf16[4,4,384,128]{2,3,1,0:T(8,128)(2,1)} %broadcast_in_dim.9), calls=%async_computation.1 | async-start | bytes 3145728 | tf_op jit(solution)/shard_map/all_to_all | solution.py:23
  47.7 4.7 %copy-start.2 = (bf16[128,128]{1,0:T(8,128)(2,1)S(1)}, bf16[128,128]{1,0:T(8,128)(2,1)}, u32[]{:S(2)}) copy-start(bf16[128,128]{1,0:T(8,128)(2,1)} %param.11) | copy-start | bytes 98308
  47.7 4.8 %copy-start.4 = (f32[3,3,128]{2,1,0:T(4,128)S(1)}, f32[3,3,128]{2,1,0:T(4,128)}, u32[]{:S(2)}) copy-start(f32[3,3,128]{2,1,0:T(4,128)} %param.10) | copy-start | bytes 13828
  74.4 0.8 copy-start.3
  75.3 1.9 %copy-start = (bf16[4096,3,128]{0,2,1:T(8,128)(2,1)S(1)}, bf16[4096,3,128]{0,2,1:T(8,128)(2,1)}, u32[]{:S(2)}) copy-start(bf16[4096,3,128]{0,2,1:T(8,128)(2,1)} %copy.29) | copy-start | bytes 9437188
  77.2 5.4 %copy-start.1 = (bf16[128,4096]{1,0:T(8,128)(2,1)S(1)}, bf16[128,4096]{1,0:T(8,128)(2,1)}, u32[]{:S(2)}) copy-start(bf16[128,4096]{1,0:T(8,128)(2,1)} %param.13) | copy-start | bytes 3145732
  79.0 9.0 %collective-permute-start = (bf16[129,384]{1,0:T(8,128)(2,1)S(1)}, bf16[129,384]{1,0:T(8,128)(2,1)S(1)}, u32[]{:S(2)}, u32[]{:S(2)}) collective-permute-start(bf16[129,384]{1,0:T(8,128)(2,1)S(1)} %slice.110), channel_id=1, source_target_pairs={{0,32},{32,64},{64,96},{96,128},{128,160},{160,192},{192,224},{224... | collective-permute-start | bytes 297224 | tf_op jit(solution)/shard_map/ppermute | solution.py:18
  91.1 6.2 %copy-start.5 = (f32[128]{0:T(128)S(1)}, f32[128]{0:T(128)}, u32[]{:S(2)}) copy-start(f32[128]{0:T(128)} %param.12) | copy-start | bytes 1540

commit v6 on v3

--- a/solution.py
+++ b/solution.py
@@ -36,7 +36,7 @@
     left = shifted(block, name, count, 1)
     right = shifted(block, name, count, -1)
     far = jnp.concatenate(
-        [shifted(halves(left)[0], name, count, 1), shifted(halves(right)[1], name, count, -1)], axis=-2
+        [shifted(halves(block)[0], name, count, 2), shifted(halves(right)[1], name, count, -1)], axis=-2
     )
     out = lax.dynamic_update_index_in_dim(out, left, (index - 1) % count, 0)
     out = lax.dynamic_update_index_in_dim(out, right, (index + 1) % count, 0)
@@ -48,14 +48,14 @@
     if count == 2:
         return own + shifted(stack[1], name, 2, 1).astype(jnp.float32)
     far_a, far_b = halves(stack[2])
-    from_left = shifted(far_a, name, count, 1).astype(jnp.float32)
-    from_right = shifted(far_b, name, count, -1).astype(jnp.float32)
-    next_a, next_b = halves(stack[1])
+    straight = shifted(far_a, name, count, 2).astype(jnp.float32)
+    passed = shifted(far_b, name, count, -1).astype(jnp.float32)
+    from_left = shifted(stack[1], name, count, 1).astype(jnp.float32)
     prev_a, prev_b = halves(stack[3])
-    to_next = jnp.concatenate([(next_a.astype(jnp.float32) + from_left).astype(jnp.bfloat16), next_b], axis=-2)
-    to_prev = jnp.concatenate([prev_a, (prev_b.astype(jnp.float32) + from_right).astype(jnp.bfloat16)], axis=-2)
-    total = own + shifted(to_next, name, count, 1).astype(jnp.float32)
-    return total + shifted(to_prev, name, count, -1).astype(jnp.float32)
+    to_prev = jnp.concatenate([prev_a, (prev_b.astype(jnp.float32) + passed).astype(jnp.bfloat16)], axis=-2)
+    total = own + from_left + shifted(to_prev, name, count, -1).astype(jnp.float32)
+    total_a, total_b = halves(total)
+    return jnp.concatenate([total_a + straight, total_b], axis=-2)
 
 
 def featurize(extended, feat_taps, count):
@@ -118,11 +118,14 @@
     normed = (wide * inverse * norm_gain).astype(jnp.bfloat16)
     mixed_in = jnp.dot(normed, w_flat, preferred_element_type=jnp.float32)
     projected = mixed_in.astype(jnp.bfloat16)
-    earlier = passed_along(projected[tok - (feat_len - 1) :], CTX, CTX_COUNT, 1)
-    feats = featurize(jnp.concatenate([earlier, projected], axis=0), feat_taps, tok)
+    earlier = passed_along(projected[tok - (taps - 1) - (feat_len - 1) :], CTX, CTX_COUNT, 1)
+    early_feats = featurize(earlier, feat_taps, taps - 1)
+    before = (early_feats[:, 1, :] * early_feats[:, 2, :]).astype(jnp.bfloat16)
+    feats = featurize(
+        jnp.concatenate([earlier[earlier.shape[0] - (feat_len - 1) :], projected], axis=0), feat_taps, tok
+    )
     query = feats[:, 0, :]
     product = (feats[:, 1, :] * feats[:, 2, :]).astype(jnp.bfloat16)
-    before = passed_along(product[tok - (taps - 1) :], CTX, CTX_COUNT, 1)
     extended = jnp.concatenate(
         [jnp.zeros((1, chans), jnp.bfloat16), before, product], axis=0
     ).astype(jnp.float32)

time: 174 us -> 176 us (1.011)
  the two profiles are of different devices: /device:TPU:102 before, /device:TPU:6 now
where the time goes in v6:
time: 176 us; the launch traced here: 175 us
  starting transfers between devices  79.6 us (45%)
  waiting for transfers between devices  63.6 us (36%)
  local copies, waits for them, and re-layouts  15.6 us (9%)
  other arithmetic  6.62 us (4%)
  matrix products  4.4 us (3%)
  Pallas kernels  4.32 us (2%)
    ppermute x18, starting transfers between devices, shifted(): lax.ppermute(value, name, [(k, (k + steps) % count) for k in range(count)])  76.1 us
    ppermute x18, waiting for transfers between devices, shifted(): lax.ppermute(value, name, [(k, (k + steps) % count) for k in range(count)])  62.6 us
    unnamed x16, local copies, waits for them, and re-layouts  8.46 us
    pallas_call x1, Pallas kernels, causal_filter(): pl.pallas_call(filter_kernel, out_shape=jax.ShapeDtypeStruct((count, chan...  4.32 us
  transfers between devices with their start and end apart: 19, of which 11 were waited for; matrix products, arithmetic and copies ran while one was open for 7% of the time, Pallas kernels for 0%

profile of v6, /device:TPU:6, one launch (start us, length us, event | category | flops | bytes accessed | tf_op | source)
XLA Modules:
  0.0 175.1 jit_solution(7110588052519357472)
XLA Ops:
  1.0 9.1 %collective-permute-start = (bf16[384,128]{0,1:T(8,128)(2,1)S(1)}, bf16[384,128]{0,1:T(8,128)(2,1)S(1)}, u32[]{:S(2)}, u32[]{:S(2)}) collective-permute-start(bf16[384,128]{0,1:T(8,128)(2,1)S(1)} %copy.13), channel_id=1, source_target_pairs={{0,8},{8,16},{16,24},{24,0},{1,9},{9,17},{17,25},{25,1},{2,10},{10... | collective-permute-start | bytes 294920 | tf_op jit(solution)/shard_map/ppermute | solution.py:22
  10.1 5.6 %collective-permute-start.1 = (bf16[384,128]{0,1:T(8,128)(2,1)S(1)}, bf16[384,128]{0,1:T(8,128)(2,1)S(1)}, u32[]{:S(2)}, u32[]{:S(2)}) collective-permute-start(bf16[384,128]{0,1:T(8,128)(2,1)S(1)} %copy.13), channel_id=1, source_target_pairs={{0,24},{8,0},{16,8},{24,16},{1,25},{9,1},{17,9},{25,17},{2,26},{10... | collective-permute-start | bytes 294920 | tf_op jit(solution)/shard_map/ppermute | solution.py:22
  15.7 10.8 %collective-permute-start.2 = (bf16[192,128]{0,1:T(8,128)(2,1)S(1)}, bf16[192,128]{0,1:T(8,128)(2,1)S(1)}, u32[]{:S(2)}, u32[]{:S(2)}) collective-permute-start(bf16[192,128]{0,1:T(8,128)(2,1)S(1)} %slice.193), channel_id=1, source_target_pairs={{0,16},{8,24},{16,0},{24,8},{1,17},{9,25},{17,1},{25,9},{2,18},{10... | collective-permute-start | bytes 147464 | tf_op jit(solution)/shard_map/ppermute | solution.py:22
  28.3 4.3 %collective-permute-start.3 = (bf16[192,128]{0,1:T(8,128)(2,1)S(1)}, bf16[192,128]{0,1:T(8,128)(2,1)S(1)}, u32[]{:S(2)}, u32[]{:S(2)}) collective-permute-start(bf16[192,128]{0,1:T(8,128)(2,1)S(1)} %slice.194), channel_id=1, source_target_pairs={{0,24},{8,0},{16,8},{24,16},{1,25},{9,1},{17,9},{25,17},{2,26},{10... | collective-permute-start | bytes 147464 | tf_op jit(solution)/shard_map/ppermute | solution.py:22
  32.7 10.4 %collective-permute-done.3 = bf16[192,128]{0,1:T(8,128)(2,1)S(1)} collective-permute-done((bf16[192,128]{0,1:T(8,128)(2,1)S(1)}, bf16[192,128]{0,1:T(8,128)(2,1)S(1)}, u32[]{:S(2)}, u32[]{:S(2)}) %collective-permute-start.3) | collective-permute-done | bytes 49184 | tf_op jit(solution)/shard_map/ppermute | solution.py:22
  43.1 2.7 %collective-permute-start.5 = (bf16[4,384,128]{1,2,0:T(8,128)(2,1)S(1)}, bf16[4,384,128]{1,2,0:T(8,128)(2,1)S(1)}, u32[]{:S(2)}, u32[]{:S(2)}) collective-permute-start(bf16[4,384,128]{1,2,0:T(8,128)(2,1)S(1)} %fusion.26), channel_id=1, source_target_pairs={{0,6},{2,0},{4,2},{6,4},{1,7},{3,1},{5,3},{7,5},{8,14},{10,8},{12,... | collective-permute-start | bytes 1179656 | tf_op jit(solution)/shard_map/ppermute | solution.py:22
  45.9 4.3 %collective-permute-start.4 = (bf16[4,384,128]{1,2,0:T(8,128)(2,1)S(1)}, bf16[4,384,128]{1,2,0:T(8,128)(2,1)S(1)}, u32[]{:S(2)}, u32[]{:S(2)}) collective-permute-start(bf16[4,384,128]{1,2,0:T(8,128)(2,1)S(1)} %fusion.26), channel_id=1, source_target_pairs={{0,2},{2,4},{4,6},{6,0},{1,3},{3,5},{5,7},{7,1},{8,10},{10,12},{12... | collective-permute-start | bytes 1179656 | tf_op jit(solution)/shard_map/ppermute | solution.py:22
  50.3 2.1 %collective-permute-start.6 = (bf16[4,192,128]{1,2,0:T(8,128)(2,1)S(1)}, bf16[4,192,128]{1,2,0:T(8,128)(2,1)S(1)}, u32[]{:S(2)}, u32[]{:S(2)}) collective-permute-start(bf16[4,192,128]{1,2,0:T(8,128)(2,1)S(1)} %slice.195), channel_id=1, source_target_pairs={{0,4},{2,6},{4,0},{6,2},{1,5},{3,7},{5,1},{7,3},{8,12},{10,14},{12... | collective-permute-start | bytes 589832 | tf_op jit(solution)/shard_map/ppermute | solution.py:22
  52.7 10.2 %collective-permute-done.5 = bf16[4,384,128]{1,2,0:T(8,128)(2,1)S(1)} collective-permute-done((bf16[4,384,128]{1,2,0:T(8,128)(2,1)S(1)}, bf16[4,384,128]{1,2,0:T(8,128)(2,1)S(1)}, u32[]{:S(2)}, u32[]{:S(2)}) %collective-permute-start.5) | collective-permute-done | bytes 393248 | tf_op jit(solution)/shard_map/ppermute | solution.py:22
  63.0 1.9 %collective-permute-start.7 = (bf16[4,192,128]{1,2,0:T(8,128)(2,1)S(1)}, bf16[4,192,128]{1,2,0:T(8,128)(2,1)S(1)}, u32[]{:S(2)}, u32[]{:S(2)}) collective-permute-start(bf16[4,192,128]{1,2,0:T(8,128)(2,1)S(1)} %slice.196), channel_id=1, source_target_pairs={{0,6},{2,0},{4,2},{6,4},{1,7},{3,1},{5,3},{7,5},{8,14},{10,8},{12,... | collective-permute-start | bytes 589832 | tf_op jit(solution)/shard_map/ppermute | solution.py:22
  65.1 7.4 %collective-permute-done.7 = bf16[4,192,128]{1,2,0:T(8,128)(2,1)S(1)} collective-permute-done((bf16[4,192,128]{1,2,0:T(8,128)(2,1)S(1)}, bf16[4,192,128]{1,2,0:T(8,128)(2,1)S(1)}, u32[]{:S(2)}, u32[]{:S(2)}) %collective-permute-start.7) | collective-permute-done | bytes 196640 | tf_op jit(solution)/shard_map/ppermute | solution.py:22
  72.7 1.9 %collective-permute-start.8 = (bf16[4,4,384,128]{2,3,0,1:T(8,128)(2,1)S(1)}, bf16[4,4,384,128]{2,3,0,1:T(8,128)(2,1)}, u32[]{:S(2)}, u32[]{:S(2)}) collective-permute-start(bf16[4,4,384,128]{2,3,0,1:T(8,128)(2,1)S(1)} %fusion.12), channel_id=1, source_target_pairs={{0,1},{1,0},{2,3},{3,2},{4,5},{5,4},{6,7},{7,6},{8,9},{9,8},{10,11... | collective-permute-start | bytes 4718600 | tf_op jit(solution)/shard_map/ppermute | solution.py:22
  74.7 4.7 %copy.21 = bf16[4096,3,128]{0,2,1:T(8,128)(2,1)} copy(bf16[4096,3,128]{2,0,1:T(8,128)(2,1)} %param.9) | data formatting | bytes 6291456 | tf_op args[2]
  82.8 1.8 %bitcast_dynamic-update-slice_fusion.1 = bf16[2,4,4,384,128]{3,4,0,1,2:T(8,128)(2,1)S(1)} fusion(bf16[2,4,4,384,128]{3,4,0,1,2:T(8,128)(2,1)S(1)} %bitcast_dynamic-update-slice_fusion, s32[]{:T(128)S(6)} %select_n.113, bf16[4,4,384,128]{2,3,0,1:T(8,128)(2,1)} %collective-permute-done.8), kind=kLoop, calls=%fused_computation.18 | loop fusion | bytes 3145732 | tf_op jit(solution)/shard_map/jit(dynamic_update_index_in_dim)/dynamic_update_slice | solution.py:35
  87.3 1.8 %convolution_convert_fusion = bf16[384,384]{1,0:T(8,128)(2,1)S(1)} fusion(bf16[384,4096]{0,1:T(8,128)(2,1)S(1)} %bitcast.122, bf16[4096,384]{0,1:T(8,128)(2,1)S(1)} %bitcast.121), kind=kOutput, calls=%fused_computation.19 | convolution fusion | flops 1208107008 | bytes 6586368 | tf_op jit(solution)/shard_map/dot_general | solution.py:119
  89.1 3.5 %collective-permute-start.9 = (bf16[129,384]{1,0:T(8,128)(2,1)S(1)}, bf16[129,384]{1,0:T(8,128)(2,1)S(1)}, u32[]{:S(2)}, u32[]{:S(2)}) collective-permute-start(bf16[129,384]{1,0:T(8,128)(2,1)S(1)} %slice.197), channel_id=1, source_target_pairs={{0,32},{32,64},{64,96},{96,128},{128,160},{160,192},{192,224},{224... | collective-permute-start | bytes 297224 | tf_op jit(solution)/shard_map/ppermute | solution.py:18
  98.5 4.3 %shard_map.73 = f32[384,128]{1,0:T(8,128)} custom-call(f32[512,128]{1,0:T(8,128)} %maximum_convert_fusion.ext_ref, f32[128,128]{1,0:T(8,128)} %convert_bitcast_fusion.1.filt_ref), custom_call_target="tpu_custom_call" | custom-call | tf_op jit(solution)/shard_map/pallas_call | solution.py:99
  102.8 2.6 %convert_bitcast_fusion = bf16[2,4,4,384,128]{3,4,2,1,0:T(8,128)(2,1)S(1)} fusion(s32[]{:T(128)S(6)} %select_n.97, f32[384,128]{1,0:T(8,128)} %shard_map.73, bf16[384,128]{1,0:T(8,128)(2,1)S(1)} %fusion.24, f32[384,3,128]{2,0,1:T(8,128)S(1)} %multiply_add_fusion, f32[128]{0:T(128)S(1)} %copy-done.4, s32[]{:T(128)S(6)} %select_n.95, ...), kind=kOutput, calls=%fused_computation.8 | convolution fusion | flops 407093248 | bytes 4686344 | tf_op jit(solution)/shard_map/tk,cxzki->cxzti/dot_general | solution.py:139
  105.6 1.9 %collective-permute-start.10 = (bf16[4,4,384,128]{2,3,1,0:T(8,128)(2,1)S(1)}, bf16[4,4,384,128]{2,3,1,0:T(8,128)(2,1)S(1)}, u32[]{:S(2)}, u32[]{:S(2)}) collective-permute-start(bf16[4,4,384,128]{2,3,1,0:T(8,128)(2,1)S(1)} %slice_bitcast_fusion), channel_id=1, source_target_pairs={{0,1},{1,0},{2,3},{3,2},{4,5},{5,4},{6,7},{7,6},{8,9},{9,8},{10,11... | collective-permute-start | bytes 4718600 | tf_op jit(solution)/shard_map/ppermute | solution.py:22
  107.5 3.4 %collective-permute-done.10 = bf16[4,4,384,128]{2,3,1,0:T(8,128)(2,1)S(1)} collective-permute-done((bf16[4,4,384,128]{2,3,1,0:T(8,128)(2,1)S(1)}, bf16[4,4,384,128]{2,3,1,0:T(8,128)(2,1)S(1)}, u32[]{:S(2)}, u32[]{:S(2)}) %collective-permute-start.10) | collective-permute-done | bytes 1572896 | tf_op jit(solution)/shard_map/ppermute | solution.py:22
  111.7 1.9 %collective-permute-start.12 = (bf16[4,192,128]{1,2,0:T(8,128)(2,1)S(1)}, bf16[4,192,128]{1,2,0:T(8,128)(2,1)S(1)}, u32[]{:S(2)}, u32[]{:S(2)}) collective-permute-start(bf16[4,192,128]{1,2,0:T(8,128)(2,1)S(1)} %get-tuple-element.11), channel_id=1, source_target_pairs={{0,6},{2,0},{4,2},{6,4},{1,7},{3,1},{5,3},{7,5},{8,14},{10,8},{12,... | collective-permute-start | bytes 589832 | tf_op jit(solution)/shard_map/ppermute | solution.py:22
  113.6 5.1 %collective-permute-start.11 = (bf16[4,384,128]{1,2,0:T(8,128)(2,1)S(1)}, bf16[4,384,128]{1,2,0:T(8,128)(2,1)S(1)}, u32[]{:S(2)}, u32[]{:S(2)}) collective-permute-start(bf16[4,384,128]{1,2,0:T(8,128)(2,1)S(1)} %get-tuple-element.7), channel_id=1, source_target_pairs={{0,2},{2,4},{4,6},{6,0},{1,3},{3,5},{5,7},{7,1},{8,10},{10,12},{12... | collective-permute-start | bytes 1179656 | tf_op jit(solution)/shard_map/ppermute | solution.py:22
  118.8 4.4 %collective-permute-done.12 = bf16[4,192,128]{1,2,0:T(8,128)(2,1)S(1)} collective-permute-done((bf16[4,192,128]{1,2,0:T(8,128)(2,1)S(1)}, bf16[4,192,128]{1,2,0:T(8,128)(2,1)S(1)}, u32[]{:S(2)}, u32[]{:S(2)}) %collective-permute-start.12) | collective-permute-done | bytes 196640 | tf_op jit(solution)/shard_map/ppermute | solution.py:22
  123.4 1.9 %collective-permute-start.13 = (bf16[4,384,128]{1,2,0:T(8,128)(2,1)S(1)}, bf16[4,384,128]{1,2,0:T(8,128)(2,1)S(1)}, u32[]{:S(2)}, u32[]{:S(2)}) collective-permute-start(bf16[4,384,128]{1,2,0:T(8,128)(2,1)S(1)} %pad_maximum_fusion), channel_id=1, source_target_pairs={{0,6},{2,0},{4,2},{6,4},{1,7},{3,1},{5,3},{7,5},{8,14},{10,8},{12,... | collective-permute-start | bytes 1179656 | tf_op jit(solution)/shard_map/ppermute | solution.py:22
  125.3 2.9 %collective-permute-start.14 = (bf16[4,192,128]{1,2,0:T(8,128)(2,1)S(1)}, bf16[4,192,128]{1,2,0:T(8,128)(2,1)S(1)}, u32[]{:S(2)}, u32[]{:S(2)}) collective-permute-start(bf16[4,192,128]{1,2,0:T(8,128)(2,1)S(1)} %get-tuple-element.10), channel_id=1, source_target_pairs={{0,4},{2,6},{4,0},{6,2},{1,5},{3,7},{5,1},{7,3},{8,12},{10,14},{12... | collective-permute-start | bytes 589832 | tf_op jit(solution)/shard_map/ppermute | solution.py:22
  128.3 14.2 %collective-permute-done.13 = bf16[4,384,128]{1,2,0:T(8,128)(2,1)S(1)} collective-permute-done((bf16[4,384,128]{1,2,0:T(8,128)(2,1)S(1)}, bf16[4,384,128]{1,2,0:T(8,128)(2,1)S(1)}, u32[]{:S(2)}, u32[]{:S(2)}) %collective-permute-start.13) | collective-permute-done | bytes 393248 | tf_op jit(solution)/shard_map/ppermute | solution.py:22
  143.0 3.6 %collective-permute-start.16 = (bf16[192,128]{0,1:T(8,128)(2,1)S(1)}, bf16[192,128]{0,1:T(8,128)(2,1)S(1)}, u32[]{:S(2)}, u32[]{:S(2)}) collective-permute-start(bf16[192,128]{0,1:T(8,128)(2,1)S(1)} %slice_bitcast_fusion.8), channel_id=1, source_target_pairs={{0,24},{8,0},{16,8},{24,16},{1,25},{9,1},{17,9},{25,17},{2,26},{10... | collective-permute-start | bytes 147464 | tf_op jit(solution)/shard_map/ppermute | solution.py:22
  146.7 6.1 %collective-permute-start.15 = (bf16[384,128]{0,1:T(8,128)(2,1)S(1)}, bf16[384,128]{0,1:T(8,128)(2,1)S(1)}, u32[]{:S(2)}, u32[]{:S(2)}) collective-permute-start(bf16[384,128]{0,1:T(8,128)(2,1)S(1)} %fusion.25), channel_id=1, source_target_pairs={{0,8},{8,16},{16,24},{24,0},{1,9},{9,17},{17,25},{25,1},{2,10},{10... | collective-permute-start | bytes 294920 | tf_op jit(solution)/shard_map/ppermute | solution.py:22
  154.7 2.9 %collective-permute-start.17 = (bf16[384,128]{0,1:T(8,128)(2,1)S(1)}, bf16[384,128]{0,1:T(8,128)(2,1)S(1)}, u32[]{:S(2)}, u32[]{:S(2)}) collective-permute-start(bf16[384,128]{0,1:T(8,128)(2,1)S(1)} %pad_maximum_fusion.3), channel_id=1, source_target_pairs={{0,24},{8,0},{16,8},{24,16},{1,25},{9,1},{17,9},{25,17},{2,26},{10... | collective-permute-start | bytes 294920 | tf_op jit(solution)/shard_map/ppermute | solution.py:22
  157.6 6.9 %collective-permute-start.18 = (bf16[192,128]{0,1:T(8,128)(2,1)S(1)}, bf16[192,128]{0,1:T(8,128)(2,1)S(1)}, u32[]{:S(2)}, u32[]{:S(2)}) collective-permute-start(bf16[192,128]{0,1:T(8,128)(2,1)S(1)} %get-tuple-element.14), channel_id=1, source_target_pairs={{0,16},{8,24},{16,0},{24,8},{1,17},{9,25},{17,1},{25,9},{2,18},{10... | collective-permute-start | bytes 147464 | tf_op jit(solution)/shard_map/ppermute | solution.py:22
  164.6 2.1 %collective-permute-done.17 = bf16[384,128]{0,1:T(8,128)(2,1)S(1)} collective-permute-done((bf16[384,128]{0,1:T(8,128)(2,1)S(1)}, bf16[384,128]{0,1:T(8,128)(2,1)S(1)}, u32[]{:S(2)}, u32[]{:S(2)}) %collective-permute-start.17) | collective-permute-done | bytes 98336 | tf_op jit(solution)/shard_map/ppermute | solution.py:22
  166.8 7.4 %collective-permute-done.18 = bf16[192,128]{0,1:T(8,128)(2,1)S(1)} collective-permute-done((bf16[192,128]{0,1:T(8,128)(2,1)S(1)}, bf16[192,128]{0,1:T(8,128)(2,1)S(1)}, u32[]{:S(2)}, u32[]{:S(2)}) %collective-permute-start.18) | collective-permute-done | bytes 49184 | tf_op jit(solution)/shard_map/ppermute | solution.py:22
  (90 shorter events, 20.0 us)
Async XLA Ops:
  1.0 31.6 %collective-permute-start = (bf16[384,128]{0,1:T(8,128)(2,1)S(1)}, bf16[384,128]{0,1:T(8,128)(2,1)S(1)}, u32[]{:S(2)}, u32[]{:S(2)}) collective-permute-start(bf16[384,128]{0,1:T(8,128)(2,1)S(1)} %copy.13), channel_id=1, source_target_pairs={{0,8},{8,16},{16,24},{24,0},{1,9},{9,17},{17,25},{25,1},{2,10},{10... | collective-permute-start | bytes 294920 | tf_op jit(solution)/shard_map/ppermute | solution.py:22
  10.1 18.1 %collective-permute-start.1 = (bf16[384,128]{0,1:T(8,128)(2,1)S(1)}, bf16[384,128]{0,1:T(8,128)(2,1)S(1)}, u32[]{:S(2)}, u32[]{:S(2)}) collective-permute-start(bf16[384,128]{0,1:T(8,128)(2,1)S(1)} %copy.13), channel_id=1, source_target_pairs={{0,24},{8,0},{16,8},{24,16},{1,25},{9,1},{17,9},{25,17},{2,26},{10... | collective-permute-start | bytes 294920 | tf_op jit(solution)/shard_map/ppermute | solution.py:22
  15.7 17.0 %collective-permute-start.2 = (bf16[192,128]{0,1:T(8,128)(2,1)S(1)}, bf16[192,128]{0,1:T(8,128)(2,1)S(1)}, u32[]{:S(2)}, u32[]{:S(2)}) collective-permute-start(bf16[192,128]{0,1:T(8,128)(2,1)S(1)} %slice.193), channel_id=1, source_target_pairs={{0,16},{8,24},{16,0},{24,8},{1,17},{9,25},{17,1},{25,9},{2,18},{10... | collective-permute-start | bytes 147464 | tf_op jit(solution)/shard_map/ppermute | solution.py:22
  28.3 14.7 %collective-permute-start.3 = (bf16[192,128]{0,1:T(8,128)(2,1)S(1)}, bf16[192,128]{0,1:T(8,128)(2,1)S(1)}, u32[]{:S(2)}, u32[]{:S(2)}) collective-permute-start(bf16[192,128]{0,1:T(8,128)(2,1)S(1)} %slice.194), channel_id=1, source_target_pairs={{0,24},{8,0},{16,8},{24,16},{1,25},{9,1},{17,9},{25,17},{2,26},{10... | collective-permute-start | bytes 147464 | tf_op jit(solution)/shard_map/ppermute | solution.py:22
  43.1 19.7 %collective-permute-start.5 = (bf16[4,384,128]{1,2,0:T(8,128)(2,1)S(1)}, bf16[4,384,128]{1,2,0:T(8,128)(2,1)S(1)}, u32[]{:S(2)}, u32[]{:S(2)}) collective-permute-start(bf16[4,384,128]{1,2,0:T(8,128)(2,1)S(1)} %fusion.26), channel_id=1, source_target_pairs={{0,6},{2,0},{4,2},{6,4},{1,7},{3,1},{5,3},{7,5},{8,14},{10,8},{12,... | collective-permute-start | bytes 1179656 | tf_op jit(solution)/shard_map/ppermute | solution.py:22
  45.9 19.1 %collective-permute-start.4 = (bf16[4,384,128]{1,2,0:T(8,128)(2,1)S(1)}, bf16[4,384,128]{1,2,0:T(8,128)(2,1)S(1)}, u32[]{:S(2)}, u32[]{:S(2)}) collective-permute-start(bf16[4,384,128]{1,2,0:T(8,128)(2,1)S(1)} %fusion.26), channel_id=1, source_target_pairs={{0,2},{2,4},{4,6},{6,0},{1,3},{3,5},{5,7},{7,1},{8,10},{10,12},{12... | collective-permute-start | bytes 1179656 | tf_op jit(solution)/shard_map/ppermute | solution.py:22
  50.3 14.8 %collective-permute-start.6 = (bf16[4,192,128]{1,2,0:T(8,128)(2,1)S(1)}, bf16[4,192,128]{1,2,0:T(8,128)(2,1)S(1)}, u32[]{:S(2)}, u32[]{:S(2)}) collective-permute-start(bf16[4,192,128]{1,2,0:T(8,128)(2,1)S(1)} %slice.195), channel_id=1, source_target_pairs={{0,4},{2,6},{4,0},{6,2},{1,5},{3,7},{5,1},{7,3},{8,12},{10,14},{12... | collective-permute-start | bytes 589832 | tf_op jit(solution)/shard_map/ppermute | solution.py:22
  63.0 9.5 %collective-permute-start.7 = (bf16[4,192,128]{1,2,0:T(8,128)(2,1)S(1)}, bf16[4,192,128]{1,2,0:T(8,128)(2,1)S(1)}, u32[]{:S(2)}, u32[]{:S(2)}) collective-permute-start(bf16[4,192,128]{1,2,0:T(8,128)(2,1)S(1)} %slice.196), channel_id=1, source_target_pairs={{0,6},{2,0},{4,2},{6,4},{1,7},{3,1},{5,3},{7,5},{8,14},{10,8},{12,... | collective-permute-start | bytes 589832 | tf_op jit(solution)/shard_map/ppermute | solution.py:22
  72.7 10.1 %collective-permute-start.8 = (bf16[4,4,384,128]{2,3,0,1:T(8,128)(2,1)S(1)}, bf16[4,4,384,128]{2,3,0,1:T(8,128)(2,1)}, u32[]{:S(2)}, u32[]{:S(2)}) collective-permute-start(bf16[4,4,384,128]{2,3,0,1:T(8,128)(2,1)S(1)} %fusion.12), channel_id=1, source_target_pairs={{0,1},{1,0},{2,3},{3,2},{4,5},{5,4},{6,7},{7,6},{8,9},{9,8},{10,11... | collective-permute-start | bytes 4718600 | tf_op jit(solution)/shard_map/ppermute | solution.py:22
  74.7 4.8 %copy-start.3 = (f32[3,3,128]{2,1,0:T(4,128)S(1)}, f32[3,3,128]{2,1,0:T(4,128)}, u32[]{:S(2)}) copy-start(f32[3,3,128]{2,1,0:T(4,128)} %param.10) | copy-start | bytes 13828
  74.7 4.8 %copy-start.1 = (bf16[128,128]{1,0:T(8,128)(2,1)S(1)}, bf16[128,128]{1,0:T(8,128)(2,1)}, u32[]{:S(2)}) copy-start(bf16[128,128]{1,0:T(8,128)(2,1)} %param.11) | copy-start | bytes 98308
  82.7 2.6 %copy-start.2 = (f32[4096]{0:T(1024)S(1)}, f32[4096]{0:T(1024)}, u32[]{:S(2)}) copy-start(f32[4096]{0:T(1024)} %param.8) | copy-start | bytes 49156
  85.4 1.9 %copy-start = (bf16[4096,3,128]{0,2,1:T(8,128)(2,1)S(1)}, bf16[4096,3,128]{0,2,1:T(8,128)(2,1)}, u32[]{:S(2)}) copy-start(bf16[4096,3,128]{0,2,1:T(8,128)(2,1)} %copy.21) | copy-start | bytes 9437188
  89.1 6.3 %collective-permute-start.9 = (bf16[129,384]{1,0:T(8,128)(2,1)S(1)}, bf16[129,384]{1,0:T(8,128)(2,1)S(1)}, u32[]{:S(2)}, u32[]{:S(2)}) collective-permute-start(bf16[129,384]{1,0:T(8,128)(2,1)S(1)} %slice.197), channel_id=1, source_target_pairs={{0,32},{32,64},{64,96},{96,128},{128,160},{160,192},{192,224},{224... | collective-permute-start | bytes 297224 | tf_op jit(solution)/shard_map/ppermute | solution.py:18
  97.0 5.8 %copy-start.4 = (f32[128]{0:T(128)S(1)}, f32[128]{0:T(128)}, u32[]{:S(2)}) copy-start(f32[128]{0:T(128)} %param.12) | copy-start | bytes 1540
  105.6 5.3 %collective-permute-start.10 = (bf16[4,4,384,128]{2,3,1,0:T(8,128)(2,1)S(1)}, bf16[4,4,384,128]{2,3,1,0:T(8,128)(2,1)S(1)}, u32[]{:S(2)}, u32[]{:S(2)}) collective-permute-start(bf16[4,4,384,128]{2,3,1,0:T(8,128)(2,1)S(1)} %slice_bitcast_fusion), channel_id=1, source_target_pairs={{0,1},{1,0},{2,3},{3,2},{4,5},{5,4},{6,7},{7,6},{8,9},{9,8},{10,11... | collective-permute-start | bytes 4718600 | tf_op jit(solution)/shard_map/ppermute | solution.py:22
  111.7 11.5 %collective-permute-start.12 = (bf16[4,192,128]{1,2,0:T(8,128)(2,1)S(1)}, bf16[4,192,128]{1,2,0:T(8,128)(2,1)S(1)}, u32[]{:S(2)}, u32[]{:S(2)}) collective-permute-start(bf16[4,192,128]{1,2,0:T(8,128)(2,1)S(1)} %get-tuple-element.11), channel_id=1, source_target_pairs={{0,6},{2,0},{4,2},{6,4},{1,7},{3,1},{5,3},{7,5},{8,14},{10,8},{12,... | collective-permute-start | bytes 589832 | tf_op jit(solution)/shard_map/ppermute | solution.py:22
  113.6 14.6 %collective-permute-start.11 = (bf16[4,384,128]{1,2,0:T(8,128)(2,1)S(1)}, bf16[4,384,128]{1,2,0:T(8,128)(2,1)S(1)}, u32[]{:S(2)}, u32[]{:S(2)}) collective-permute-start(bf16[4,384,128]{1,2,0:T(8,128)(2,1)S(1)} %get-tuple-element.7), channel_id=1, source_target_pairs={{0,2},{2,4},{4,6},{6,0},{1,3},{3,5},{5,7},{7,1},{8,10},{10,12},{12... | collective-permute-start | bytes 1179656 | tf_op jit(solution)/shard_map/ppermute | solution.py:22
  123.4 19.1 %collective-permute-start.13 = (bf16[4,384,128]{1,2,0:T(8,128)(2,1)S(1)}, bf16[4,384,128]{1,2,0:T(8,128)(2,1)S(1)}, u32[]{:S(2)}, u32[]{:S(2)}) collective-permute-start(bf16[4,384,128]{1,2,0:T(8,128)(2,1)S(1)} %pad_maximum_fusion), channel_id=1, source_target_pairs={{0,6},{2,0},{4,2},{6,4},{1,7},{3,1},{5,3},{7,5},{8,14},{10,8},{12,... | collective-permute-start | bytes 1179656 | tf_op jit(solution)/shard_map/ppermute | solution.py:22
  125.3 17.5 %collective-permute-start.14 = (bf16[4,192,128]{1,2,0:T(8,128)(2,1)S(1)}, bf16[4,192,128]{1,2,0:T(8,128)(2,1)S(1)}, u32[]{:S(2)}, u32[]{:S(2)}) collective-permute-start(bf16[4,192,128]{1,2,0:T(8,128)(2,1)S(1)} %get-tuple-element.10), channel_id=1, source_target_pairs={{0,4},{2,6},{4,0},{6,2},{1,5},{3,7},{5,1},{7,3},{8,12},{10,14},{12... | collective-permute-start | bytes 589832 | tf_op jit(solution)/shard_map/ppermute | solution.py:22
  143.0 11.6 %collective-permute-start.16 = (bf16[192,128]{0,1:T(8,128)(2,1)S(1)}, bf16[192,128]{0,1:T(8,128)(2,1)S(1)}, u32[]{:S(2)}, u32[]{:S(2)}) collective-permute-start(bf16[192,128]{0,1:T(8,128)(2,1)S(1)} %slice_bitcast_fusion.8), channel_id=1, source_target_pairs={{0,24},{8,0},{16,8},{24,16},{1,25},{9,1},{17,9},{25,17},{2,26},{10... | collective-permute-start | bytes 147464 | tf_op jit(solution)/shard_map/ppermute | solution.py:22
  146.7 17.9 %collective-permute-start.15 = (bf16[384,128]{0,1:T(8,128)(2,1)S(1)}, bf16[384,128]{0,1:T(8,128)(2,1)S(1)}, u32[]{:S(2)}, u32[]{:S(2)}) collective-permute-start(bf16[384,128]{0,1:T(8,128)(2,1)S(1)} %fusion.25), channel_id=1, source_target_pairs={{0,8},{8,16},{16,24},{24,0},{1,9},{9,17},{17,25},{25,1},{2,10},{10... | collective-permute-start | bytes 294920 | tf_op jit(solution)/shard_map/ppermute | solution.py:22
  154.7 11.9 %collective-permute-start.17 = (bf16[384,128]{0,1:T(8,128)(2,1)S(1)}, bf16[384,128]{0,1:T(8,128)(2,1)S(1)}, u32[]{:S(2)}, u32[]{:S(2)}) collective-permute-start(bf16[384,128]{0,1:T(8,128)(2,1)S(1)} %pad_maximum_fusion.3), channel_id=1, source_target_pairs={{0,24},{8,0},{16,8},{24,16},{1,25},{9,1},{17,9},{25,17},{2,26},{10... | collective-permute-start | bytes 294920 | tf_op jit(solution)/shard_map/ppermute | solution.py:22
  157.6 16.6 %collective-permute-start.18 = (bf16[192,128]{0,1:T(8,128)(2,1)S(1)}, bf16[192,128]{0,1:T(8,128)(2,1)S(1)}, u32[]{:S(2)}, u32[]{:S(2)}) collective-permute-start(bf16[192,128]{0,1:T(8,128)(2,1)S(1)} %get-tuple-element.14), channel_id=1, source_target_pairs={{0,16},{8,24},{16,0},{24,8},{1,17},{9,25},{17,1},{25,9},{2,18},{10... | collective-permute-start | bytes 147464 | tf_op jit(solution)/shard_map/ppermute | solution.py:22

commit v7 on v5

--- a/solution.py
+++ b/solution.py
@@ -82,9 +82,12 @@
     taps = long_filter.shape[1]
     feat_len = feat_taps.shape[1]
     w_flat = w_in.reshape(width, 3 * chans)
-    stacked = bases_in
-    for name, size in CH_PARTS:
-        stacked = gathered(stacked, name, size)
+    stacked = lax.all_gather(bases_in, CH[0], axis=0)
+    half = tok // 2
+    stacked = jnp.concatenate(
+        [lax.all_gather(part, CH[1], axis=0) for part in (stacked[:, :half], stacked[:, half:])], axis=-2
+    )
+    stacked = gathered(stacked, CH[2], CH_PARTS[2][1])
     whole = stacked.transpose(3, 2, 1, 0, 4).reshape(tok, width)
     wide = whole.astype(jnp.float32)
     inverse = lax.rsqrt(jnp.mean(wide * wide, axis=1, keepdims=True) + 1e-05)

time: 159 us -> 159 us (level)
  blocking collectives: 105 us -> 125 us
  waiting for transfers between devices: 18.6 us -> 3.46 us
  starting transfers between devices: 7.78 us -> 3.61 us
  local copies, waits for them, and re-layouts: 12.7 us -> 11.1 us
    all_gather x0 -> x3, blocking collectives: none -> 57.3 us  [the longest x1 29.4 us: shards(): stacked = lax.all_gather(bases_in, CH[0], axis=0)]
    all_to_all x2 -> x1, blocking collectives: 47.2 us -> 6.26 us  [gathered(): return lax.all_to_all(copies, name, 0, 0)]
    all_to_all x1 -> x0, waiting for transfers between devices: 14.3 us -> none  [gathered(): return lax.all_to_all(copies, name, 0, 0)]
    all_to_all x1 -> x0, starting transfers between devices: 4.29 us -> none  [gathered(): return lax.all_to_all(copies, name, 0, 0)]
    all_to_all x3, blocking collectives: 57.7 us -> 61.9 us  [reduced(): parts = lax.all_to_all(stack, name, 0, 0)]
    unnamed x17 -> x16, local copies, waits for them, and re-layouts: 6.81 us -> 5.87 us
  transfers between devices with their start and end apart: 2 -> 1, of which waited for: 2 -> 1; matrix products, arithmetic and copies ran while one was open for 4% -> 1% of each run, Pallas kernels for 0% -> 0%
where the time goes in v7:
time: 159 us; the launch traced here: 158 us
  blocking collectives  125 us (79%)
  local copies, waits for them, and re-layouts  11.1 us (7%)
  other arithmetic  5.95 us (4%)
  Pallas kernels  4.33 us (3%)
  matrix products  3.93 us (2%)
  starting transfers between devices  3.61 us (2%)
  waiting for transfers between devices  3.46 us (2%)
    all_to_all x3, blocking collectives, reduced(): parts = lax.all_to_all(stack, name, 0, 0)  61.9 us
    all_gather x1, blocking collectives, shards(): stacked = lax.all_gather(bases_in, CH[0], axis=0)  29.4 us
    all_gather x2, blocking collectives, shards(): lax.all_gather(part, CH[1], axis=0)  27.9 us
    all_to_all x1, blocking collectives, gathered(): return lax.all_to_all(copies, name, 0, 0)  6.26 us
    unnamed x16, local copies, waits for them, and re-layouts  5.87 us
    pallas_call x1, Pallas kernels, causal_filter(): pl.pallas_call(filter_kernel, out_shape=jax.ShapeDtypeStruct((count, chan...  4.33 us
    ppermute x1, starting transfers between devices, passed_along(): lax.ppermute(value, axis, [(source, source + steps) for source in range(i...  3.61 us
    ppermute x1, waiting for transfers between devices, passed_along(): lax.ppermute(value, axis, [(source, source + steps) for source in range(i...  3.46 us
  transfers between devices with their start and end apart: 1, of which 1 were waited for; matrix products, arithmetic and copies ran while one was open for 1% of the time, Pallas kernels for 0%

profile of v7, /device:TPU:32, one launch (start us, length us, event | category | flops | bytes accessed | tf_op | source)
XLA Modules:
  0.0 158.1 jit_solution(2799865536181359741)
XLA Ops:
  0.0 29.4 %all-gather = bf16[1536,128]{1,0:T(8,128)(2,1)S(1)} all-gather(bf16[384,128]{1,0:T(8,128)(2,1)} %param.7), channel_id=2, replica_groups=mesh['z_lo'=4,'y'=4,'z_hi'=4,'x'=4,'core'=2] {'z_hi'}, dimensions={0}, use_global_device_ids=true | all-gather | bytes 491520 | tf_op jit(solution)/shard_map/all_gather | solution.py:85
  29.5 14.6 %all-gather.1 = bf16[16,192,128]{2,1,0:T(8,128)(2,1)S(1)} all-gather(bf16[4,192,128]{2,1,0:T(8,128)(2,1)S(1)} %get-tuple-element.5), channel_id=3, replica_groups=mesh['z_lo'=4,'y'=4,'z_hi'=4,'x'=4,'core'=2] {'x'}, dimensions={0}, use_global_device_ids=true | all-gather | bytes 983040 | tf_op jit(solution)/shard_map/all_gather | solution.py:88
  44.1 13.3 %all-gather.2 = bf16[16,192,128]{2,1,0:T(8,128)(2,1)S(1)} all-gather(bf16[4,192,128]{2,1,0:T(8,128)(2,1)S(1)} %get-tuple-element.6), channel_id=4, replica_groups=mesh['z_lo'=4,'y'=4,'z_hi'=4,'x'=4,'core'=2] {'x'}, dimensions={0}, use_global_device_ids=true | all-gather | bytes 983040 | tf_op jit(solution)/shard_map/all_gather | solution.py:88
  57.5 0.9 copy.41
  58.4 0.5 broadcast_in_dim.4
  58.8 6.3 %all_to_all.20 = bf16[2,4,4,384,128]{3,4,1,2,0:T(8,128)(2,1)S(1)} all-to-all(bf16[2,4,4,384,128]{3,4,1,2,0:T(8,128)(2,1)S(1)} %broadcast_in_dim.4), channel_id=1, replica_groups=mesh['z_lo'=4,'y'=4,'z_hi'=4,'x'=4,'core'=2] {'core'}, dimensions={0} | all-to-all | bytes 6291456 | tf_op jit(solution)/shard_map/all_to_all | solution.py:23
  65.1 0.8 fusion
  65.9 4.7 %copy.43 = bf16[4096,3,128]{0,2,1:T(8,128)(2,1)} copy(bf16[4096,3,128]{2,0,1:T(8,128)(2,1)} %param.9) | data formatting | bytes 6291456 | tf_op args[2]
  70.6 0.9 fusion.3
  71.5 1.0 copy-done
  72.5 1.8 %convolution_convert_fusion = bf16[384,384]{1,0:T(8,128)(2,1)S(1)} fusion(bf16[384,4096]{0,1:T(8,128)(2,1)S(1)} %bitcast.60, bf16[4096,384]{0,1:T(8,128)(2,1)S(1)} %bitcast.59), kind=kOutput, calls=%fused_computation.10 | convolution fusion | flops 1208107008 | bytes 6586368 | tf_op jit(solution)/shard_map/dot_general | solution.py:95
  74.4 3.6 %collective-permute-start = (bf16[129,384]{1,0:T(8,128)(2,1)S(1)}, bf16[129,384]{1,0:T(8,128)(2,1)S(1)}, u32[]{:S(2)}, u32[]{:S(2)}) collective-permute-start(bf16[129,384]{1,0:T(8,128)(2,1)S(1)} %slice.120), channel_id=1, source_target_pairs={{0,32},{32,64},{64,96},{96,128},{128,160},{160,192},{192,224},{224... | collective-permute-start | bytes 297224 | tf_op jit(solution)/shard_map/ppermute | solution.py:18
  78.2 0.6 convert_bitcast_fusion.1.filt_ref
  78.8 0.2 copy.44
  79.0 0.2 copy.45
  79.3 0.8 reshape.77
  80.0 3.5 %collective-permute-done = bf16[129,384]{1,0:T(8,128)(2,1)S(1)} collective-permute-done((bf16[129,384]{1,0:T(8,128)(2,1)S(1)}, bf16[129,384]{1,0:T(8,128)(2,1)S(1)}, u32[]{:S(2)}, u32[]{:S(2)}) %collective-permute-start) | collective-permute-done | bytes 99104 | tf_op jit(solution)/shard_map/ppermute | solution.py:18
  83.6 0.2 copy.46
  83.8 1.1 copy.47
  84.9 0.2 copy.48
  85.1 0.2 copy.49
  85.4 1.2 multiply_add_fusion
  86.8 0.1 copy.51
  87.6 0.8 maximum_convert_fusion.ext_ref
  88.4 4.3 %shard_map.73 = f32[384,128]{1,0:T(8,128)} custom-call(f32[512,128]{1,0:T(8,128)} %maximum_convert_fusion.ext_ref, f32[128,128]{1,0:T(8,128)} %convert_bitcast_fusion.1.filt_ref), custom_call_target="tpu_custom_call" | custom-call | tf_op jit(solution)/shard_map/pallas_call | solution.py:72
  92.7 2.1 %convert_bitcast_fusion = bf16[2,4,4,384,128]{4,3,2,1,0:T(8,128)(2,1)S(1)} fusion(bf16[128,4,4,2,128]{4,3,2,1,0:T(2,128)(2,1)S(1)} %reshape.77, f32[384,128]{1,0:T(8,128)} %shard_map.73, bf16[384,128]{1,0:T(8,128)(2,1)S(1)} %fusion.17, f32[384,3,128]{2,0,1:T(8,128)S(1)} %multiply_add_fusion, f32[128]{0:T(128)S(1)} %copy-done.5), kind=kOutput, calls=%fused_computation.7 | convolution fusion | flops 404471808 | bytes 4686336 | tf_op jit(solution)/shard_map/tk,cxzki->cxzti/dot_general | solution.py:112
  94.9 6.3 %all_to_all.21 = bf16[2,4,4,384,128]{4,3,2,1,0:T(8,128)(2,1)S(1)} all-to-all(bf16[2,4,4,384,128]{4,3,2,1,0:T(8,128)(2,1)S(1)} %convert_bitcast_fusion), channel_id=1, replica_groups=mesh['z_lo'=4,'y'=4,'z_hi'=4,'x'=4,'core'=2] {'core'}, dimensions={0} | all-to-all | bytes 6291456 | tf_op jit(solution)/shard_map/all_to_all | solution.py:27
  101.1 0.4 fusion.4
  101.5 24.6 %all_to_all.22 = bf16[4,4,384,128]{3,2,1,0:T(8,128)(2,1)S(1)} all-to-all(bf16[4,4,384,128]{3,2,1,0:T(8,128)(2,1)S(1)} %fusion.4), channel_id=1, replica_groups=mesh['z_lo'=4,'y'=4,'z_hi'=4,'x'=4,'core'=2] {'x'}, dimensions={0} | all-to-all | bytes 3145728 | tf_op jit(solution)/shard_map/all_to_all | solution.py:27
  126.1 0.2 fusion.7
  126.3 31.0 %all_to_all.23 = bf16[4,384,128]{2,1,0:T(8,128)(2,1)S(1)} all-to-all(bf16[4,384,128]{2,1,0:T(8,128)(2,1)S(1)} %fusion.7), channel_id=1, replica_groups=mesh['z_lo'=4,'y'=4,'z_hi'=4,'x'=4,'core'=2] {'z_hi'}, dimensions={0} | all-to-all | bytes 786432 | tf_op jit(solution)/shard_map/all_to_all | solution.py:27
  157.4 0.7 fusion.14
  (31 shorter events, 1.3 us)
Async XLA Ops:
  65.9 4.7 %copy-start.3 = (f32[4096]{0:T(1024)S(1)}, f32[4096]{0:T(1024)}, u32[]{:S(2)}) copy-start(f32[4096]{0:T(1024)} %param.8) | copy-start | bytes 49156
  70.6 1.9 %copy-start = (bf16[4096,3,128]{0,2,1:T(8,128)(2,1)S(1)}, bf16[4096,3,128]{0,2,1:T(8,128)(2,1)}, u32[]{:S(2)}) copy-start(bf16[4096,3,128]{0,2,1:T(8,128)(2,1)} %copy.43) | copy-start | bytes 9437188
  72.5 5.5 %copy-start.4 = (f32[3,3,128]{2,1,0:T(4,128)S(1)}, f32[3,3,128]{2,1,0:T(4,128)}, u32[]{:S(2)}) copy-start(f32[3,3,128]{2,1,0:T(4,128)} %param.10) | copy-start | bytes 13828
  72.5 5.5 %copy-start.2 = (bf16[128,128]{1,0:T(8,128)(2,1)S(1)}, bf16[128,128]{1,0:T(8,128)(2,1)}, u32[]{:S(2)}) copy-start(bf16[128,128]{1,0:T(8,128)(2,1)} %param.11) | copy-start | bytes 98308
  74.3 4.9 %copy-start.1 = (bf16[128,4096]{1,0:T(8,128)(2,1)S(1)}, bf16[128,4096]{1,0:T(8,128)(2,1)}, u32[]{:S(2)}) copy-start(bf16[128,4096]{1,0:T(8,128)(2,1)} %param.13) | copy-start | bytes 3145732
  74.4 9.1 %collective-permute-start = (bf16[129,384]{1,0:T(8,128)(2,1)S(1)}, bf16[129,384]{1,0:T(8,128)(2,1)S(1)}, u32[]{:S(2)}, u32[]{:S(2)}) collective-permute-start(bf16[129,384]{1,0:T(8,128)(2,1)S(1)} %slice.120), channel_id=1, source_target_pairs={{0,32},{32,64},{64,96},{96,128},{128,160},{160,192},{192,224},{224... | collective-permute-start | bytes 297224 | tf_op jit(solution)/shard_map/ppermute | solution.py:18
  86.5 6.2 %copy-start.5 = (f32[128]{0:T(128)S(1)}, f32[128]{0:T(128)}, u32[]{:S(2)}) copy-start(f32[128]{0:T(128)} %param.12) | copy-start | bytes 1540

commit v8 on v5

--- a/solution.py
+++ b/solution.py
@@ -82,8 +82,8 @@
     taps = long_filter.shape[1]
     feat_len = feat_taps.shape[1]
     w_flat = w_in.reshape(width, 3 * chans)
-    stacked = bases_in
-    for name, size in CH_PARTS:
+    stacked = lax.all_gather(bases_in, CH[0], axis=0)
+    for name, size in CH_PARTS[1:]:
         stacked = gathered(stacked, name, size)
     whole = stacked.transpose(3, 2, 1, 0, 4).reshape(tok, width)
     wide = whole.astype(jnp.float32)

time: 159 us -> 148 us (0.931)
  blocking collectives: 105 us -> 97.4 us
  waiting for transfers between devices: 18.6 us -> 15.9 us
    all_to_all x2 -> x1, blocking collectives: 47.2 us -> 6.26 us  [gathered(): return lax.all_to_all(copies, name, 0, 0)]
    all_gather x0 -> x1, blocking collectives: none -> 29.4 us  [shards(): stacked = lax.all_gather(bases_in, CH[0], axis=0)]
    all_to_all x3, blocking collectives: 57.7 us -> 61.7 us  [reduced(): parts = lax.all_to_all(stack, name, 0, 0)]
    all_to_all x1, waiting for transfers between devices: 14.3 us -> 11.4 us  [gathered(): return lax.all_to_all(copies, name, 0, 0)]
    unnamed x17 -> x16, local copies, waits for them, and re-layouts: 6.81 us -> 5.8 us
  transfers between devices with their start and end apart: 2 -> 2, of which waited for: 2 -> 2; matrix products, arithmetic and copies ran while one was open for 4% -> 5% of each run, Pallas kernels for 0% -> 0%
where the time goes in v8:
time: 148 us; the launch traced here: 147 us
  blocking collectives  97.4 us (66%)
  waiting for transfers between devices  15.9 us (11%)
  local copies, waits for them, and re-layouts  11.9 us (8%)
  starting transfers between devices  7.78 us (5%)
  other arithmetic  5.94 us (4%)
  Pallas kernels  4.33 us (3%)
  matrix products  3.95 us (3%)
    all_to_all x3, blocking collectives, reduced(): parts = lax.all_to_all(stack, name, 0, 0)  61.7 us
    all_gather x1, blocking collectives, shards(): stacked = lax.all_gather(bases_in, CH[0], axis=0)  29.4 us
    all_to_all x1, waiting for transfers between devices, gathered(): return lax.all_to_all(copies, name, 0, 0)  11.4 us
    all_to_all x1, blocking collectives, gathered(): return lax.all_to_all(copies, name, 0, 0)  6.26 us
    unnamed x16, local copies, waits for them, and re-layouts  5.8 us
    ppermute x1, waiting for transfers between devices, passed_along(): lax.ppermute(value, axis, [(source, source + steps) for source in range(i...  4.54 us
    pallas_call x1, Pallas kernels, causal_filter(): pl.pallas_call(filter_kernel, out_shape=jax.ShapeDtypeStruct((count, chan...  4.33 us
    all_to_all x1, starting transfers between devices, gathered(): return lax.all_to_all(copies, name, 0, 0)  4.29 us
  transfers between devices with their start and end apart: 2, of which 2 were waited for; matrix products, arithmetic and copies ran while one was open for 5% of the time, Pallas kernels for 0%

profile of v8, /device:TPU:32, one launch (start us, length us, event | category | flops | bytes accessed | tf_op | source)
XLA Modules:
  0.0 147.4 jit_solution(8750216219662741412)
XLA Ops:
  0.0 29.4 %all-gather = bf16[1536,128]{1,0:T(8,128)(2,1)S(1)} all-gather(bf16[384,128]{1,0:T(8,128)(2,1)} %param.7), channel_id=2, replica_groups=mesh['z_lo'=4,'y'=4,'z_hi'=4,'x'=4,'core'=2] {'z_hi'}, dimensions={0}, use_global_device_ids=true | all-gather | bytes 491520 | tf_op jit(solution)/shard_map/all_gather | solution.py:85
  29.4 0.2 copy.26
  29.7 1.4 broadcast_in_dim.6
  31.0 4.3 %all-to-all-start = ((bf16[4,4,384,128]{2,3,1,0:T(8,128)(2,1)}), bf16[4,4,384,128]{2,3,1,0:T(8,128)(2,1)S(1)}, u32[]{:S(2)}, u32[]{:S(2)}) async-start(bf16[4,4,384,128]{2,3,1,0:T(8,128)(2,1)} %broadcast_in_dim.6), calls=%async_computation | async-start | bytes 3145728 | tf_op jit(solution)/shard_map/all_to_all | solution.py:23
  35.3 4.7 %copy.29 = bf16[4096,3,128]{0,2,1:T(8,128)(2,1)} copy(bf16[4096,3,128]{2,0,1:T(8,128)(2,1)} %param.9) | data formatting | bytes 6291456 | tf_op args[2]
  40.2 0.6 convert_bitcast_fusion.1.filt_ref
  40.8 11.4 %all-to-all-done = bf16[4,4,384,128]{2,3,1,0:T(8,128)(2,1)S(1)} async-done(((bf16[4,4,384,128]{2,3,1,0:T(8,128)(2,1)}), bf16[4,4,384,128]{2,3,1,0:T(8,128)(2,1)S(1)}, u32[]{:S(2)}, u32[]{:S(2)}) %all-to-all-start) | async-done | bytes 1572896 | tf_op jit(solution)/shard_map/all_to_all | solution.py:23
  52.2 0.2 copy.27
  52.4 0.5 broadcast_in_dim.7
  52.9 6.3 %all_to_all.25 = bf16[2,4,4,384,128]{3,4,1,2,0:T(8,128)(2,1)S(1)} all-to-all(bf16[2,4,4,384,128]{3,4,1,2,0:T(8,128)(2,1)S(1)} %broadcast_in_dim.7), channel_id=1, replica_groups=mesh['z_lo'=4,'y'=4,'z_hi'=4,'x'=4,'core'=2] {'core'}, dimensions={0} | all-to-all | bytes 6291456 | tf_op jit(solution)/shard_map/all_to_all | solution.py:23
  59.1 0.8 fusion
  60.0 0.9 fusion.3
  60.9 1.0 copy-done
  61.8 1.8 %convolution_convert_fusion = bf16[384,384]{1,0:T(8,128)(2,1)S(1)} fusion(bf16[384,4096]{0,1:T(8,128)(2,1)S(1)} %bitcast.58, bf16[4096,384]{0,1:T(8,128)(2,1)S(1)} %bitcast.57), kind=kOutput, calls=%fused_computation.9 | convolution fusion | flops 1208107008 | bytes 6586368 | tf_op jit(solution)/shard_map/dot_general | solution.py:92
  63.7 3.5 %collective-permute-start = (bf16[129,384]{1,0:T(8,128)(2,1)S(1)}, bf16[129,384]{1,0:T(8,128)(2,1)S(1)}, u32[]{:S(2)}, u32[]{:S(2)}) collective-permute-start(bf16[129,384]{1,0:T(8,128)(2,1)S(1)} %slice.110), channel_id=1, source_target_pairs={{0,32},{32,64},{64,96},{96,128},{128,160},{160,192},{192,224},{224... | collective-permute-start | bytes 297224 | tf_op jit(solution)/shard_map/ppermute | solution.py:18
  67.2 0.8 reshape.78
  68.2 0.2 copy.31
  68.4 4.5 %collective-permute-done = bf16[129,384]{1,0:T(8,128)(2,1)S(1)} collective-permute-done((bf16[129,384]{1,0:T(8,128)(2,1)S(1)}, bf16[129,384]{1,0:T(8,128)(2,1)S(1)}, u32[]{:S(2)}, u32[]{:S(2)}) %collective-permute-start) | collective-permute-done | bytes 99104 | tf_op jit(solution)/shard_map/ppermute | solution.py:18
  73.1 0.2 copy.32
  73.3 1.1 copy.33
  74.4 0.2 copy.34
  74.6 0.2 copy.35
  74.8 1.2 multiply_add_fusion
  77.1 0.8 maximum_convert_fusion.ext_ref
  77.9 4.3 %shard_map.73 = f32[384,128]{1,0:T(8,128)} custom-call(f32[512,128]{1,0:T(8,128)} %maximum_convert_fusion.ext_ref, f32[128,128]{1,0:T(8,128)} %convert_bitcast_fusion.1.filt_ref), custom_call_target="tpu_custom_call" | custom-call | tf_op jit(solution)/shard_map/pallas_call | solution.py:72
  82.3 2.1 %convert_bitcast_fusion = bf16[2,4,4,384,128]{4,3,2,1,0:T(8,128)(2,1)S(1)} fusion(bf16[128,4,4,2,128]{4,3,2,1,0:T(2,128)(2,1)S(1)} %reshape.78, f32[384,128]{1,0:T(8,128)} %shard_map.73, bf16[384,128]{1,0:T(8,128)(2,1)S(1)} %fusion.17, f32[384,3,128]{2,0,1:T(8,128)S(1)} %multiply_add_fusion, f32[128]{0:T(128)S(1)} %copy-done.5), kind=kOutput, calls=%fused_computation.7 | convolution fusion | flops 404471808 | bytes 4686336 | tf_op jit(solution)/shard_map/tk,cxzki->cxzti/dot_general | solution.py:109
  84.4 6.3 %all_to_all.26 = bf16[2,4,4,384,128]{4,3,2,1,0:T(8,128)(2,1)S(1)} all-to-all(bf16[2,4,4,384,128]{4,3,2,1,0:T(8,128)(2,1)S(1)} %convert_bitcast_fusion), channel_id=1, replica_groups=mesh['z_lo'=4,'y'=4,'z_hi'=4,'x'=4,'core'=2] {'core'}, dimensions={0} | all-to-all | bytes 6291456 | tf_op jit(solution)/shard_map/all_to_all | solution.py:27
  90.7 0.4 fusion.4
  91.1 23.7 %all_to_all.27 = bf16[4,4,384,128]{3,2,1,0:T(8,128)(2,1)S(1)} all-to-all(bf16[4,4,384,128]{3,2,1,0:T(8,128)(2,1)S(1)} %fusion.4), channel_id=1, replica_groups=mesh['z_lo'=4,'y'=4,'z_hi'=4,'x'=4,'core'=2] {'x'}, dimensions={0} | all-to-all | bytes 3145728 | tf_op jit(solution)/shard_map/all_to_all | solution.py:27
  114.8 0.2 fusion.7
  115.0 31.7 %all_to_all.28 = bf16[4,384,128]{2,1,0:T(8,128)(2,1)S(1)} all-to-all(bf16[4,384,128]{2,1,0:T(8,128)(2,1)S(1)} %fusion.7), channel_id=1, replica_groups=mesh['z_lo'=4,'y'=4,'z_hi'=4,'x'=4,'core'=2] {'z_hi'}, dimensions={0} | all-to-all | bytes 786432 | tf_op jit(solution)/shard_map/all_to_all | solution.py:27
  146.7 0.7 fusion.14
  (31 shorter events, 1.5 us)
Async XLA Ops:
  31.0 21.2 %all-to-all-start = ((bf16[4,4,384,128]{2,3,1,0:T(8,128)(2,1)}), bf16[4,4,384,128]{2,3,1,0:T(8,128)(2,1)S(1)}, u32[]{:S(2)}, u32[]{:S(2)}) async-start(bf16[4,4,384,128]{2,3,1,0:T(8,128)(2,1)} %broadcast_in_dim.6), calls=%async_computation | async-start | bytes 3145728 | tf_op jit(solution)/shard_map/all_to_all | solution.py:23
  35.3 4.7 %copy-start.2 = (bf16[128,128]{1,0:T(8,128)(2,1)S(1)}, bf16[128,128]{1,0:T(8,128)(2,1)}, u32[]{:S(2)}) copy-start(bf16[128,128]{1,0:T(8,128)(2,1)} %param.11) | copy-start | bytes 98308
  35.3 4.8 %copy-start.4 = (f32[3,3,128]{2,1,0:T(4,128)S(1)}, f32[3,3,128]{2,1,0:T(4,128)}, u32[]{:S(2)}) copy-start(f32[3,3,128]{2,1,0:T(4,128)} %param.10) | copy-start | bytes 13828
  59.1 0.8 copy-start.3
  59.9 1.9 %copy-start = (bf16[4096,3,128]{0,2,1:T(8,128)(2,1)S(1)}, bf16[4096,3,128]{0,2,1:T(8,128)(2,1)}, u32[]{:S(2)}) copy-start(bf16[4096,3,128]{0,2,1:T(8,128)(2,1)} %copy.29) | copy-start | bytes 9437188
  61.8 5.4 %copy-start.1 = (bf16[128,4096]{1,0:T(8,128)(2,1)S(1)}, bf16[128,4096]{1,0:T(8,128)(2,1)}, u32[]{:S(2)}) copy-start(bf16[128,4096]{1,0:T(8,128)(2,1)} %param.13) | copy-start | bytes 3145732
  63.7 9.3 %collective-permute-start = (bf16[129,384]{1,0:T(8,128)(2,1)S(1)}, bf16[129,384]{1,0:T(8,128)(2,1)S(1)}, u32[]{:S(2)}, u32[]{:S(2)}) collective-permute-start(bf16[129,384]{1,0:T(8,128)(2,1)S(1)} %slice.110), channel_id=1, source_target_pairs={{0,32},{32,64},{64,96},{96,128},{128,160},{160,192},{192,224},{224... | collective-permute-start | bytes 297224 | tf_op jit(solution)/shard_map/ppermute | solution.py:18
  76.0 6.2 %copy-start.5 = (f32[128]{0:T(128)S(1)}, f32[128]{0:T(128)}, u32[]{:S(2)}) copy-start(f32[128]{0:T(128)} %param.12) | copy-start | bytes 1540

commit v9 on v8

--- a/solution.py
+++ b/solution.py
@@ -106,10 +106,16 @@
     gated = (query * (filtered + skip_gain * product.astype(jnp.float32))).astype(jnp.bfloat16)
     sizes = [size for _, size in CH_PARTS]
     blocks = w_out.reshape(chans, *sizes, chans).transpose(3, 2, 1, 0, 4)
+    core = lax.axis_index(CH[2])
+    mine = lax.dynamic_index_in_dim(blocks, core, 0, keepdims=False)
+    theirs = lax.dynamic_index_in_dim(blocks, 1 - core, 0, keepdims=False)
+    partner = lambda value: lax.ppermute(value, CH[2], [(0, 1), (1, 0)])
+    pair_gated = jnp.concatenate([gated, partner(gated)], axis=1)
+    pair_rows = jnp.concatenate([mine, partner(theirs)], axis=2)
     split = jnp.einsum(
-        "tk,cxzki->cxzti", gated, blocks, preferred_element_type=jnp.float32
+        "tk,xzki->xzti", pair_gated, pair_rows, preferred_element_type=jnp.float32
     ).astype(jnp.bfloat16)
-    for name, size in CH_PARTS[::-1]:
+    for name, size in CH_PARTS[1::-1]:
         split = reduced(split, name, size).astype(jnp.bfloat16)
     return split
 

time: 148 us -> 143 us (0.966)
  blocking collectives: 97.4 us -> 91.1 us
  starting transfers between devices: 7.78 us -> 11.6 us
  waiting for transfers between devices: 15.9 us -> 14.1 us
    all_to_all x3 -> x2, blocking collectives: 61.7 us -> 55.4 us  [reduced(): parts = lax.all_to_all(stack, name, 0, 0)]
    ppermute x0 -> x2, starting transfers between devices: none -> 3.84 us  [shards(): partner = lambda value: lax.ppermute(value, CH[2], [(0, 1), (1, 0)])]
    all_to_all x1, waiting for transfers between devices: 11.4 us -> 7.6 us  [gathered(): return lax.all_to_all(copies, name, 0, 0)]
    unnamed x16 -> x17, local copies, waits for them, and re-layouts: 5.8 us -> 7.54 us
  transfers between devices with their start and end apart: 2 -> 4, of which waited for: 2 -> 3; matrix products, arithmetic and copies ran while one was open for 5% -> 11% of each run, Pallas kernels for 0% -> 3%
where the time goes in v9:
time: 143 us
  blocking collectives  91.1 us (64%)
  waiting for transfers between devices  14.1 us (10%)
  local copies, waits for them, and re-layouts  12.9 us (9%)
  starting transfers between devices  11.6 us (8%)
  other arithmetic  4.76 us (3%)
  Pallas kernels  4.35 us (3%)
  matrix products  3.6 us (3%)
    all_to_all x2, blocking collectives, reduced(): parts = lax.all_to_all(stack, name, 0, 0)  55.4 us
    all_gather x1, blocking collectives, shards(): stacked = lax.all_gather(bases_in, CH[0], axis=0)  29.4 us
    all_to_all x1, waiting for transfers between devices, gathered(): return lax.all_to_all(copies, name, 0, 0)  7.6 us
    unnamed x17, local copies, waits for them, and re-layouts  7.54 us
    all_to_all x1, blocking collectives, gathered(): return lax.all_to_all(copies, name, 0, 0)  6.26 us
    ppermute x1, waiting for transfers between devices, passed_along(): lax.ppermute(value, axis, [(source, source + steps) for source in range(i...  5.33 us
    pallas_call x1, Pallas kernels, causal_filter(): pl.pallas_call(filter_kernel, out_shape=jax.ShapeDtypeStruct((count, chan...  4.35 us
    all_to_all x1, starting transfers between devices, gathered(): return lax.all_to_all(copies, name, 0, 0)  4.29 us
  transfers between devices with their start and end apart: 4, of which 3 were waited for; matrix products, arithmetic and copies ran while one was open for 11% of the time, Pallas kernels for 3%

profile of v9, /device:TPU:32, one launch (start us, length us, event | category | flops | bytes accessed | tf_op | source)
XLA Modules:
  0.0 142.8 jit_solution(5829295515114039108)
XLA Ops:
  0.0 29.4 %all-gather = bf16[1536,128]{1,0:T(8,128)(2,1)S(1)} all-gather(bf16[384,128]{1,0:T(8,128)(2,1)} %param.7), channel_id=2, replica_groups=mesh['z_lo'=4,'y'=4,'z_hi'=4,'x'=4,'core'=2] {'z_hi'}, dimensions={0}, use_global_device_ids=true | all-gather | bytes 491520 | tf_op jit(solution)/shard_map/all_gather | solution.py:85
  29.4 0.2 copy.32
  29.7 1.4 broadcast_in_dim.6
  31.0 4.3 %all-to-all-start = ((bf16[4,4,384,128]{2,3,1,0:T(8,128)(2,1)}), bf16[4,4,384,128]{2,3,1,0:T(8,128)(2,1)S(1)}, u32[]{:S(2)}, u32[]{:S(2)}) async-start(bf16[4,4,384,128]{2,3,1,0:T(8,128)(2,1)} %broadcast_in_dim.6), calls=%async_computation | async-start | bytes 3145728 | tf_op jit(solution)/shard_map/all_to_all | solution.py:23
  35.3 1.6 %copy.29 = bf16[128,4096]{0,1:T(8,128)(2,1)S(1)} copy(bf16[128,4096]{1,0:T(8,128)(2,1)} %param.13) | data formatting | bytes 2097152 | tf_op args[6]
  37.1 1.9 %collective-permute-start = (bf16[4,4,128,128]{2,3,1,0:T(8,128)(2,1)S(1)}, bf16[4,4,128,128]{2,3,1,0:T(8,128)(2,1)}, u32[]{:S(2)}, u32[]{:S(2)}) collective-permute-start(bf16[4,4,128,128]{2,3,1,0:T(8,128)(2,1)S(1)} %bitcast.72), channel_id=1, source_target_pairs={{0,1},{1,0},{2,3},{3,2},{4,5},{5,4},{6,7},{7,6},{8,9},{9,8},{10,11... | collective-permute-start | bytes 1572872 | tf_op jit(solution)/shard_map/ppermute | solution.py:112
  39.0 4.8 %copy.35 = bf16[4096,3,128]{0,2,1:T(8,128)(2,1)} copy(bf16[4096,3,128]{2,0,1:T(8,128)(2,1)} %param.9) | data formatting | bytes 6291456 | tf_op args[2]
  43.9 0.6 convert_bitcast_fusion.filt_ref
  44.6 7.6 %all-to-all-done = bf16[4,4,384,128]{2,3,1,0:T(8,128)(2,1)S(1)} async-done(((bf16[4,4,384,128]{2,3,1,0:T(8,128)(2,1)}), bf16[4,4,384,128]{2,3,1,0:T(8,128)(2,1)S(1)}, u32[]{:S(2)}, u32[]{:S(2)}) %all-to-all-start) | async-done | bytes 1572896 | tf_op jit(solution)/shard_map/all_to_all | solution.py:23
  52.4 0.5 broadcast_in_dim.7
  52.9 6.3 %all_to_all.20 = bf16[2,4,4,384,128]{3,4,1,2,0:T(8,128)(2,1)S(1)} all-to-all(bf16[2,4,4,384,128]{3,4,1,2,0:T(8,128)(2,1)S(1)} %broadcast_in_dim.7), channel_id=1, replica_groups=mesh['z_lo'=4,'y'=4,'z_hi'=4,'x'=4,'core'=2] {'core'}, dimensions={0} | all-to-all | bytes 6291456 | tf_op jit(solution)/shard_map/all_to_all | solution.py:23
  59.1 0.8 fusion
  59.9 0.9 fusion.3
  60.9 1.0 copy-done
  61.8 1.8 %convolution_convert_fusion.1 = bf16[384,384]{1,0:T(8,128)(2,1)S(1)} fusion(bf16[384,4096]{0,1:T(8,128)(2,1)S(1)} %bitcast.64, bf16[4096,384]{0,1:T(8,128)(2,1)S(1)} %bitcast.63), kind=kOutput, calls=%fused_computation.8 | convolution fusion | flops 1208107008 | bytes 6586368 | tf_op jit(solution)/shard_map/dot_general | solution.py:92
  63.7 3.5 %collective-permute-start.1 = (bf16[129,384]{1,0:T(8,128)(2,1)S(1)}, bf16[129,384]{1,0:T(8,128)(2,1)S(1)}, u32[]{:S(2)}, u32[]{:S(2)}) collective-permute-start(bf16[129,384]{1,0:T(8,128)(2,1)S(1)} %slice.102), channel_id=1, source_target_pairs={{0,32},{32,64},{64,96},{96,128},{128,160},{160,192},{192,224},{224... | collective-permute-start | bytes 297224 | tf_op jit(solution)/shard_map/ppermute | solution.py:18
  67.4 0.2 copy.37
  67.6 5.3 %collective-permute-done.1 = bf16[129,384]{1,0:T(8,128)(2,1)S(1)} collective-permute-done((bf16[129,384]{1,0:T(8,128)(2,1)S(1)}, bf16[129,384]{1,0:T(8,128)(2,1)S(1)}, u32[]{:S(2)}, u32[]{:S(2)}) %collective-permute-start.1) | collective-permute-done | bytes 99104 | tf_op jit(solution)/shard_map/ppermute | solution.py:18
  73.1 0.2 copy.38
  73.3 0.2 copy.39
  73.6 0.2 copy.40
  73.8 0.2 copy.41
  75.2 0.8 maximum_convert_fusion.ext_ref
  76.0 4.4 %shard_map.73 = f32[384,128]{1,0:T(8,128)} custom-call(f32[512,128]{1,0:T(8,128)} %maximum_convert_fusion.ext_ref, f32[128,128]{1,0:T(8,128)} %convert_bitcast_fusion.filt_ref), custom_call_target="tpu_custom_call" | custom-call | tf_op jit(solution)/shard_map/pallas_call | solution.py:72
  80.4 1.0 fusion.14
  81.3 1.9 %collective-permute-start.2 = (bf16[384,128]{1,0:T(8,128)(2,1)S(1)}, bf16[384,128]{1,0:T(8,128)(2,1)S(1)}, u32[]{:S(2)}, u32[]{:S(2)}) collective-permute-start(bf16[384,128]{1,0:T(8,128)(2,1)S(1)} %fusion.14), channel_id=1, source_target_pairs={{0,1},{1,0},{2,3},{3,2},{4,5},{5,4},{6,7},{7,6},{8,9},{9,8},{10,11... | collective-permute-start | bytes 294920 | tf_op jit(solution)/shard_map/ppermute | solution.py:112
  83.3 1.2 collective-permute-done.2
  84.5 1.8 %fusion.4 = bf16[4,4,384,128]{2,3,1,0:T(8,128)(2,1)S(1)} fusion(bf16[4,4,128,128]{2,3,1,0:T(8,128)(2,1)} %collective-permute-done, bf16[4,4,128,128]{2,3,1,0:T(8,128)(2,1)S(1)} %bitcast.73, bf16[384,128]{1,0:T(8,128)(2,1)S(1)} %collective-permute-done.2, bf16[384,128]{1,0:T(8,128)(2,1)S(1)} %fusion.14), kind=kOutput, calls=%fused_computation.7 | convolution fusion | flops 405929984 | bytes 2818048 | tf_op jit(solution)/shard_map/tk,xzki->xzti/dot_general | solution.py:115
  86.3 23.8 %all_to_all.21 = bf16[4,4,384,128]{2,3,1,0:T(8,128)(2,1)S(1)} all-to-all(bf16[4,4,384,128]{2,3,1,0:T(8,128)(2,1)S(1)} %fusion.4), channel_id=1, replica_groups=mesh['z_lo'=4,'y'=4,'z_hi'=4,'x'=4,'core'=2] {'x'}, dimensions={0} | all-to-all | bytes 3145728 | tf_op jit(solution)/shard_map/all_to_all | solution.py:27
  110.1 0.2 fusion.8
  110.3 31.7 %all_to_all.22 = bf16[4,384,128]{1,2,0:T(8,128)(2,1)S(1)} all-to-all(bf16[4,384,128]{1,2,0:T(8,128)(2,1)S(1)} %fusion.8), channel_id=1, replica_groups=mesh['z_lo'=4,'y'=4,'z_hi'=4,'x'=4,'core'=2] {'z_hi'}, dimensions={0} | all-to-all | bytes 786432 | tf_op jit(solution)/shard_map/all_to_all | solution.py:27
  142.0 0.8 copy.49
  (36 shorter events, 2.0 us)
Async XLA Ops:
  31.0 21.2 %all-to-all-start = ((bf16[4,4,384,128]{2,3,1,0:T(8,128)(2,1)}), bf16[4,4,384,128]{2,3,1,0:T(8,128)(2,1)S(1)}, u32[]{:S(2)}, u32[]{:S(2)}) async-start(bf16[4,4,384,128]{2,3,1,0:T(8,128)(2,1)} %broadcast_in_dim.6), calls=%async_computation | async-start | bytes 3145728 | tf_op jit(solution)/shard_map/all_to_all | solution.py:23
  37.1 6.7 %copy-start.1 = (bf16[128,128]{1,0:T(8,128)(2,1)S(1)}, bf16[128,128]{1,0:T(8,128)(2,1)}, u32[]{:S(2)}) copy-start(bf16[128,128]{1,0:T(8,128)(2,1)} %param.11) | copy-start | bytes 98308
  37.1 6.8 %copy-start.3 = (f32[3,3,128]{2,1,0:T(4,128)S(1)}, f32[3,3,128]{2,1,0:T(4,128)}, u32[]{:S(2)}) copy-start(f32[3,3,128]{2,1,0:T(4,128)} %param.10) | copy-start | bytes 13828
  37.1 46.2 %collective-permute-start = (bf16[4,4,128,128]{2,3,1,0:T(8,128)(2,1)S(1)}, bf16[4,4,128,128]{2,3,1,0:T(8,128)(2,1)}, u32[]{:S(2)}, u32[]{:S(2)}) collective-permute-start(bf16[4,4,128,128]{2,3,1,0:T(8,128)(2,1)S(1)} %bitcast.72), channel_id=1, source_target_pairs={{0,1},{1,0},{2,3},{3,2},{4,5},{5,4},{6,7},{7,6},{8,9},{9,8},{10,11... | collective-permute-start | bytes 1572872 | tf_op jit(solution)/shard_map/ppermute | solution.py:112
  59.1 0.8 copy-start.2
  59.9 1.9 %copy-start = (bf16[4096,3,128]{0,2,1:T(8,128)(2,1)S(1)}, bf16[4096,3,128]{0,2,1:T(8,128)(2,1)}, u32[]{:S(2)}) copy-start(bf16[4096,3,128]{0,2,1:T(8,128)(2,1)} %copy.35) | copy-start | bytes 9437188
  63.7 9.3 %collective-permute-start.1 = (bf16[129,384]{1,0:T(8,128)(2,1)S(1)}, bf16[129,384]{1,0:T(8,128)(2,1)S(1)}, u32[]{:S(2)}, u32[]{:S(2)}) collective-permute-start(bf16[129,384]{1,0:T(8,128)(2,1)S(1)} %slice.102), channel_id=1, source_target_pairs={{0,32},{32,64},{64,96},{96,128},{128,160},{160,192},{192,224},{224... | collective-permute-start | bytes 297224 | tf_op jit(solution)/shard_map/ppermute | solution.py:18
  74.1 6.2 %copy-start.4 = (f32[128]{0:T(128)S(1)}, f32[128]{0:T(128)}, u32[]{:S(2)}) copy-start(f32[128]{0:T(128)} %param.12) | copy-start | bytes 1540
  81.3 3.2 %collective-permute-start.2 = (bf16[384,128]{1,0:T(8,128)(2,1)S(1)}, bf16[384,128]{1,0:T(8,128)(2,1)S(1)}, u32[]{:S(2)}, u32[]{:S(2)}) collective-permute-start(bf16[384,128]{1,0:T(8,128)(2,1)S(1)} %fusion.14), channel_id=1, source_target_pairs={{0,1},{1,0},{2,3},{3,2},{4,5},{5,4},{6,7},{7,6},{8,9},{9,8},{10,11... | collective-permute-start | bytes 294920 | tf_op jit(solution)/shard_map/ppermute | solution.py:112

commit v10 on v9

--- a/solution.py
+++ b/solution.py
@@ -28,6 +28,16 @@
     total = parts[0].astype(jnp.float32)
     for member in range(1, count):
         total = total + parts[member].astype(jnp.float32)
+    return total
+
+
+def reduced_by_shifts(stack, name, count):
+    index = lax.axis_index(name)
+    total = lax.dynamic_index_in_dim(stack, index, 0, keepdims=False).astype(jnp.float32)
+    for shift in range(1, count):
+        part = lax.dynamic_index_in_dim(stack, (index + shift) % count, 0, keepdims=False)
+        got = lax.ppermute(part, name, [(k, (k + shift) % count) for k in range(count)])
+        total = total + got.astype(jnp.float32)
     return total
 
 
@@ -115,9 +125,14 @@
     split = jnp.einsum(
         "tk,xzki->xzti", pair_gated, pair_rows, preferred_element_type=jnp.float32
     ).astype(jnp.bfloat16)
-    for name, size in CH_PARTS[1::-1]:
-        split = reduced(split, name, size).astype(jnp.bfloat16)
-    return split
+    half = tok // 2
+    (x_name, x_size), (z_name, z_size) = CH_PARTS[1], CH_PARTS[0]
+    first = reduced(split[:, :, :half], x_name, x_size).astype(jnp.bfloat16)
+    first, rest = lax.optimization_barrier((first, split[:, :, half:]))
+    first = reduced(first, z_name, z_size)
+    second = reduced_by_shifts(rest, x_name, x_size).astype(jnp.bfloat16)
+    second = reduced(second, z_name, z_size)
+    return jnp.concatenate([first, second], axis=0).astype(jnp.bfloat16)
 
 
 def solution(mesh):

time: 143 us -> 161 us (1.13)
  the two profiles are of different devices: /device:TPU:32 before, /device:TPU:38 now
where the time goes in v10:
time: 161 us; the launch traced here: 160 us
  blocking collectives  51 us (32%)
  waiting for transfers between devices  40.2 us (25%)
  starting transfers between devices  40 us (25%)
  local copies, waits for them, and re-layouts  14.1 us (9%)
  other arithmetic  6.12 us (4%)
  Pallas kernels  4.32 us (3%)
  matrix products  3.6 us (2%)
    all_gather x1, blocking collectives, shards(): stacked = lax.all_gather(bases_in, CH[0], axis=0)  29.4 us
    all_to_all x2, starting transfers between devices, reduced(): parts = lax.all_to_all(stack, name, 0, 0)  18.7 us
    all_to_all x2, waiting for transfers between devices, reduced(): parts = lax.all_to_all(stack, name, 0, 0)  17.4 us
    all_to_all x1, blocking collectives, reduced(): parts = lax.all_to_all(stack, name, 0, 0)  15.3 us
    ppermute x3, waiting for transfers between devices, reduced_by_shifts(): lax.ppermute(part, name, [(k, (k + shift) % count) for k in range(count)])  10.7 us
    ppermute x3, starting transfers between devices, reduced_by_shifts(): lax.ppermute(part, name, [(k, (k + shift) % count) for k in range(count)])  9.22 us
    unnamed x17, local copies, waits for them, and re-layouts  7.51 us
    all_to_all x1, blocking collectives, gathered(): return lax.all_to_all(copies, name, 0, 0)  6.26 us
  transfers between devices with their start and end apart: 9, of which 7 were waited for; matrix products, arithmetic and copies ran while one was open for 11% of the time, Pallas kernels for 3%

profile of v10, /device:TPU:38, one launch (start us, length us, event | category | flops | bytes accessed | tf_op | source)
XLA Modules:
  0.0 159.7 jit_solution(8236089718918744685)
XLA Ops:
  0.0 29.4 %all-gather = bf16[1536,128]{1,0:T(8,128)(2,1)S(1)} all-gather(bf16[384,128]{1,0:T(8,128)(2,1)} %param.7), channel_id=2, replica_groups=mesh['z_lo'=4,'y'=4,'z_hi'=4,'x'=4,'core'=2] {'z_hi'}, dimensions={0}, use_global_device_ids=true | all-gather | bytes 491520 | tf_op jit(solution)/shard_map/all_gather | solution.py:95
  29.7 1.4 broadcast_in_dim.6
  31.0 4.8 %all-to-all-start = ((bf16[4,4,384,128]{2,3,1,0:T(8,128)(2,1)}), bf16[4,4,384,128]{2,3,1,0:T(8,128)(2,1)S(1)}, u32[]{:S(2)}, u32[]{:S(2)}) async-start(bf16[4,4,384,128]{2,3,1,0:T(8,128)(2,1)} %broadcast_in_dim.6), calls=%async_computation | async-start | bytes 3145728 | tf_op jit(solution)/shard_map/all_to_all | solution.py:23
  35.8 1.6 %copy.29 = bf16[128,4096]{0,1:T(8,128)(2,1)S(1)} copy(bf16[128,4096]{1,0:T(8,128)(2,1)} %param.13) | data formatting | bytes 2097152 | tf_op args[6]
  37.6 1.9 %collective-permute-start = (bf16[4,4,128,128]{2,3,1,0:T(8,128)(2,1)S(1)}, bf16[4,4,128,128]{2,3,1,0:T(8,128)(2,1)}, u32[]{:S(2)}, u32[]{:S(2)}) collective-permute-start(bf16[4,4,128,128]{2,3,1,0:T(8,128)(2,1)S(1)} %bitcast.83), channel_id=1, source_target_pairs={{0,1},{1,0},{2,3},{3,2},{4,5},{5,4},{6,7},{7,6},{8,9},{9,8},{10,11... | collective-permute-start | bytes 1572872 | tf_op jit(solution)/shard_map/ppermute | solution.py:122
  39.5 4.7 %copy.35 = bf16[4096,3,128]{0,2,1:T(8,128)(2,1)} copy(bf16[4096,3,128]{2,0,1:T(8,128)(2,1)} %param.9) | data formatting | bytes 6291456 | tf_op args[2]
  45.0 5.6 %all-to-all-done = bf16[4,4,384,128]{2,3,1,0:T(8,128)(2,1)S(1)} async-done(((bf16[4,4,384,128]{2,3,1,0:T(8,128)(2,1)}), bf16[4,4,384,128]{2,3,1,0:T(8,128)(2,1)S(1)}, u32[]{:S(2)}, u32[]{:S(2)}) %all-to-all-start) | async-done | bytes 1572896 | tf_op jit(solution)/shard_map/all_to_all | solution.py:23
  51.3 6.3 %all_to_all.25 = bf16[2,4,4,384,128]{3,4,1,2,0:T(8,128)(2,1)S(1)} all-to-all(bf16[2,4,4,384,128]{3,4,1,2,0:T(8,128)(2,1)S(1)} %broadcast_in_dim.7), channel_id=1, replica_groups=mesh['z_lo'=4,'y'=4,'z_hi'=4,'x'=4,'core'=2] {'core'}, dimensions={0} | all-to-all | bytes 6291456 | tf_op jit(solution)/shard_map/all_to_all | solution.py:23
  57.6 0.8 fusion
  58.4 0.9 fusion.3
  59.3 1.0 copy-done
  60.3 1.8 %convolution_convert_fusion.1 = bf16[384,384]{1,0:T(8,128)(2,1)S(1)} fusion(bf16[384,4096]{0,1:T(8,128)(2,1)S(1)} %bitcast.75, bf16[4096,384]{0,1:T(8,128)(2,1)S(1)} %bitcast.74), kind=kOutput, calls=%fused_computation.8 | convolution fusion | flops 1208107008 | bytes 6586368 | tf_op jit(solution)/shard_map/dot_general | solution.py:102
  62.2 3.5 %collective-permute-start.1 = (bf16[129,384]{1,0:T(8,128)(2,1)S(1)}, bf16[129,384]{1,0:T(8,128)(2,1)S(1)}, u32[]{:S(2)}, u32[]{:S(2)}) collective-permute-start(bf16[129,384]{1,0:T(8,128)(2,1)S(1)} %slice.126), channel_id=1, source_target_pairs={{0,32},{32,64},{64,96},{96,128},{128,160},{160,192},{192,224},{224... | collective-permute-start | bytes 297224 | tf_op jit(solution)/shard_map/ppermute | solution.py:18
  66.1 5.3 %collective-permute-done.1 = bf16[129,384]{1,0:T(8,128)(2,1)S(1)} collective-permute-done((bf16[129,384]{1,0:T(8,128)(2,1)S(1)}, bf16[129,384]{1,0:T(8,128)(2,1)S(1)}, u32[]{:S(2)}, u32[]{:S(2)}) %collective-permute-start.1) | collective-permute-done | bytes 99104 | tf_op jit(solution)/shard_map/ppermute | solution.py:18
  73.6 0.8 maximum_convert_fusion.ext_ref
  74.4 4.3 %shard_map.73 = f32[384,128]{1,0:T(8,128)} custom-call(f32[512,128]{1,0:T(8,128)} %maximum_convert_fusion.ext_ref, f32[128,128]{1,0:T(8,128)} %convert_bitcast_fusion.filt_ref), custom_call_target="tpu_custom_call" | custom-call | tf_op jit(solution)/shard_map/pallas_call | solution.py:82
  78.7 1.0 fusion.17
  79.7 1.9 %collective-permute-start.2 = (bf16[384,128]{1,0:T(8,128)(2,1)S(1)}, bf16[384,128]{1,0:T(8,128)(2,1)S(1)}, u32[]{:S(2)}, u32[]{:S(2)}) collective-permute-start(bf16[384,128]{1,0:T(8,128)(2,1)S(1)} %fusion.17), channel_id=1, source_target_pairs={{0,1},{1,0},{2,3},{3,2},{4,5},{5,4},{6,7},{7,6},{8,9},{9,8},{10,11... | collective-permute-start | bytes 294920 | tf_op jit(solution)/shard_map/ppermute | solution.py:122
  81.7 1.2 collective-permute-done.2
  82.9 1.8 %fusion.4 = bf16[4,4,384,128]{2,3,1,0:T(8,128)(2,1)S(1)} fusion(bf16[4,4,128,128]{2,3,1,0:T(8,128)(2,1)} %collective-permute-done, bf16[4,4,128,128]{2,3,1,0:T(8,128)(2,1)S(1)} %bitcast.84, bf16[384,128]{1,0:T(8,128)(2,1)S(1)} %collective-permute-done.2, bf16[384,128]{1,0:T(8,128)(2,1)S(1)} %fusion.17), kind=kOutput, calls=%fused_computation.7 | convolution fusion | flops 405929984 | bytes 2818048 | tf_op jit(solution)/shard_map/tk,xzki->xzti/dot_general | solution.py:125
  85.9 15.3 %all_to_all.26 = bf16[4,4,192,128]{3,2,1,0:T(8,128)(2,1)S(1)} all-to-all(bf16[4,4,192,128]{3,2,1,0:T(8,128)(2,1)S(1)} %copy.49), channel_id=1, replica_groups=mesh['z_lo'=4,'y'=4,'z_hi'=4,'x'=4,'core'=2] {'x'}, dimensions={0} | all-to-all | bytes 1572864 | tf_op jit(solution)/shard_map/all_to_all | solution.py:27
  101.2 0.8 fusion.14
  101.9 7.0 %all-to-all-start.3 = ((bf16[4,192,128]{2,1,0:T(8,128)(2,1)}), bf16[4,192,128]{2,1,0:T(8,128)(2,1)S(1)}, u32[]{:S(2)}, u32[]{:S(2)}) async-start(bf16[4,192,128]{2,1,0:T(8,128)(2,1)} %fusion.14), calls=%async_computation.3 | async-start | bytes 393216 | tf_op jit(solution)/shard_map/all_to_all | solution.py:27
  109.0 4.0 %collective-permute-start.3 = (bf16[4,192,128]{1,2,0:T(8,128)(2,1)S(1)}, bf16[4,192,128]{1,2,0:T(8,128)(2,1)S(1)}, u32[]{:S(2)}, u32[]{:S(2)}) collective-permute-start(bf16[4,192,128]{1,2,0:T(8,128)(2,1)S(1)} %get-tuple-element.11), channel_id=1, source_target_pairs={{0,2},{2,4},{4,6},{6,0},{1,3},{3,5},{5,7},{7,1},{8,10},{10,12},{12... | collective-permute-start | bytes 589832 | tf_op jit(solution)/shard_map/ppermute | solution.py:39
  113.0 2.1 %collective-permute-start.4 = (bf16[4,192,128]{1,2,0:T(8,128)(2,1)S(1)}, bf16[4,192,128]{1,2,0:T(8,128)(2,1)S(1)}, u32[]{:S(2)}, u32[]{:S(2)}) collective-permute-start(bf16[4,192,128]{1,2,0:T(8,128)(2,1)S(1)} %get-tuple-element.13), channel_id=1, source_target_pairs={{0,4},{2,6},{4,0},{6,2},{1,5},{3,7},{5,1},{7,3},{8,12},{10,14},{12... | collective-permute-start | bytes 589832 | tf_op jit(solution)/shard_map/ppermute | solution.py:39
  115.1 3.1 %collective-permute-start.5 = (bf16[4,192,128]{1,2,0:T(8,128)(2,1)S(1)}, bf16[4,192,128]{1,2,0:T(8,128)(2,1)S(1)}, u32[]{:S(2)}, u32[]{:S(2)}) collective-permute-start(bf16[4,192,128]{1,2,0:T(8,128)(2,1)S(1)} %get-tuple-element.12), channel_id=1, source_target_pairs={{0,6},{2,0},{4,2},{6,4},{1,7},{3,1},{5,3},{7,5},{8,14},{10,8},{12,... | collective-permute-start | bytes 589832 | tf_op jit(solution)/shard_map/ppermute | solution.py:39
  118.2 5.1 %collective-permute-done.3 = bf16[4,192,128]{1,2,0:T(8,128)(2,1)S(1)} collective-permute-done((bf16[4,192,128]{1,2,0:T(8,128)(2,1)S(1)}, bf16[4,192,128]{1,2,0:T(8,128)(2,1)S(1)}, u32[]{:S(2)}, u32[]{:S(2)}) %collective-permute-start.3) | collective-permute-done | bytes 196640 | tf_op jit(solution)/shard_map/ppermute | solution.py:39
  123.4 2.3 %collective-permute-done.4 = bf16[4,192,128]{1,2,0:T(8,128)(2,1)S(1)} collective-permute-done((bf16[4,192,128]{1,2,0:T(8,128)(2,1)S(1)}, bf16[4,192,128]{1,2,0:T(8,128)(2,1)S(1)}, u32[]{:S(2)}, u32[]{:S(2)}) %collective-permute-start.4) | collective-permute-done | bytes 196640 | tf_op jit(solution)/shard_map/ppermute | solution.py:39
  125.7 3.3 %collective-permute-done.5 = bf16[4,192,128]{1,2,0:T(8,128)(2,1)S(1)} collective-permute-done((bf16[4,192,128]{1,2,0:T(8,128)(2,1)S(1)}, bf16[4,192,128]{1,2,0:T(8,128)(2,1)S(1)}, u32[]{:S(2)}, u32[]{:S(2)}) %collective-permute-start.5) | collective-permute-done | bytes 196640 | tf_op jit(solution)/shard_map/ppermute | solution.py:39
  129.1 0.8 copy.50
  129.9 11.7 %all-to-all-start.4 = ((bf16[4,192,128]{2,1,0:T(8,128)(2,1)}), bf16[4,192,128]{2,1,0:T(8,128)(2,1)S(1)}, u32[]{:S(2)}, u32[]{:S(2)}) async-start(bf16[4,192,128]{2,1,0:T(8,128)(2,1)} %copy.50), calls=%async_computation.4 | async-start | bytes 393216 | tf_op jit(solution)/shard_map/all_to_all | solution.py:27
  141.7 17.4 %all-to-all-done.4 = bf16[4,192,128]{2,1,0:T(8,128)(2,1)S(1)} async-done(((bf16[4,192,128]{2,1,0:T(8,128)(2,1)}), bf16[4,192,128]{2,1,0:T(8,128)(2,1)S(1)}, u32[]{:S(2)}, u32[]{:S(2)}) %all-to-all-start.4) | async-done | bytes 196640 | tf_op jit(solution)/shard_map/all_to_all | solution.py:27
  (51 shorter events, 6.5 us)
Async XLA Ops:
  31.0 19.6 %all-to-all-start = ((bf16[4,4,384,128]{2,3,1,0:T(8,128)(2,1)}), bf16[4,4,384,128]{2,3,1,0:T(8,128)(2,1)S(1)}, u32[]{:S(2)}, u32[]{:S(2)}) async-start(bf16[4,4,384,128]{2,3,1,0:T(8,128)(2,1)} %broadcast_in_dim.6), calls=%async_computation | async-start | bytes 3145728 | tf_op jit(solution)/shard_map/all_to_all | solution.py:23
  37.6 6.7 %copy-start.1 = (bf16[128,128]{1,0:T(8,128)(2,1)S(1)}, bf16[128,128]{1,0:T(8,128)(2,1)}, u32[]{:S(2)}) copy-start(bf16[128,128]{1,0:T(8,128)(2,1)} %param.11) | copy-start | bytes 98308
  37.6 6.8 %copy-start.3 = (f32[3,3,128]{2,1,0:T(4,128)S(1)}, f32[3,3,128]{2,1,0:T(4,128)}, u32[]{:S(2)}) copy-start(f32[3,3,128]{2,1,0:T(4,128)} %param.10) | copy-start | bytes 13828
  37.6 44.1 %collective-permute-start = (bf16[4,4,128,128]{2,3,1,0:T(8,128)(2,1)S(1)}, bf16[4,4,128,128]{2,3,1,0:T(8,128)(2,1)}, u32[]{:S(2)}, u32[]{:S(2)}) collective-permute-start(bf16[4,4,128,128]{2,3,1,0:T(8,128)(2,1)S(1)} %bitcast.83), channel_id=1, source_target_pairs={{0,1},{1,0},{2,3},{3,2},{4,5},{5,4},{6,7},{7,6},{8,9},{9,8},{10,11... | collective-permute-start | bytes 1572872 | tf_op jit(solution)/shard_map/ppermute | solution.py:122
  57.6 0.8 copy-start.2
  58.4 1.9 %copy-start = (bf16[4096,3,128]{0,2,1:T(8,128)(2,1)S(1)}, bf16[4096,3,128]{0,2,1:T(8,128)(2,1)}, u32[]{:S(2)}) copy-start(bf16[4096,3,128]{0,2,1:T(8,128)(2,1)} %copy.35) | copy-start | bytes 9437188
  62.2 9.2 %collective-permute-start.1 = (bf16[129,384]{1,0:T(8,128)(2,1)S(1)}, bf16[129,384]{1,0:T(8,128)(2,1)S(1)}, u32[]{:S(2)}, u32[]{:S(2)}) collective-permute-start(bf16[129,384]{1,0:T(8,128)(2,1)S(1)} %slice.126), channel_id=1, source_target_pairs={{0,32},{32,64},{64,96},{96,128},{128,160},{160,192},{192,224},{224... | collective-permute-start | bytes 297224 | tf_op jit(solution)/shard_map/ppermute | solution.py:18
  72.6 6.2 %copy-start.4 = (f32[128]{0:T(128)S(1)}, f32[128]{0:T(128)}, u32[]{:S(2)}) copy-start(f32[128]{0:T(128)} %param.12) | copy-start | bytes 1540
  79.7 3.2 %collective-permute-start.2 = (bf16[384,128]{1,0:T(8,128)(2,1)S(1)}, bf16[384,128]{1,0:T(8,128)(2,1)S(1)}, u32[]{:S(2)}, u32[]{:S(2)}) collective-permute-start(bf16[384,128]{1,0:T(8,128)(2,1)S(1)} %fusion.17), channel_id=1, source_target_pairs={{0,1},{1,0},{2,3},{3,2},{4,5},{5,4},{6,7},{7,6},{8,9},{9,8},{10,11... | collective-permute-start | bytes 294920 | tf_op jit(solution)/shard_map/ppermute | solution.py:122
  101.9 28.0 %all-to-all-start.3 = ((bf16[4,192,128]{2,1,0:T(8,128)(2,1)}), bf16[4,192,128]{2,1,0:T(8,128)(2,1)S(1)}, u32[]{:S(2)}, u32[]{:S(2)}) async-start(bf16[4,192,128]{2,1,0:T(8,128)(2,1)} %fusion.14), calls=%async_computation.3 | async-start | bytes 393216 | tf_op jit(solution)/shard_map/all_to_all | solution.py:27
  109.0 14.4 %collective-permute-start.3 = (bf16[4,192,128]{1,2,0:T(8,128)(2,1)S(1)}, bf16[4,192,128]{1,2,0:T(8,128)(2,1)S(1)}, u32[]{:S(2)}, u32[]{:S(2)}) collective-permute-start(bf16[4,192,128]{1,2,0:T(8,128)(2,1)S(1)} %get-tuple-element.11), channel_id=1, source_target_pairs={{0,2},{2,4},{4,6},{6,0},{1,3},{3,5},{5,7},{7,1},{8,10},{10,12},{12... | collective-permute-start | bytes 589832 | tf_op jit(solution)/shard_map/ppermute | solution.py:39
  113.0 12.7 %collective-permute-start.4 = (bf16[4,192,128]{1,2,0:T(8,128)(2,1)S(1)}, bf16[4,192,128]{1,2,0:T(8,128)(2,1)S(1)}, u32[]{:S(2)}, u32[]{:S(2)}) collective-permute-start(bf16[4,192,128]{1,2,0:T(8,128)(2,1)S(1)} %get-tuple-element.13), channel_id=1, source_target_pairs={{0,4},{2,6},{4,0},{6,2},{1,5},{3,7},{5,1},{7,3},{8,12},{10,14},{12... | collective-permute-start | bytes 589832 | tf_op jit(solution)/shard_map/ppermute | solution.py:39
  115.1 13.9 %collective-permute-start.5 = (bf16[4,192,128]{1,2,0:T(8,128)(2,1)S(1)}, bf16[4,192,128]{1,2,0:T(8,128)(2,1)S(1)}, u32[]{:S(2)}, u32[]{:S(2)}) collective-permute-start(bf16[4,192,128]{1,2,0:T(8,128)(2,1)S(1)} %get-tuple-element.12), channel_id=1, source_target_pairs={{0,6},{2,0},{4,2},{6,4},{1,7},{3,1},{5,3},{7,5},{8,14},{10,8},{12,... | collective-permute-start | bytes 589832 | tf_op jit(solution)/shard_map/ppermute | solution.py:39
  129.9 29.1 %all-to-all-start.4 = ((bf16[4,192,128]{2,1,0:T(8,128)(2,1)}), bf16[4,192,128]{2,1,0:T(8,128)(2,1)S(1)}, u32[]{:S(2)}, u32[]{:S(2)}) async-start(bf16[4,192,128]{2,1,0:T(8,128)(2,1)} %copy.50), calls=%async_computation.4 | async-start | bytes 393216 | tf_op jit(solution)/shard_map/all_to_all | solution.py:27

commit v11 on v9

--- a/solution.py
+++ b/solution.py
@@ -92,17 +92,27 @@
     mixed_in = jnp.dot(normed, w_flat, preferred_element_type=jnp.float32)
     projected = mixed_in.astype(jnp.bfloat16)
     earlier = passed_along(projected[tok - (taps - 1) - (feat_len - 1) :], CTX, CTX_COUNT, 1)
+    local_feats = featurize(projected, feat_taps, tok - (feat_len - 1))
+    local_product = (local_feats[:, 1, :] * local_feats[:, 2, :]).astype(jnp.bfloat16)
+    filt_rows = long_filter.astype(jnp.float32).T
+    half = tok // 2
+    tail = causal_filter(local_product[half - taps - (feat_len - 1) :].astype(jnp.float32), filt_rows)
+    tail, earlier = lax.optimization_barrier((tail, earlier))
     early_feats = featurize(earlier, feat_taps, taps - 1)
     before = (early_feats[:, 1, :] * early_feats[:, 2, :]).astype(jnp.bfloat16)
-    feats = featurize(
-        jnp.concatenate([earlier[earlier.shape[0] - (feat_len - 1) :], projected], axis=0), feat_taps, tok
+    head_feats = featurize(
+        jnp.concatenate([earlier[earlier.shape[0] - (feat_len - 1) :], projected[: feat_len - 1]], axis=0),
+        feat_taps,
+        feat_len - 1,
     )
-    query = feats[:, 0, :]
-    product = (feats[:, 1, :] * feats[:, 2, :]).astype(jnp.bfloat16)
-    extended = jnp.concatenate(
-        [jnp.zeros((1, chans), jnp.bfloat16), before, product], axis=0
-    ).astype(jnp.float32)
-    filtered = causal_filter(extended, long_filter.astype(jnp.float32).T)
+    query = jnp.concatenate([head_feats[:, 0, :], local_feats[:, 0, :]], axis=0)
+    head_product = (head_feats[:, 1, :] * head_feats[:, 2, :]).astype(jnp.bfloat16)
+    product = jnp.concatenate([head_product, local_product], axis=0)
+    head = causal_filter(
+        jnp.concatenate([jnp.zeros((1, chans), jnp.bfloat16), before, product[:half]], axis=0).astype(jnp.float32),
+        filt_rows,
+    )
+    filtered = jnp.concatenate([head, tail], axis=0)
     gated = (query * (filtered + skip_gain * product.astype(jnp.float32))).astype(jnp.bfloat16)
     sizes = [size for _, size in CH_PARTS]
     blocks = w_out.reshape(chans, *sizes, chans).transpose(3, 2, 1, 0, 4)
@@ -110,11 +120,11 @@
     mine = lax.dynamic_index_in_dim(blocks, core, 0, keepdims=False)
     theirs = lax.dynamic_index_in_dim(blocks, 1 - core, 0, keepdims=False)
     partner = lambda value: lax.ppermute(value, CH[2], [(0, 1), (1, 0)])
-    pair_gated = jnp.concatenate([gated, partner(gated)], axis=1)
-    pair_rows = jnp.concatenate([mine, partner(theirs)], axis=2)
-    split = jnp.einsum(
-        "tk,xzki->xzti", pair_gated, pair_rows, preferred_element_type=jnp.float32
-    ).astype(jnp.bfloat16)
+    own_part = jnp.einsum("tk,xzki->xzti", gated, mine, preferred_element_type=jnp.float32)
+    their_part = jnp.einsum(
+        "tk,xzki->xzti", partner(gated), partner(theirs), preferred_element_type=jnp.float32
+    )
+    split = (own_part + their_part).astype(jnp.bfloat16)
     for name, size in CH_PARTS[1::-1]:
         split = reduced(split, name, size).astype(jnp.bfloat16)
     return split

time: 143 us -> 143 us (level)
  waiting for transfers between devices: 14.1 us -> 9.56 us
  Pallas kernels: 4.35 us -> 5.86 us
    ppermute x1, waiting for transfers between devices: 5.33 us -> 2.15 us  [passed_along(): lax.ppermute(value, axis, [(source, source + steps) for source in range(i...]
    pallas_call x1 -> x2, Pallas kernels: 4.35 us -> 5.86 us  [causal_filter(): pl.pallas_call(filter_kernel, out_shape=jax.ShapeDtypeStruct((count, chan...]
    unnamed x17 -> x20, local copies, waits for them, and re-layouts: 7.54 us -> 8.24 us
  transfers between devices with their start and end apart: 4 -> 4, of which waited for: 3 -> 3; matrix products, arithmetic and copies ran while one was open for 11% -> 13% of each run, Pallas kernels for 3% -> 4%
where the time goes in v11:
time: 143 us; the launch traced here: 142 us
  blocking collectives  91.8 us (64%)
  local copies, waits for them, and re-layouts  13.7 us (10%)
  starting transfers between devices  11.7 us (8%)
  waiting for transfers between devices  9.56 us (7%)
  Pallas kernels  5.86 us (4%)
  other arithmetic  5.46 us (4%)
  matrix products  4.01 us (3%)
    all_to_all x2, blocking collectives, reduced(): parts = lax.all_to_all(stack, name, 0, 0)  56.1 us
    all_gather x1, blocking collectives, shards(): stacked = lax.all_gather(bases_in, CH[0], axis=0)  29.4 us
    unnamed x20, local copies, waits for them, and re-layouts  8.24 us
    all_to_all x1, waiting for transfers between devices, gathered(): return lax.all_to_all(copies, name, 0, 0)  6.73 us
    all_to_all x1, blocking collectives, gathered(): return lax.all_to_all(copies, name, 0, 0)  6.26 us
    pallas_call x2, Pallas kernels, causal_filter(): pl.pallas_call(filter_kernel, out_shape=jax.ShapeDtypeStruct((count, chan...  5.86 us
    all_to_all x1, starting transfers between devices, gathered(): return lax.all_to_all(copies, name, 0, 0)  4.29 us
    ppermute x2, starting transfers between devices, shards(): partner = lambda value: lax.ppermute(value, CH[2], [(0, 1), (1, 0)])  3.96 us
  transfers between devices with their start and end apart: 4, of which 3 were waited for; matrix products, arithmetic and copies ran while one was open for 13% of the time, Pallas kernels for 4%

profile of v11, /device:TPU:32, one launch (start us, length us, event | category | flops | bytes accessed | tf_op | source)
XLA Modules:
  0.0 142.4 jit_solution(13172464111107279734)
XLA Ops:
  0.0 29.4 %all-gather = bf16[1536,128]{1,0:T(8,128)(2,1)S(1)} all-gather(bf16[384,128]{1,0:T(8,128)(2,1)} %param.7), channel_id=2, replica_groups=mesh['z_lo'=4,'y'=4,'z_hi'=4,'x'=4,'core'=2] {'z_hi'}, dimensions={0}, use_global_device_ids=true | all-gather | bytes 491520 | tf_op jit(solution)/shard_map/all_gather | solution.py:85
  29.7 1.4 broadcast_in_dim.6
  31.0 4.3 %all-to-all-start = ((bf16[4,4,384,128]{2,3,1,0:T(8,128)(2,1)}), bf16[4,4,384,128]{2,3,1,0:T(8,128)(2,1)S(1)}, u32[]{:S(2)}, u32[]{:S(2)}) async-start(bf16[4,4,384,128]{2,3,1,0:T(8,128)(2,1)} %broadcast_in_dim.6), calls=%async_computation | async-start | bytes 3145728 | tf_op jit(solution)/shard_map/all_to_all | solution.py:23
  35.3 1.6 %copy.51 = bf16[128,4096]{0,1:T(8,128)(2,1)S(1)} copy(bf16[128,4096]{1,0:T(8,128)(2,1)} %param.13) | data formatting | bytes 2097152 | tf_op args[6]
  37.1 0.8 copy.92
  37.9 2.0 %collective-permute-start.1 = (bf16[4,4,128,128]{2,3,1,0:T(8,128)(2,1)}, bf16[4,4,128,128]{2,3,1,0:T(8,128)(2,1)}, u32[]{:S(2)}, u32[]{:S(2)}) collective-permute-start(bf16[4,4,128,128]{2,3,1,0:T(8,128)(2,1)} %bitcast.79), channel_id=1, source_target_pairs={{0,1},{1,0},{2,3},{3,2},{4,5},{5,4},{6,7},{7,6},{8,9},{9,8},{10,11... | collective-permute-start | bytes 1572872 | tf_op jit(solution)/shard_map/ppermute | solution.py:122
  40.0 4.7 %copy.56 = bf16[4096,3,128]{0,2,1:T(8,128)(2,1)} copy(bf16[4096,3,128]{2,0,1:T(8,128)(2,1)} %param.9) | data formatting | bytes 6291456 | tf_op args[2]
  44.8 0.6 convert_bitcast_fusion.filt_ref
  45.5 6.7 %all-to-all-done = bf16[4,4,384,128]{2,3,1,0:T(8,128)(2,1)S(1)} async-done(((bf16[4,4,384,128]{2,3,1,0:T(8,128)(2,1)}), bf16[4,4,384,128]{2,3,1,0:T(8,128)(2,1)S(1)}, u32[]{:S(2)}, u32[]{:S(2)}) %all-to-all-start) | async-done | bytes 1572896 | tf_op jit(solution)/shard_map/all_to_all | solution.py:23
  52.4 0.5 broadcast_in_dim.7
  52.9 6.3 %all_to_all.20 = bf16[2,4,4,384,128]{3,4,1,2,0:T(8,128)(2,1)S(1)} all-to-all(bf16[2,4,4,384,128]{3,4,1,2,0:T(8,128)(2,1)S(1)} %broadcast_in_dim.7), channel_id=1, replica_groups=mesh['z_lo'=4,'y'=4,'z_hi'=4,'x'=4,'core'=2] {'core'}, dimensions={0} | all-to-all | bytes 6291456 | tf_op jit(solution)/shard_map/all_to_all | solution.py:23
  59.1 0.8 fusion
  60.0 0.9 fusion.3
  60.9 1.0 copy-done.1
  61.8 1.8 %convolution_convert_fusion = bf16[384,384]{1,0:T(8,128)(2,1)S(1)} fusion(bf16[384,4096]{0,1:T(8,128)(2,1)S(1)} %bitcast.83, bf16[4096,384]{0,1:T(8,128)(2,1)S(1)} %bitcast.82), kind=kOutput, calls=%fused_computation.8 | convolution fusion | flops 1208107008 | bytes 6586368 | tf_op jit(solution)/shard_map/dot_general | solution.py:92
  63.9 0.2 copy.59
  64.3 0.2 copy.61
  64.8 0.2 copy.63
  65.4 3.5 %collective-permute-start = (bf16[129,384]{1,0:T(8,128)(2,1)S(1)}, bf16[129,384]{1,0:T(8,128)(2,1)S(1)}, u32[]{:S(2)}, u32[]{:S(2)}) collective-permute-start(bf16[129,384]{1,0:T(8,128)(2,1)S(1)} %slice.149), channel_id=1, source_target_pairs={{0,32},{32,64},{64,96},{96,128},{128,160},{160,192},{192,224},{224... | collective-permute-start | bytes 297224 | tf_op jit(solution)/shard_map/ppermute | solution.py:18
  68.9 0.7 fusion.12.ext_ref
  69.6 2.9 %shard_map.73 = f32[192,128]{1,0:T(8,128)} custom-call(f32[320,128]{1,0:T(8,128)} %fusion.12.ext_ref, f32[128,128]{1,0:T(8,128)} %convert_bitcast_fusion.filt_ref), custom_call_target="tpu_custom_call" | custom-call | tf_op jit(solution)/shard_map/pallas_call | solution.py:72
  72.6 2.2 %collective-permute-done = bf16[129,384]{1,0:T(8,128)(2,1)S(1)} collective-permute-done((bf16[129,384]{1,0:T(8,128)(2,1)S(1)}, bf16[129,384]{1,0:T(8,128)(2,1)S(1)}, u32[]{:S(2)}, u32[]{:S(2)}) %collective-permute-start) | collective-permute-done | bytes 99104 | tf_op jit(solution)/shard_map/ppermute | solution.py:18
  75.8 0.8 maximum_convert_fusion.ext_ref
  76.6 2.9 %shard_map.74 = f32[192,128]{1,0:T(8,128)} custom-call(f32[320,128]{1,0:T(8,128)} %maximum_convert_fusion.ext_ref, f32[128,128]{1,0:T(8,128)} %convert_bitcast_fusion.filt_ref), custom_call_target="tpu_custom_call" | custom-call | tf_op jit(solution)/shard_map/pallas_call | solution.py:72
  79.5 1.0 fusion.8
  80.5 1.9 %collective-permute-start.2 = (bf16[384,128]{1,0:T(8,128)(2,1)S(1)}, bf16[384,128]{1,0:T(8,128)(2,1)S(1)}, u32[]{:S(2)}, u32[]{:S(2)}) collective-permute-start(bf16[384,128]{1,0:T(8,128)(2,1)S(1)} %fusion.8), channel_id=1, source_target_pairs={{0,1},{1,0},{2,3},{3,2},{4,5},{5,4},{6,7},{7,6},{8,9},{9,8},{10,11... | collective-permute-start | bytes 294920 | tf_op jit(solution)/shard_map/ppermute | solution.py:122
  82.4 0.6 fusion.5
  83.0 0.7 collective-permute-done.2
  83.7 1.6 %fusion.4 = bf16[4,4,384,128]{2,3,1,0:T(8,128)(2,1)S(1)} fusion(f32[4,4,128,384]{3,2,1,0:T(8,128)S(1)} %fusion.5, bf16[4,4,128,128]{2,3,1,0:T(8,128)(2,1)} %collective-permute-done.1, bf16[384,128]{1,0:T(8,128)(2,1)S(1)} %collective-permute-done.2), kind=kOutput, calls=%fused_computation.7 | convolution fusion | flops 202899456 | bytes 5341184 | tf_op jit(solution)/shard_map/tk,xzki->xzti/dot_general | solution.py:124
  85.3 23.8 %all_to_all.21 = bf16[4,4,384,128]{2,3,1,0:T(8,128)(2,1)S(1)} all-to-all(bf16[4,4,384,128]{2,3,1,0:T(8,128)(2,1)S(1)} %fusion.4), channel_id=1, replica_groups=mesh['z_lo'=4,'y'=4,'z_hi'=4,'x'=4,'core'=2] {'x'}, dimensions={0} | all-to-all | bytes 3145728 | tf_op jit(solution)/shard_map/all_to_all | solution.py:27
  109.2 32.4 %all_to_all.22 = bf16[4,384,128]{1,2,0:T(8,128)(2,1)S(1)} all-to-all(bf16[4,384,128]{1,2,0:T(8,128)(2,1)S(1)} %fusion.6), channel_id=1, replica_groups=mesh['z_lo'=4,'y'=4,'z_hi'=4,'x'=4,'core'=2] {'z_hi'}, dimensions={0} | all-to-all | bytes 786432 | tf_op jit(solution)/shard_map/all_to_all | solution.py:27
  141.7 0.8 copy.75
  (47 shorter events, 2.9 us)
Async XLA Ops:
  31.0 21.2 %all-to-all-start = ((bf16[4,4,384,128]{2,3,1,0:T(8,128)(2,1)}), bf16[4,4,384,128]{2,3,1,0:T(8,128)(2,1)S(1)}, u32[]{:S(2)}, u32[]{:S(2)}) async-start(bf16[4,4,384,128]{2,3,1,0:T(8,128)(2,1)} %broadcast_in_dim.6), calls=%async_computation | async-start | bytes 3145728 | tf_op jit(solution)/shard_map/all_to_all | solution.py:23
  37.9 6.7 %copy-start.5 = (f32[3,3,128]{2,1,0:T(4,128)S(1)}, f32[3,3,128]{2,1,0:T(4,128)}, u32[]{:S(2)}) copy-start(f32[3,3,128]{2,1,0:T(4,128)} %param.10) | copy-start | bytes 13828
  37.9 6.8 %copy-start.3 = (bf16[128,128]{1,0:T(8,128)(2,1)S(1)}, bf16[128,128]{1,0:T(8,128)(2,1)}, u32[]{:S(2)}) copy-start(bf16[128,128]{1,0:T(8,128)(2,1)} %param.11) | copy-start | bytes 98308
  37.9 45.0 %collective-permute-start.1 = (bf16[4,4,128,128]{2,3,1,0:T(8,128)(2,1)}, bf16[4,4,128,128]{2,3,1,0:T(8,128)(2,1)}, u32[]{:S(2)}, u32[]{:S(2)}) collective-permute-start(bf16[4,4,128,128]{2,3,1,0:T(8,128)(2,1)} %bitcast.79), channel_id=1, source_target_pairs={{0,1},{1,0},{2,3},{3,2},{4,5},{5,4},{6,7},{7,6},{8,9},{9,8},{10,11... | collective-permute-start | bytes 1572872 | tf_op jit(solution)/shard_map/ppermute | solution.py:122
  59.1 0.8 copy-start.4
  60.0 1.9 %copy-start.1 = (bf16[4096,3,128]{0,2,1:T(8,128)(2,1)S(1)}, bf16[4096,3,128]{0,2,1:T(8,128)(2,1)}, u32[]{:S(2)}) copy-start(bf16[4096,3,128]{0,2,1:T(8,128)(2,1)} %copy.56) | copy-start | bytes 9437188
  63.7 5.9 %copy-start = (bf16[384,384]{1,0:T(8,128)(2,1)}, bf16[384,384]{1,0:T(8,128)(2,1)S(1)}, u32[]{:S(2)}) copy-start(bf16[384,384]{1,0:T(8,128)(2,1)S(1)} %convolution_convert_fusion) | copy-start | bytes 884740
  65.4 14.1 %copy-start.6 = (f32[128]{0:T(128)S(1)}, f32[128]{0:T(128)}, u32[]{:S(2)}) copy-start(f32[128]{0:T(128)} %param.12) | copy-start | bytes 1540
  65.4 9.3 %collective-permute-start = (bf16[129,384]{1,0:T(8,128)(2,1)S(1)}, bf16[129,384]{1,0:T(8,128)(2,1)S(1)}, u32[]{:S(2)}, u32[]{:S(2)}) collective-permute-start(bf16[129,384]{1,0:T(8,128)(2,1)S(1)} %slice.149), channel_id=1, source_target_pairs={{0,32},{32,64},{64,96},{96,128},{128,160},{160,192},{192,224},{224... | collective-permute-start | bytes 297224 | tf_op jit(solution)/shard_map/ppermute | solution.py:18
  69.6 6.1 %slice-start = ((bf16[384,384]{1,0:T(8,128)(2,1)}), bf16[2,384]{1,0:T(2,128)(2,1)S(1)}, s32[]{:S(2)}) async-start(bf16[384,384]{1,0:T(8,128)(2,1)} %copy-done), calls=%async_computation.4 | async-start | bytes 3072 | tf_op jit(solution)/shard_map/slice | solution.py:104
  72.6 6.9 %copy-start.2 = (f32[192,128]{1,0:T(8,128)S(1)}, f32[192,128]{1,0:T(8,128)}, u32[]{:S(2)}) copy-start(f32[192,128]{1,0:T(8,128)} %shard_map.73) | copy-start | bytes 294916
  80.5 3.2 %collective-permute-start.2 = (bf16[384,128]{1,0:T(8,128)(2,1)S(1)}, bf16[384,128]{1,0:T(8,128)(2,1)S(1)}, u32[]{:S(2)}, u32[]{:S(2)}) collective-permute-start(bf16[384,128]{1,0:T(8,128)(2,1)S(1)} %fusion.8), channel_id=1, source_target_pairs={{0,1},{1,0},{2,3},{3,2},{4,5},{5,4},{6,7},{7,6},{8,9},{9,8},{10,11... | collective-permute-start | bytes 294920 | tf_op jit(solution)/shard_map/ppermute | solution.py:122

commit v12 on v11

--- a/solution.py
+++ b/solution.py
@@ -43,12 +43,13 @@
     return feats
 
 
-def filter_kernel(ext_ref, filt_ref, out_ref, shift_ref):
+def filter_kernel(ext_ref, filt_ref, query_ref, skip_ref, out_ref, wide_ref, shift_ref):
     taps = filt_ref.shape[0]
     rows = shift_ref.shape[1]
     count = out_ref.shape[0]
+    wide_ref[...] = ext_ref[...].astype(jnp.float32)
     for b in range(8):
-        shift_ref[b] = ext_ref[pl.ds(8 - b, rows), :]
+        shift_ref[b] = wide_ref[pl.ds(8 - b, rows), :]
 
     def tile(index, carry):
         base = pl.multiple_of(index * FILTER_ROWS, 8)
@@ -59,21 +60,26 @@
                 acc = acc + filt_ref[pl.ds(tap, 1), :] * shift_ref[
                     b, pl.ds(base + taps - 8 - 8 * group, FILTER_ROWS), :
                 ]
-        out_ref[pl.ds(base, FILTER_ROWS), :] = acc
+        own = wide_ref[pl.ds(base + taps, FILTER_ROWS), :]
+        query = query_ref[pl.ds(base, FILTER_ROWS), :]
+        out_ref[pl.ds(base, FILTER_ROWS), :] = (query * (acc + skip_ref[...] * own)).astype(out_ref.dtype)
         return carry
 
     lax.fori_loop(0, count // FILTER_ROWS, tile, 0)
 
 
-def causal_filter(extended, filt_rows):
+def gated_filter(extended, filt_rows, query, skip):
     taps, chans = filt_rows.shape
     count = extended.shape[0] - taps
     rows = extended.shape[0] - 8
     return pl.pallas_call(
         filter_kernel,
-        out_shape=jax.ShapeDtypeStruct((count, chans), jnp.float32),
-        scratch_shapes=[pltpu.VMEM((8, rows, chans), jnp.float32)],
-    )(extended, filt_rows)
+        out_shape=jax.ShapeDtypeStruct((count, chans), jnp.bfloat16),
+        scratch_shapes=[
+            pltpu.VMEM((extended.shape[0], chans), jnp.float32),
+            pltpu.VMEM((8, rows, chans), jnp.float32),
+        ],
+    )(extended, filt_rows, query, skip.reshape(1, chans))
 
 
 def shards(bases_in, norm_gain, w_in, feat_taps, long_filter, skip_gain, w_out):
@@ -96,7 +102,10 @@
     local_product = (local_feats[:, 1, :] * local_feats[:, 2, :]).astype(jnp.bfloat16)
     filt_rows = long_filter.astype(jnp.float32).T
     half = tok // 2
-    tail = causal_filter(local_product[half - taps - (feat_len - 1) :].astype(jnp.float32), filt_rows)
+    local_query = local_feats[:, 0, :]
+    tail = gated_filter(
+        local_product[half - taps - (feat_len - 1) :], filt_rows, local_query[half - (feat_len - 1) :], skip_gain
+    )
     tail, earlier = lax.optimization_barrier((tail, earlier))
     early_feats = featurize(earlier, feat_taps, taps - 1)
     before = (early_feats[:, 1, :] * early_feats[:, 2, :]).astype(jnp.bfloat16)
@@ -105,15 +114,16 @@
         feat_taps,
         feat_len - 1,
     )
-    query = jnp.concatenate([head_feats[:, 0, :], local_feats[:, 0, :]], axis=0)
+    query = jnp.concatenate([head_feats[:, 0, :], local_query], axis=0)
     head_product = (head_feats[:, 1, :] * head_feats[:, 2, :]).astype(jnp.bfloat16)
     product = jnp.concatenate([head_product, local_product], axis=0)
-    head = causal_filter(
-        jnp.concatenate([jnp.zeros((1, chans), jnp.bfloat16), before, product[:half]], axis=0).astype(jnp.float32),
+    head = gated_filter(
+        jnp.concatenate([jnp.zeros((1, chans), jnp.bfloat16), before, product[:half]], axis=0),
         filt_rows,
+        query[:half],
+        skip_gain,
     )
-    filtered = jnp.concatenate([head, tail], axis=0)
-    gated = (query * (filtered + skip_gain * product.astype(jnp.float32))).astype(jnp.bfloat16)
+    gated = jnp.concatenate([head, tail], axis=0)
     sizes = [size for _, size in CH_PARTS]
     blocks = w_out.reshape(chans, *sizes, chans).transpose(3, 2, 1, 0, 4)
     core = lax.axis_index(CH[2])

time: 143 us -> 144 us (level)
    convert_element_type x5 -> x0, other arithmetic: 2.47 us -> none  [the longest x1 0.96 us: shards(): (query * (filtered + skip_gain * product.astype(jnp.float32))).astype(jnp...]
    concatenate x1 -> x3, other arithmetic: 0.02 us -> 2.19 us  [the longest x1 0.81 us: shards(): gated = jnp.concatenate([head, tail], axis=0)]
    unnamed x20 -> x16, local copies, waits for them, and re-layouts: 8.24 us -> 8.22 us
  transfers between devices with their start and end apart: 4 -> 4, of which waited for: 3 -> 2; matrix products, arithmetic and copies ran while one was open for 13% -> 14% of each run, Pallas kernels for 4% -> 4%
where the time goes in v12:
time: 144 us
  blocking collectives  92.1 us (64%)
  local copies, waits for them, and re-layouts  14.9 us (10%)
  starting transfers between devices  11.7 us (8%)
  waiting for transfers between devices  9.17 us (6%)
  Pallas kernels  5.45 us (4%)
  other arithmetic  5.18 us (4%)
  matrix products  4.81 us (3%)
    all_to_all x2, blocking collectives, reduced(): parts = lax.all_to_all(stack, name, 0, 0)  56.5 us
    all_gather x1, blocking collectives, shards(): stacked = lax.all_gather(bases_in, CH[0], axis=0)  29.4 us
    unnamed x16, local copies, waits for them, and re-layouts  8.22 us
    all_to_all x1, waiting for transfers between devices, gathered(): return lax.all_to_all(copies, name, 0, 0)  6.76 us
    all_to_all x1, blocking collectives, gathered(): return lax.all_to_all(copies, name, 0, 0)  6.26 us
    pallas_call x2, Pallas kernels, gated_filter(): pl.pallas_call(filter_kernel, out_shape=jax.ShapeDtypeStruct((count, chan...  5.45 us
    all_to_all x1, starting transfers between devices, gathered(): return lax.all_to_all(copies, name, 0, 0)  4.29 us
    ppermute x2, starting transfers between devices, shards(): partner = lambda value: lax.ppermute(value, CH[2], [(0, 1), (1, 0)])  3.95 us
  transfers between devices with their start and end apart: 4, of which 2 were waited for; matrix products, arithmetic and copies ran while one was open for 14% of the time, Pallas kernels for 4%

profile of v12, /device:TPU:32, one launch (start us, length us, event | category | flops | bytes accessed | tf_op | source)
XLA Modules:
  0.0 143.6 jit_solution(1191183427502515056)
XLA Ops:
  0.0 29.4 %all-gather = bf16[1536,128]{1,0:T(8,128)(2,1)S(1)} all-gather(bf16[384,128]{1,0:T(8,128)(2,1)} %param.7), channel_id=2, replica_groups=mesh['z_lo'=4,'y'=4,'z_hi'=4,'x'=4,'core'=2] {'z_hi'}, dimensions={0}, use_global_device_ids=true | all-gather | bytes 491520 | tf_op jit(solution)/shard_map/all_gather | solution.py:91
  29.7 1.4 broadcast_in_dim.7
  31.0 4.3 %all-to-all-start = ((bf16[4,4,384,128]{2,3,1,0:T(8,128)(2,1)}), bf16[4,4,384,128]{2,3,1,0:T(8,128)(2,1)S(1)}, u32[]{:S(2)}, u32[]{:S(2)}) async-start(bf16[4,4,384,128]{2,3,1,0:T(8,128)(2,1)} %broadcast_in_dim.7), calls=%async_computation | async-start | bytes 3145728 | tf_op jit(solution)/shard_map/all_to_all | solution.py:23
  35.3 1.6 %copy.51 = bf16[128,4096]{0,1:T(8,128)(2,1)S(1)} copy(bf16[128,4096]{1,0:T(8,128)(2,1)} %param.13) | data formatting | bytes 2097152 | tf_op args[6]
  37.0 0.8 copy.92
  37.9 2.0 %collective-permute-start.1 = (bf16[4,4,128,128]{2,3,1,0:T(8,128)(2,1)}, bf16[4,4,128,128]{2,3,1,0:T(8,128)(2,1)}, u32[]{:S(2)}, u32[]{:S(2)}) collective-permute-start(bf16[4,4,128,128]{2,3,1,0:T(8,128)(2,1)} %bitcast.79), channel_id=1, source_target_pairs={{0,1},{1,0},{2,3},{3,2},{4,5},{5,4},{6,7},{7,6},{8,9},{9,8},{10,11... | collective-permute-start | bytes 1572872 | tf_op jit(solution)/shard_map/ppermute | solution.py:132
  39.9 4.7 %copy.56 = bf16[4096,3,128]{0,2,1:T(8,128)(2,1)} copy(bf16[4096,3,128]{2,0,1:T(8,128)(2,1)} %param.9) | data formatting | bytes 6291456 | tf_op args[2]
  44.8 0.6 convert_bitcast_fusion.filt_ref
  45.4 6.8 %all-to-all-done = bf16[4,4,384,128]{2,3,1,0:T(8,128)(2,1)S(1)} async-done(((bf16[4,4,384,128]{2,3,1,0:T(8,128)(2,1)}), bf16[4,4,384,128]{2,3,1,0:T(8,128)(2,1)S(1)}, u32[]{:S(2)}, u32[]{:S(2)}) %all-to-all-start) | async-done | bytes 1572896 | tf_op jit(solution)/shard_map/all_to_all | solution.py:23
  52.4 0.5 broadcast_in_dim.8
  52.9 6.3 %all_to_all.20 = bf16[2,4,4,384,128]{3,4,1,2,0:T(8,128)(2,1)S(1)} all-to-all(bf16[2,4,4,384,128]{3,4,1,2,0:T(8,128)(2,1)S(1)} %broadcast_in_dim.8), channel_id=1, replica_groups=mesh['z_lo'=4,'y'=4,'z_hi'=4,'x'=4,'core'=2] {'core'}, dimensions={0} | all-to-all | bytes 6291456 | tf_op jit(solution)/shard_map/all_to_all | solution.py:23
  59.1 0.8 fusion
  60.0 0.9 fusion.3
  60.9 1.0 copy-done
  61.8 1.8 %convolution_convert_fusion = bf16[384,384]{1,0:T(8,128)(2,1)S(1)} fusion(bf16[384,4096]{0,1:T(8,128)(2,1)S(1)} %bitcast.83, bf16[4096,384]{0,1:T(8,128)(2,1)S(1)} %bitcast.82), kind=kOutput, calls=%fused_computation.8 | convolution fusion | flops 1208107008 | bytes 6586368 | tf_op jit(solution)/shard_map/dot_general | solution.py:98
  64.3 0.2 copy.60
  64.7 0.2 copy.62
  65.4 0.6 slice_bitcast_fusion.1.query_ref
  66.0 3.5 %collective-permute-start = (bf16[129,384]{1,0:T(8,128)(2,1)S(1)}, bf16[129,384]{1,0:T(8,128)(2,1)S(1)}, u32[]{:S(2)}, u32[]{:S(2)}) collective-permute-start(bf16[129,384]{1,0:T(8,128)(2,1)S(1)} %slice.165), channel_id=1, source_target_pairs={{0,32},{32,64},{64,96},{96,128},{128,160},{160,192},{192,224},{224... | collective-permute-start | bytes 297224 | tf_op jit(solution)/shard_map/ppermute | solution.py:18
  69.5 0.6 slice_bitcast_fusion.2.ext_ref
  70.2 2.7 %shard_map.73 = bf16[192,128]{1,0:T(8,128)(2,1)} custom-call(bf16[320,128]{1,0:T(8,128)(2,1)} %slice_bitcast_fusion.2.ext_ref, f32[128,128]{1,0:T(8,128)} %convert_bitcast_fusion.filt_ref, f32[192,128]{1,0:T(8,128)} %slice_bitcast_fusion.1.query_ref, f32[1,128]{1,0:T(1,128)} %bitcast.96), custom_call_target="tpu_custom_call" | custom-call | tf_op jit(solution)/shard_map/pallas_call | solution.py:75
  72.9 2.4 %collective-permute-done = bf16[129,384]{1,0:T(8,128)(2,1)S(1)} collective-permute-done((bf16[129,384]{1,0:T(8,128)(2,1)S(1)}, bf16[129,384]{1,0:T(8,128)(2,1)S(1)}, u32[]{:S(2)}, u32[]{:S(2)}) %collective-permute-start) | collective-permute-done | bytes 99104 | tf_op jit(solution)/shard_map/ppermute | solution.py:18
  76.3 0.7 fusion.11.ext_ref
  77.1 0.6 pad_maximum_fusion.query_ref
  77.7 2.7 %shard_map.74 = bf16[192,128]{1,0:T(8,128)(2,1)} custom-call(bf16[320,128]{1,0:T(8,128)(2,1)} %fusion.11.ext_ref, f32[128,128]{1,0:T(8,128)} %convert_bitcast_fusion.filt_ref, f32[192,128]{1,0:T(8,128)} %pad_maximum_fusion.query_ref, f32[1,128]{1,0:T(1,128)} %bitcast.97), custom_call_target="tpu_custom_call" | custom-call | tf_op jit(solution)/shard_map/pallas_call | solution.py:75
  80.4 0.8 pad_maximum_fusion.1
  81.3 1.9 %collective-permute-start.2 = (bf16[384,128]{1,0:T(8,128)(2,1)S(1)}, bf16[384,128]{1,0:T(8,128)(2,1)S(1)}, u32[]{:S(2)}, u32[]{:S(2)}) collective-permute-start(bf16[384,128]{1,0:T(8,128)(2,1)S(1)} %pad_maximum_fusion.1), channel_id=1, source_target_pairs={{0,1},{1,0},{2,3},{3,2},{4,5},{5,4},{6,7},{7,6},{8,9},{9,8},{10,11... | collective-permute-start | bytes 294920 | tf_op jit(solution)/shard_map/ppermute | solution.py:132
  83.2 1.4 fusion.5
  84.6 1.6 %fusion.4 = bf16[4,4,384,128]{2,3,1,0:T(8,128)(2,1)S(1)} fusion(f32[4,4,128,384]{3,2,1,0:T(8,128)S(1)} %fusion.5, bf16[4,4,128,128]{2,3,1,0:T(8,128)(2,1)} %collective-permute-done.1, bf16[384,128]{1,0:T(8,128)(2,1)S(1)} %collective-permute-done.2), kind=kOutput, calls=%fused_computation.7 | convolution fusion | flops 202899456 | bytes 5341184 | tf_op jit(solution)/shard_map/tk,xzki->xzti/dot_general | solution.py:134
  86.2 24.1 %all_to_all.21 = bf16[4,4,384,128]{2,3,1,0:T(8,128)(2,1)S(1)} all-to-all(bf16[4,4,384,128]{2,3,1,0:T(8,128)(2,1)S(1)} %fusion.4), channel_id=1, replica_groups=mesh['z_lo'=4,'y'=4,'z_hi'=4,'x'=4,'core'=2] {'x'}, dimensions={0} | all-to-all | bytes 3145728 | tf_op jit(solution)/shard_map/all_to_all | solution.py:27
  110.5 32.4 %all_to_all.22 = bf16[4,384,128]{1,2,0:T(8,128)(2,1)S(1)} all-to-all(bf16[4,384,128]{1,2,0:T(8,128)(2,1)S(1)} %fusion.6), channel_id=1, replica_groups=mesh['z_lo'=4,'y'=4,'z_hi'=4,'x'=4,'core'=2] {'z_hi'}, dimensions={0} | all-to-all | bytes 786432 | tf_op jit(solution)/shard_map/all_to_all | solution.py:27
  142.9 0.8 copy.75
  (43 shorter events, 3.1 us)
Async XLA Ops:
  31.0 21.2 %all-to-all-start = ((bf16[4,4,384,128]{2,3,1,0:T(8,128)(2,1)}), bf16[4,4,384,128]{2,3,1,0:T(8,128)(2,1)S(1)}, u32[]{:S(2)}, u32[]{:S(2)}) async-start(bf16[4,4,384,128]{2,3,1,0:T(8,128)(2,1)} %broadcast_in_dim.7), calls=%async_computation | async-start | bytes 3145728 | tf_op jit(solution)/shard_map/all_to_all | solution.py:23
  37.9 6.7 %copy-start.4 = (f32[3,3,128]{2,1,0:T(4,128)S(1)}, f32[3,3,128]{2,1,0:T(4,128)}, u32[]{:S(2)}) copy-start(f32[3,3,128]{2,1,0:T(4,128)} %param.10) | copy-start | bytes 13828
  37.9 6.8 %copy-start.2 = (bf16[128,128]{1,0:T(8,128)(2,1)S(1)}, bf16[128,128]{1,0:T(8,128)(2,1)}, u32[]{:S(2)}) copy-start(bf16[128,128]{1,0:T(8,128)(2,1)} %param.11) | copy-start | bytes 98308
  37.9 46.7 %collective-permute-start.1 = (bf16[4,4,128,128]{2,3,1,0:T(8,128)(2,1)}, bf16[4,4,128,128]{2,3,1,0:T(8,128)(2,1)}, u32[]{:S(2)}, u32[]{:S(2)}) collective-permute-start(bf16[4,4,128,128]{2,3,1,0:T(8,128)(2,1)} %bitcast.79), channel_id=1, source_target_pairs={{0,1},{1,0},{2,3},{3,2},{4,5},{5,4},{6,7},{7,6},{8,9},{9,8},{10,11... | collective-permute-start | bytes 1572872 | tf_op jit(solution)/shard_map/ppermute | solution.py:132
  59.1 0.8 copy-start.3
  59.9 1.9 %copy-start = (bf16[4096,3,128]{0,2,1:T(8,128)(2,1)S(1)}, bf16[4096,3,128]{0,2,1:T(8,128)(2,1)}, u32[]{:S(2)}) copy-start(bf16[4096,3,128]{0,2,1:T(8,128)(2,1)} %copy.56) | copy-start | bytes 9437188
  66.0 9.3 %collective-permute-start = (bf16[129,384]{1,0:T(8,128)(2,1)S(1)}, bf16[129,384]{1,0:T(8,128)(2,1)S(1)}, u32[]{:S(2)}, u32[]{:S(2)}) collective-permute-start(bf16[129,384]{1,0:T(8,128)(2,1)S(1)} %slice.165), channel_id=1, source_target_pairs={{0,32},{32,64},{64,96},{96,128},{128,160},{160,192},{192,224},{224... | collective-permute-start | bytes 297224 | tf_op jit(solution)/shard_map/ppermute | solution.py:18
  72.9 7.5 %copy-start.1 = (bf16[192,128]{1,0:T(8,128)(2,1)S(1)}, bf16[192,128]{1,0:T(8,128)(2,1)}, u32[]{:S(2)}) copy-start(bf16[192,128]{1,0:T(8,128)(2,1)} %shard_map.73) | copy-start | bytes 147460
  81.3 3.3 %collective-permute-start.2 = (bf16[384,128]{1,0:T(8,128)(2,1)S(1)}, bf16[384,128]{1,0:T(8,128)(2,1)S(1)}, u32[]{:S(2)}, u32[]{:S(2)}) collective-permute-start(bf16[384,128]{1,0:T(8,128)(2,1)S(1)} %pad_maximum_fusion.1), channel_id=1, source_target_pairs={{0,1},{1,0},{2,3},{3,2},{4,5},{5,4},{6,7},{7,6},{8,9},{9,8},{10,11... | collective-permute-start | bytes 294920 | tf_op jit(solution)/shard_map/ppermute | solution.py:132

commit v13 on v11

--- a/solution.py
+++ b/solution.py
@@ -19,6 +19,10 @@
 
 
 def gathered(block, name, count):
+    if count == 2:
+        index = lax.axis_index(name)
+        other = lax.ppermute(block, name, [(0, 1), (1, 0)])
+        return jnp.where(index == 0, jnp.stack([block, other]), jnp.stack([other, block]))
     copies = jnp.broadcast_to(block[None], (count,) + block.shape)
     return lax.all_to_all(copies, name, 0, 0)
 

time: 143 us -> 150 us (1.049)
  blocking collectives: 91.8 us -> 107 us
  waiting for transfers between devices: 9.56 us -> 2.71 us
  starting transfers between devices: 11.7 us -> 9.85 us
    all_to_all x1, blocking collectives: 6.26 us -> 21 us  [gathered(): return lax.all_to_all(copies, name, 0, 0)]
    all_to_all x1 -> x0, waiting for transfers between devices: 6.73 us -> none  [gathered(): return lax.all_to_all(copies, name, 0, 0)]
    all_to_all x1 -> x0, starting transfers between devices: 4.29 us -> none  [gathered(): return lax.all_to_all(copies, name, 0, 0)]
    another operation x1, local copies, waits for them, and re-layouts: 0.11 us -> 2.09 us
    ppermute x0 -> x1, starting transfers between devices: none -> 1.92 us  [gathered(): other = lax.ppermute(block, name, [(0, 1), (1, 0)])]
    broadcast_in_dim x2 -> x1, local copies, waits for them, and re-layouts: 1.86 us -> 0.2 us  [gathered(): copies = jnp.broadcast_to(block[None], (count,) + block.shape)]
    unnamed x20 -> x22, local copies, waits for them, and re-layouts: 8.24 us -> 8.33 us
  transfers between devices with their start and end apart: 4 -> 4, of which waited for: 3 -> 2; matrix products, arithmetic and copies ran while one was open for 13% -> 14% of each run, Pallas kernels for 4% -> 4%
where the time goes in v13:
time: 150 us
  blocking collectives  107 us (71%)
  local copies, waits for them, and re-layouts  14.1 us (9%)
  starting transfers between devices  9.85 us (7%)
  other arithmetic  6.31 us (4%)
  Pallas kernels  5.86 us (4%)
  matrix products  4 us (3%)
  waiting for transfers between devices  2.71 us (2%)
    all_to_all x2, blocking collectives, reduced(): parts = lax.all_to_all(stack, name, 0, 0)  56.3 us
    all_gather x1, blocking collectives, shards(): stacked = lax.all_gather(bases_in, CH[0], axis=0)  29.4 us
    all_to_all x1, blocking collectives, gathered(): return lax.all_to_all(copies, name, 0, 0)  21 us
    unnamed x22, local copies, waits for them, and re-layouts  8.33 us
    pallas_call x2, Pallas kernels, causal_filter(): pl.pallas_call(filter_kernel, out_shape=jax.ShapeDtypeStruct((count, chan...  5.86 us
    ppermute x2, starting transfers between devices, shards(): partner = lambda value: lax.ppermute(value, CH[2], [(0, 1), (1, 0)])  4.32 us
    ppermute x1, starting transfers between devices, passed_along(): lax.ppermute(value, axis, [(source, source + steps) for source in range(i...  3.61 us
  transfers between devices with their start and end apart: 4, of which 2 were waited for; matrix products, arithmetic and copies ran while one was open for 14% of the time, Pallas kernels for 4%

profile of v13, /device:TPU:32, one launch (start us, length us, event | category | flops | bytes accessed | tf_op | source)
XLA Modules:
  0.0 149.8 jit_solution(2790794181870063097)
XLA Ops:
  0.0 29.4 %all-gather = bf16[1536,128]{1,0:T(8,128)(2,1)S(1)} all-gather(bf16[384,128]{1,0:T(8,128)(2,1)} %param.7), channel_id=2, replica_groups=mesh['z_lo'=4,'y'=4,'z_hi'=4,'x'=4,'core'=2] {'z_hi'}, dimensions={0}, use_global_device_ids=true | all-gather | bytes 491520 | tf_op jit(solution)/shard_map/all_gather | solution.py:89
  29.9 21.0 %all_to_all.15 = bf16[4,4,384,128]{2,3,1,0:T(8,128)(2,1)S(1)} all-to-all(bf16[4,4,384,128]{2,3,1,0:T(8,128)(2,1)S(1)} %broadcast_in_dim.4), channel_id=1, replica_groups=mesh['z_lo'=4,'y'=4,'z_hi'=4,'x'=4,'core'=2] {'x'}, dimensions={0} | all-to-all | bytes 3145728 | tf_op jit(solution)/shard_map/all_to_all | solution.py:27
  51.0 1.9 %collective-permute-start = (bf16[4,4,384,128]{2,3,0,1:T(8,128)(2,1)S(1)}, bf16[4,4,384,128]{2,3,0,1:T(8,128)(2,1)S(1)}, u32[]{:S(2)}, u32[]{:S(2)}) collective-permute-start(bf16[4,4,384,128]{2,3,0,1:T(8,128)(2,1)S(1)} %copy.94), channel_id=1, source_target_pairs={{0,1},{1,0},{2,3},{3,2},{4,5},{5,4},{6,7},{7,6},{8,9},{9,8},{10,11... | collective-permute-start | bytes 4718600 | tf_op jit(solution)/shard_map/ppermute | solution.py:24
  52.9 2.3 %copy.51 = bf16[128,4096]{0,1:T(8,128)(2,1)} copy(bf16[128,4096]{1,0:T(8,128)(2,1)} %param.13) | data formatting | bytes 2097152 | tf_op args[6]
  55.2 2.1 %constant_dynamic-slice_fusion = (bf16[128,4,4,1,128]{0,4,3,2,1:T(8,128)(2,1)S(1)}, bf16[128,4,4,1,128]{0,4,3,2,1:T(8,128)(2,1)}) fusion(bf16[128,4,4,2,128]{0,4,3,2,1:T(8,128)(2,1)} %bitcast.88, s32[]{:T(128)S(6)} %select_n.18, s32[]{:T(128)S(6)} %select_n.15), kind=kLoop, calls=%fused_computation.58 | loop fusion | bytes 2097160 | tf_op jit(solution)/shard_map/dynamic-slice.1
  57.3 0.8 copy.92
  58.1 2.4 %collective-permute-start.2 = (bf16[4,4,128,128]{2,3,1,0:T(8,128)(2,1)}, bf16[4,4,128,128]{2,3,1,0:T(8,128)(2,1)}, u32[]{:S(2)}, u32[]{:S(2)}) collective-permute-start(bf16[4,4,128,128]{2,3,1,0:T(8,128)(2,1)} %bitcast.82), channel_id=1, source_target_pairs={{0,1},{1,0},{2,3},{3,2},{4,5},{5,4},{6,7},{7,6},{8,9},{9,8},{10,11... | collective-permute-start | bytes 1572872 | tf_op jit(solution)/shard_map/ppermute | solution.py:126
  60.6 4.7 %copy.56 = bf16[4096,3,128]{0,2,1:T(8,128)(2,1)} copy(bf16[4096,3,128]{2,0,1:T(8,128)(2,1)} %param.9) | data formatting | bytes 6291456 | tf_op args[2]
  65.4 0.6 convert_bitcast_fusion.filt_ref
  66.1 1.1 fusion
  67.2 1.5 fusion.3
  68.7 0.4 copy-done.1
  69.1 1.8 %convolution_convert_fusion = bf16[384,384]{1,0:T(8,128)(2,1)S(1)} fusion(bf16[384,4096]{0,1:T(8,128)(2,1)S(1)} %bitcast.90, bf16[4096,384]{0,1:T(8,128)(2,1)S(1)} %bitcast.89), kind=kOutput, calls=%fused_computation.9 | convolution fusion | flops 1208107008 | bytes 6586368 | tf_op jit(solution)/shard_map/dot_general | solution.py:96
  71.1 0.2 copy.59
  71.3 0.2 copy.60
  71.6 0.2 copy.61
  71.8 0.2 copy.62
  72.0 0.2 copy.63
  72.7 3.6 %collective-permute-start.1 = (bf16[129,384]{1,0:T(8,128)(2,1)S(1)}, bf16[129,384]{1,0:T(8,128)(2,1)S(1)}, u32[]{:S(2)}, u32[]{:S(2)}) collective-permute-start(bf16[129,384]{1,0:T(8,128)(2,1)S(1)} %slice.149), channel_id=1, source_target_pairs={{0,32},{32,64},{64,96},{96,128},{128,160},{160,192},{192,224},{224... | collective-permute-start | bytes 297224 | tf_op jit(solution)/shard_map/ppermute | solution.py:18
  76.3 0.7 fusion.12.ext_ref
  77.0 2.9 %shard_map.73 = f32[192,128]{1,0:T(8,128)} custom-call(f32[320,128]{1,0:T(8,128)} %fusion.12.ext_ref, f32[128,128]{1,0:T(8,128)} %convert_bitcast_fusion.filt_ref), custom_call_target="tpu_custom_call" | custom-call | tf_op jit(solution)/shard_map/pallas_call | solution.py:76
  79.9 2.0 %collective-permute-done.1 = bf16[129,384]{1,0:T(8,128)(2,1)S(1)} collective-permute-done((bf16[129,384]{1,0:T(8,128)(2,1)S(1)}, bf16[129,384]{1,0:T(8,128)(2,1)S(1)}, u32[]{:S(2)}, u32[]{:S(2)}) %collective-permute-start.1) | collective-permute-done | bytes 99104 | tf_op jit(solution)/shard_map/ppermute | solution.py:18
  83.0 0.8 maximum_convert_fusion.ext_ref
  83.8 2.9 %shard_map.74 = f32[192,128]{1,0:T(8,128)} custom-call(f32[320,128]{1,0:T(8,128)} %maximum_convert_fusion.ext_ref, f32[128,128]{1,0:T(8,128)} %convert_bitcast_fusion.filt_ref), custom_call_target="tpu_custom_call" | custom-call | tf_op jit(solution)/shard_map/pallas_call | solution.py:76
  86.7 1.0 fusion.8
  87.7 1.9 %collective-permute-start.3 = (bf16[384,128]{1,0:T(8,128)(2,1)S(1)}, bf16[384,128]{1,0:T(8,128)(2,1)S(1)}, u32[]{:S(2)}, u32[]{:S(2)}) collective-permute-start(bf16[384,128]{1,0:T(8,128)(2,1)S(1)} %fusion.8), channel_id=1, source_target_pairs={{0,1},{1,0},{2,3},{3,2},{4,5},{5,4},{6,7},{7,6},{8,9},{9,8},{10,11... | collective-permute-start | bytes 294920 | tf_op jit(solution)/shard_map/ppermute | solution.py:126
  89.6 0.6 fusion.5
  90.2 0.7 collective-permute-done.3
  90.9 1.6 %fusion.4 = bf16[4,4,384,128]{2,3,1,0:T(8,128)(2,1)S(1)} fusion(f32[4,4,128,384]{3,2,1,0:T(8,128)S(1)} %fusion.5, bf16[4,4,128,128]{2,3,1,0:T(8,128)(2,1)} %collective-permute-done.2, bf16[384,128]{1,0:T(8,128)(2,1)S(1)} %collective-permute-done.3), kind=kOutput, calls=%fused_computation.8 | convolution fusion | flops 202899456 | bytes 5341184 | tf_op jit(solution)/shard_map/tk,xzki->xzti/dot_general | solution.py:128
  92.5 23.8 %all_to_all.16 = bf16[4,4,384,128]{2,3,1,0:T(8,128)(2,1)S(1)} all-to-all(bf16[4,4,384,128]{2,3,1,0:T(8,128)(2,1)S(1)} %fusion.4), channel_id=1, replica_groups=mesh['z_lo'=4,'y'=4,'z_hi'=4,'x'=4,'core'=2] {'x'}, dimensions={0} | all-to-all | bytes 3145728 | tf_op jit(solution)/shard_map/all_to_all | solution.py:31
  116.5 32.5 %all_to_all.17 = bf16[4,384,128]{1,2,0:T(8,128)(2,1)S(1)} all-to-all(bf16[4,384,128]{1,2,0:T(8,128)(2,1)S(1)} %fusion.6), channel_id=1, replica_groups=mesh['z_lo'=4,'y'=4,'z_hi'=4,'x'=4,'core'=2] {'z_hi'}, dimensions={0} | all-to-all | bytes 786432 | tf_op jit(solution)/shard_map/all_to_all | solution.py:31
  149.1 0.8 copy.75
  (48 shorter events, 2.6 us)
Async XLA Ops:
  51.0 15.1 %collective-permute-start = (bf16[4,4,384,128]{2,3,0,1:T(8,128)(2,1)S(1)}, bf16[4,4,384,128]{2,3,0,1:T(8,128)(2,1)S(1)}, u32[]{:S(2)}, u32[]{:S(2)}) collective-permute-start(bf16[4,4,384,128]{2,3,0,1:T(8,128)(2,1)S(1)} %copy.94), channel_id=1, source_target_pairs={{0,1},{1,0},{2,3},{3,2},{4,5},{5,4},{6,7},{7,6},{8,9},{9,8},{10,11... | collective-permute-start | bytes 4718600 | tf_op jit(solution)/shard_map/ppermute | solution.py:24
  58.1 32.1 %collective-permute-start.2 = (bf16[4,4,128,128]{2,3,1,0:T(8,128)(2,1)}, bf16[4,4,128,128]{2,3,1,0:T(8,128)(2,1)}, u32[]{:S(2)}, u32[]{:S(2)}) collective-permute-start(bf16[4,4,128,128]{2,3,1,0:T(8,128)(2,1)} %bitcast.82), channel_id=1, source_target_pairs={{0,1},{1,0},{2,3},{3,2},{4,5},{5,4},{6,7},{7,6},{8,9},{9,8},{10,11... | collective-permute-start | bytes 1572872 | tf_op jit(solution)/shard_map/ppermute | solution.py:126
  60.6 4.7 %copy-start.6 = (f32[3,3,128]{2,1,0:T(4,128)S(1)}, f32[3,3,128]{2,1,0:T(4,128)}, u32[]{:S(2)}) copy-start(f32[3,3,128]{2,1,0:T(4,128)} %param.10) | copy-start | bytes 13828
  60.6 4.7 %copy-start.4 = (bf16[128,128]{1,0:T(8,128)(2,1)S(1)}, bf16[128,128]{1,0:T(8,128)(2,1)}, u32[]{:S(2)}) copy-start(bf16[128,128]{1,0:T(8,128)(2,1)} %param.11) | copy-start | bytes 98308
  65.3 1.9 %copy-start.5 = (f32[4096]{0:T(1024)S(1)}, f32[4096]{0:T(1024)}, u32[]{:S(2)}) copy-start(f32[4096]{0:T(1024)} %param.8) | copy-start | bytes 49156
  67.2 1.9 %copy-start.1 = (bf16[4096,3,128]{0,2,1:T(8,128)(2,1)S(1)}, bf16[4096,3,128]{0,2,1:T(8,128)(2,1)}, u32[]{:S(2)}) copy-start(bf16[4096,3,128]{0,2,1:T(8,128)(2,1)} %copy.56) | copy-start | bytes 9437188
  70.9 6.1 %copy-start = (bf16[384,384]{1,0:T(8,128)(2,1)}, bf16[384,384]{1,0:T(8,128)(2,1)S(1)}, u32[]{:S(2)}) copy-start(bf16[384,384]{1,0:T(8,128)(2,1)S(1)} %convolution_convert_fusion) | copy-start | bytes 884740
  72.6 14.1 %copy-start.7 = (f32[128]{0:T(128)S(1)}, f32[128]{0:T(128)}, u32[]{:S(2)}) copy-start(f32[128]{0:T(128)} %param.12) | copy-start | bytes 1540
  72.7 17.0 %copy-start.2 = (bf16[128,4,4,1,128]{0,4,3,2,1:T(8,128)(2,1)S(1)}, bf16[128,4,4,1,128]{0,4,3,2,1:T(8,128)(2,1)}, u32[]{:S(2)}) copy-start(bf16[128,4,4,1,128]{0,4,3,2,1:T(8,128)(2,1)} %get-tuple-element.12) | copy-start | bytes 1572868
  72.7 9.3 %collective-permute-start.1 = (bf16[129,384]{1,0:T(8,128)(2,1)S(1)}, bf16[129,384]{1,0:T(8,128)(2,1)S(1)}, u32[]{:S(2)}, u32[]{:S(2)}) collective-permute-start(bf16[129,384]{1,0:T(8,128)(2,1)S(1)} %slice.149), channel_id=1, source_target_pairs={{0,32},{32,64},{64,96},{96,128},{128,160},{160,192},{192,224},{224... | collective-permute-start | bytes 297224 | tf_op jit(solution)/shard_map/ppermute | solution.py:18
  77.0 6.0 %slice-start = ((bf16[384,384]{1,0:T(8,128)(2,1)}), bf16[2,384]{1,0:T(2,128)(2,1)S(1)}, s32[]{:S(2)}) async-start(bf16[384,384]{1,0:T(8,128)(2,1)} %copy-done), calls=%async_computation.3 | async-start | bytes 3072 | tf_op jit(solution)/shard_map/slice | solution.py:108
  79.9 6.8 %copy-start.3 = (f32[192,128]{1,0:T(8,128)S(1)}, f32[192,128]{1,0:T(8,128)}, u32[]{:S(2)}) copy-start(f32[192,128]{1,0:T(8,128)} %shard_map.73) | copy-start | bytes 294916
  87.7 3.2 %collective-permute-start.3 = (bf16[384,128]{1,0:T(8,128)(2,1)S(1)}, bf16[384,128]{1,0:T(8,128)(2,1)S(1)}, u32[]{:S(2)}, u32[]{:S(2)}) collective-permute-start(bf16[384,128]{1,0:T(8,128)(2,1)S(1)} %fusion.8), channel_id=1, source_target_pairs={{0,1},{1,0},{2,3},{3,2},{4,5},{5,4},{6,7},{7,6},{8,9},{9,8},{10,11... | collective-permute-start | bytes 294920 | tf_op jit(solution)/shard_map/ppermute | solution.py:126

commit v14 on v11

--- a/solution.py
+++ b/solution.py
@@ -10,7 +10,7 @@
 CTX = tuple(name for name, _ in CTX_PARTS)
 CH = tuple(name for name, _ in CH_PARTS)
 CTX_COUNT = 16
-FILTER_ROWS = 64
+FILTER_ROWS = 32
 
 
 def passed_along(value, axis, count, steps):
@@ -95,7 +95,7 @@
     local_feats = featurize(projected, feat_taps, tok - (feat_len - 1))
     local_product = (local_feats[:, 1, :] * local_feats[:, 2, :]).astype(jnp.bfloat16)
     filt_rows = long_filter.astype(jnp.float32).T
-    half = tok // 2
+    half = taps + 32
     tail = causal_filter(local_product[half - taps - (feat_len - 1) :].astype(jnp.float32), filt_rows)
     tail, earlier = lax.optimization_barrier((tail, earlier))
     early_feats = featurize(earlier, feat_taps, taps - 1)

time: 143 us -> 143 us (level)
  no operation moved by 1% of the time
where the time goes in v14:
time: 143 us
  blocking collectives  92 us (64%)
  local copies, waits for them, and re-layouts  13.7 us (10%)
  starting transfers between devices  11.7 us (8%)
  waiting for transfers between devices  9.15 us (6%)
  Pallas kernels  6.17 us (4%)
  other arithmetic  5.45 us (4%)
  matrix products  4.01 us (3%)
    all_to_all x2, blocking collectives, reduced(): parts = lax.all_to_all(stack, name, 0, 0)  56.3 us
    all_gather x1, blocking collectives, shards(): stacked = lax.all_gather(bases_in, CH[0], axis=0)  29.4 us
    unnamed x20, local copies, waits for them, and re-layouts  8.24 us
    all_to_all x1, waiting for transfers between devices, gathered(): return lax.all_to_all(copies, name, 0, 0)  6.73 us
    all_to_all x1, blocking collectives, gathered(): return lax.all_to_all(copies, name, 0, 0)  6.26 us
    pallas_call x2, Pallas kernels, causal_filter(): pl.pallas_call(filter_kernel, out_shape=jax.ShapeDtypeStruct((count, chan...  6.17 us
    all_to_all x1, starting transfers between devices, gathered(): return lax.all_to_all(copies, name, 0, 0)  4.29 us
    ppermute x2, starting transfers between devices, shards(): partner = lambda value: lax.ppermute(value, CH[2], [(0, 1), (1, 0)])  3.96 us
  transfers between devices with their start and end apart: 4, of which 3 were waited for; matrix products, arithmetic and copies ran while one was open for 13% of the time, Pallas kernels for 4%

profile of v14, /device:TPU:32, one launch (start us, length us, event | category | flops | bytes accessed | tf_op | source)
XLA Modules:
  0.0 142.5 jit_solution(8378296559139604655)
XLA Ops:
  0.0 29.4 %all-gather = bf16[1536,128]{1,0:T(8,128)(2,1)S(1)} all-gather(bf16[384,128]{1,0:T(8,128)(2,1)} %param.7), channel_id=2, replica_groups=mesh['z_lo'=4,'y'=4,'z_hi'=4,'x'=4,'core'=2] {'z_hi'}, dimensions={0}, use_global_device_ids=true | all-gather | bytes 491520 | tf_op jit(solution)/shard_map/all_gather | solution.py:85
  29.7 1.4 broadcast_in_dim.6
  31.0 4.3 %all-to-all-start = ((bf16[4,4,384,128]{2,3,1,0:T(8,128)(2,1)}), bf16[4,4,384,128]{2,3,1,0:T(8,128)(2,1)S(1)}, u32[]{:S(2)}, u32[]{:S(2)}) async-start(bf16[4,4,384,128]{2,3,1,0:T(8,128)(2,1)} %broadcast_in_dim.6), calls=%async_computation | async-start | bytes 3145728 | tf_op jit(solution)/shard_map/all_to_all | solution.py:23
  35.3 1.6 %copy.51 = bf16[128,4096]{0,1:T(8,128)(2,1)S(1)} copy(bf16[128,4096]{1,0:T(8,128)(2,1)} %param.13) | data formatting | bytes 2097152 | tf_op args[6]
  37.1 0.8 copy.92
  37.9 2.0 %collective-permute-start.1 = (bf16[4,4,128,128]{2,3,1,0:T(8,128)(2,1)}, bf16[4,4,128,128]{2,3,1,0:T(8,128)(2,1)}, u32[]{:S(2)}, u32[]{:S(2)}) collective-permute-start(bf16[4,4,128,128]{2,3,1,0:T(8,128)(2,1)} %bitcast.79), channel_id=1, source_target_pairs={{0,1},{1,0},{2,3},{3,2},{4,5},{5,4},{6,7},{7,6},{8,9},{9,8},{10,11... | collective-permute-start | bytes 1572872 | tf_op jit(solution)/shard_map/ppermute | solution.py:122
  40.0 4.7 %copy.56 = bf16[4096,3,128]{0,2,1:T(8,128)(2,1)} copy(bf16[4096,3,128]{2,0,1:T(8,128)(2,1)} %param.9) | data formatting | bytes 6291456 | tf_op args[2]
  44.8 0.6 convert_bitcast_fusion.filt_ref
  45.5 6.7 %all-to-all-done = bf16[4,4,384,128]{2,3,1,0:T(8,128)(2,1)S(1)} async-done(((bf16[4,4,384,128]{2,3,1,0:T(8,128)(2,1)}), bf16[4,4,384,128]{2,3,1,0:T(8,128)(2,1)S(1)}, u32[]{:S(2)}, u32[]{:S(2)}) %all-to-all-start) | async-done | bytes 1572896 | tf_op jit(solution)/shard_map/all_to_all | solution.py:23
  52.4 0.5 broadcast_in_dim.7
  52.9 6.3 %all_to_all.20 = bf16[2,4,4,384,128]{3,4,1,2,0:T(8,128)(2,1)S(1)} all-to-all(bf16[2,4,4,384,128]{3,4,1,2,0:T(8,128)(2,1)S(1)} %broadcast_in_dim.7), channel_id=1, replica_groups=mesh['z_lo'=4,'y'=4,'z_hi'=4,'x'=4,'core'=2] {'core'}, dimensions={0} | all-to-all | bytes 6291456 | tf_op jit(solution)/shard_map/all_to_all | solution.py:23
  59.1 0.8 fusion
  60.0 0.9 fusion.3
  60.9 1.0 copy-done.1
  61.8 1.8 %convolution_convert_fusion = bf16[384,384]{1,0:T(8,128)(2,1)S(1)} fusion(bf16[384,4096]{0,1:T(8,128)(2,1)S(1)} %bitcast.83, bf16[4096,384]{0,1:T(8,128)(2,1)S(1)} %bitcast.82), kind=kOutput, calls=%fused_computation.8 | convolution fusion | flops 1208107008 | bytes 6586368 | tf_op jit(solution)/shard_map/dot_general | solution.py:92
  63.9 0.2 copy.59
  64.3 0.2 copy.61
  64.8 0.2 copy.63
  65.4 3.5 %collective-permute-start = (bf16[129,384]{1,0:T(8,128)(2,1)S(1)}, bf16[129,384]{1,0:T(8,128)(2,1)S(1)}, u32[]{:S(2)}, u32[]{:S(2)}) collective-permute-start(bf16[129,384]{1,0:T(8,128)(2,1)S(1)} %slice.149), channel_id=1, source_target_pairs={{0,32},{32,64},{64,96},{96,128},{128,160},{160,192},{192,224},{224... | collective-permute-start | bytes 297224 | tf_op jit(solution)/shard_map/ppermute | solution.py:18
  68.9 0.7 fusion.12.ext_ref
  69.6 3.3 %shard_map.73 = f32[224,128]{1,0:T(8,128)} custom-call(f32[352,128]{1,0:T(8,128)} %fusion.12.ext_ref, f32[128,128]{1,0:T(8,128)} %convert_bitcast_fusion.filt_ref), custom_call_target="tpu_custom_call" | custom-call | tf_op jit(solution)/shard_map/pallas_call | solution.py:72
  73.0 1.7 %collective-permute-done = bf16[129,384]{1,0:T(8,128)(2,1)S(1)} collective-permute-done((bf16[129,384]{1,0:T(8,128)(2,1)S(1)}, bf16[129,384]{1,0:T(8,128)(2,1)S(1)}, u32[]{:S(2)}, u32[]{:S(2)}) %collective-permute-start) | collective-permute-done | bytes 99104 | tf_op jit(solution)/shard_map/ppermute | solution.py:18
  75.8 0.8 maximum_convert_fusion.ext_ref
  76.6 2.8 %shard_map.74 = f32[160,128]{1,0:T(8,128)} custom-call(f32[288,128]{1,0:T(8,128)} %maximum_convert_fusion.ext_ref, f32[128,128]{1,0:T(8,128)} %convert_bitcast_fusion.filt_ref), custom_call_target="tpu_custom_call" | custom-call | tf_op jit(solution)/shard_map/pallas_call | solution.py:72
  79.4 1.0 fusion.8
  80.3 1.9 %collective-permute-start.2 = (bf16[384,128]{1,0:T(8,128)(2,1)S(1)}, bf16[384,128]{1,0:T(8,128)(2,1)S(1)}, u32[]{:S(2)}, u32[]{:S(2)}) collective-permute-start(bf16[384,128]{1,0:T(8,128)(2,1)S(1)} %fusion.8), channel_id=1, source_target_pairs={{0,1},{1,0},{2,3},{3,2},{4,5},{5,4},{6,7},{7,6},{8,9},{9,8},{10,11... | collective-permute-start | bytes 294920 | tf_op jit(solution)/shard_map/ppermute | solution.py:122
  82.3 0.6 fusion.5
  82.8 0.7 collective-permute-done.2
  83.5 1.6 %fusion.4 = bf16[4,4,384,128]{2,3,1,0:T(8,128)(2,1)S(1)} fusion(f32[4,4,128,384]{3,2,1,0:T(8,128)S(1)} %fusion.5, bf16[4,4,128,128]{2,3,1,0:T(8,128)(2,1)} %collective-permute-done.1, bf16[384,128]{1,0:T(8,128)(2,1)S(1)} %collective-permute-done.2), kind=kOutput, calls=%fused_computation.7 | convolution fusion | flops 202899456 | bytes 5341184 | tf_op jit(solution)/shard_map/tk,xzki->xzti/dot_general | solution.py:124
  85.2 23.8 %all_to_all.21 = bf16[4,4,384,128]{2,3,1,0:T(8,128)(2,1)S(1)} all-to-all(bf16[4,4,384,128]{2,3,1,0:T(8,128)(2,1)S(1)} %fusion.4), channel_id=1, replica_groups=mesh['z_lo'=4,'y'=4,'z_hi'=4,'x'=4,'core'=2] {'x'}, dimensions={0} | all-to-all | bytes 3145728 | tf_op jit(solution)/shard_map/all_to_all | solution.py:27
  109.1 32.6 %all_to_all.22 = bf16[4,384,128]{1,2,0:T(8,128)(2,1)S(1)} all-to-all(bf16[4,384,128]{1,2,0:T(8,128)(2,1)S(1)} %fusion.6), channel_id=1, replica_groups=mesh['z_lo'=4,'y'=4,'z_hi'=4,'x'=4,'core'=2] {'z_hi'}, dimensions={0} | all-to-all | bytes 786432 | tf_op jit(solution)/shard_map/all_to_all | solution.py:27
  141.8 0.8 copy.75
  (47 shorter events, 2.9 us)
Async XLA Ops:
  31.0 21.2 %all-to-all-start = ((bf16[4,4,384,128]{2,3,1,0:T(8,128)(2,1)}), bf16[4,4,384,128]{2,3,1,0:T(8,128)(2,1)S(1)}, u32[]{:S(2)}, u32[]{:S(2)}) async-start(bf16[4,4,384,128]{2,3,1,0:T(8,128)(2,1)} %broadcast_in_dim.6), calls=%async_computation | async-start | bytes 3145728 | tf_op jit(solution)/shard_map/all_to_all | solution.py:23
  37.9 6.7 %copy-start.5 = (f32[3,3,128]{2,1,0:T(4,128)S(1)}, f32[3,3,128]{2,1,0:T(4,128)}, u32[]{:S(2)}) copy-start(f32[3,3,128]{2,1,0:T(4,128)} %param.10) | copy-start | bytes 13828
  37.9 6.8 %copy-start.3 = (bf16[128,128]{1,0:T(8,128)(2,1)S(1)}, bf16[128,128]{1,0:T(8,128)(2,1)}, u32[]{:S(2)}) copy-start(bf16[128,128]{1,0:T(8,128)(2,1)} %param.11) | copy-start | bytes 98308
  37.9 44.9 %collective-permute-start.1 = (bf16[4,4,128,128]{2,3,1,0:T(8,128)(2,1)}, bf16[4,4,128,128]{2,3,1,0:T(8,128)(2,1)}, u32[]{:S(2)}, u32[]{:S(2)}) collective-permute-start(bf16[4,4,128,128]{2,3,1,0:T(8,128)(2,1)} %bitcast.79), channel_id=1, source_target_pairs={{0,1},{1,0},{2,3},{3,2},{4,5},{5,4},{6,7},{7,6},{8,9},{9,8},{10,11... | collective-permute-start | bytes 1572872 | tf_op jit(solution)/shard_map/ppermute | solution.py:122
  59.1 0.8 copy-start.4
  60.0 1.9 %copy-start.1 = (bf16[4096,3,128]{0,2,1:T(8,128)(2,1)S(1)}, bf16[4096,3,128]{0,2,1:T(8,128)(2,1)}, u32[]{:S(2)}) copy-start(bf16[4096,3,128]{0,2,1:T(8,128)(2,1)} %copy.56) | copy-start | bytes 9437188
  63.7 5.9 %copy-start = (bf16[384,384]{1,0:T(8,128)(2,1)}, bf16[384,384]{1,0:T(8,128)(2,1)S(1)}, u32[]{:S(2)}) copy-start(bf16[384,384]{1,0:T(8,128)(2,1)S(1)} %convolution_convert_fusion) | copy-start | bytes 884740
  65.4 14.0 %copy-start.6 = (f32[128]{0:T(128)S(1)}, f32[128]{0:T(128)}, u32[]{:S(2)}) copy-start(f32[128]{0:T(128)} %param.12) | copy-start | bytes 1540
  65.4 9.3 %collective-permute-start = (bf16[129,384]{1,0:T(8,128)(2,1)S(1)}, bf16[129,384]{1,0:T(8,128)(2,1)S(1)}, u32[]{:S(2)}, u32[]{:S(2)}) collective-permute-start(bf16[129,384]{1,0:T(8,128)(2,1)S(1)} %slice.149), channel_id=1, source_target_pairs={{0,32},{32,64},{64,96},{96,128},{128,160},{160,192},{192,224},{224... | collective-permute-start | bytes 297224 | tf_op jit(solution)/shard_map/ppermute | solution.py:18
  69.6 6.1 %slice-start = ((bf16[384,384]{1,0:T(8,128)(2,1)}), bf16[2,384]{1,0:T(2,128)(2,1)S(1)}, s32[]{:S(2)}) async-start(bf16[384,384]{1,0:T(8,128)(2,1)} %copy-done), calls=%async_computation.4 | async-start | bytes 3072 | tf_op jit(solution)/shard_map/slice | solution.py:104
  73.0 6.4 %copy-start.2 = (f32[224,128]{1,0:T(8,128)S(1)}, f32[224,128]{1,0:T(8,128)}, u32[]{:S(2)}) copy-start(f32[224,128]{1,0:T(8,128)} %shard_map.73) | copy-start | bytes 344068
  80.3 3.2 %collective-permute-start.2 = (bf16[384,128]{1,0:T(8,128)(2,1)S(1)}, bf16[384,128]{1,0:T(8,128)(2,1)S(1)}, u32[]{:S(2)}, u32[]{:S(2)}) collective-permute-start(bf16[384,128]{1,0:T(8,128)(2,1)S(1)} %fusion.8), channel_id=1, source_target_pairs={{0,1},{1,0},{2,3},{3,2},{4,5},{5,4},{6,7},{7,6},{8,9},{9,8},{10,11... | collective-permute-start | bytes 294920 | tf_op jit(solution)/shard_map/ppermute | solution.py:122

commit v15 on v11

--- a/solution.py
+++ b/solution.py
@@ -76,6 +76,28 @@
     )(extended, filt_rows)
 
 
+def norm_kernel(xs_ref, gain_ref, w_ref, out_ref, normed_ref):
+    blocks, _, chans = xs_ref.shape
+    total = jnp.zeros((xs_ref.shape[1], 1), jnp.float32)
+    for b in range(blocks):
+        wide = xs_ref[b].astype(jnp.float32)
+        total = total + jnp.sum(wide * wide, axis=1, keepdims=True)
+    inverse = lax.rsqrt(total / (blocks * chans) + 1e-05)
+    for b in range(blocks):
+        wide = xs_ref[b].astype(jnp.float32)
+        normed_ref[:, b * chans : (b + 1) * chans] = (wide * inverse * gain_ref[pl.ds(b, 1), :]).astype(jnp.bfloat16)
+    out_ref[...] = jnp.dot(normed_ref[...], w_ref[...], preferred_element_type=jnp.float32).astype(out_ref.dtype)
+
+
+def normed_projection(xs, gain, w):
+    blocks, tok, chans = xs.shape
+    return pl.pallas_call(
+        norm_kernel,
+        out_shape=jax.ShapeDtypeStruct((tok, w.shape[1]), jnp.bfloat16),
+        scratch_shapes=[pltpu.VMEM((tok, blocks * chans), jnp.bfloat16)],
+    )(xs, gain, w)
+
+
 def shards(bases_in, norm_gain, w_in, feat_taps, long_filter, skip_gain, w_out):
     tok, chans = bases_in.shape
     width = norm_gain.shape[0]
@@ -85,12 +107,12 @@
     stacked = lax.all_gather(bases_in, CH[0], axis=0)
     for name, size in CH_PARTS[1:]:
         stacked = gathered(stacked, name, size)
-    whole = stacked.transpose(3, 2, 1, 0, 4).reshape(tok, width)
-    wide = whole.astype(jnp.float32)
-    inverse = lax.rsqrt(jnp.mean(wide * wide, axis=1, keepdims=True) + 1e-05)
-    normed = (wide * inverse * norm_gain).astype(jnp.bfloat16)
-    mixed_in = jnp.dot(normed, w_flat, preferred_element_type=jnp.float32)
-    projected = mixed_in.astype(jnp.bfloat16)
+    sizes = [size for _, size in CH_PARTS]
+    order = lambda value: value.reshape(*sizes, chans, *value.shape[1:]).transpose(2, 1, 0, *range(3, value.ndim + 3))
+    xs = stacked.reshape(-1, tok, chans)
+    gain = order(norm_gain).reshape(-1, chans)
+    w_rows = order(w_flat).reshape(width, 3 * chans)
+    projected = normed_projection(xs, gain, w_rows)
     earlier = passed_along(projected[tok - (taps - 1) - (feat_len - 1) :], CTX, CTX_COUNT, 1)
     local_feats = featurize(projected, feat_taps, tok - (feat_len - 1))
     local_product = (local_feats[:, 1, :] * local_feats[:, 2, :]).astype(jnp.bfloat16)

time: 143 us -> 157 us (1.098)
  local copies, waits for them, and re-layouts: 13.7 us -> 27.3 us
  Pallas kernels: 5.86 us -> 12.9 us
  waiting for transfers between devices: 9.56 us -> 2.55 us
  blocking collectives: 91.8 us -> 93.9 us
  matrix products: 4.01 us -> 2.19 us
    transpose x0 -> x2, local copies, waits for them, and re-layouts: none -> 7.52 us  [shards(): value.reshape(*sizes, chans, *value.shape[1:])]
    pallas_call x0 -> x1, Pallas kernels: none -> 7.03 us  [normed_projection(): pl.pallas_call(norm_kernel, out_shape=jax.ShapeDtypeStruct((tok, w.shape[...]
    all_to_all x1, waiting for transfers between devices: 6.73 us -> 0.01 us  [gathered(): return lax.all_to_all(copies, name, 0, 0)]
    another operation x1 -> x2, local copies, waits for them, and re-layouts: 0.11 us -> 5.57 us  [the longest x1 4.67 us: shards(): value.reshape(*sizes, chans, *value.shape[1:])]
    broadcast_in_dim x2, local copies, waits for them, and re-layouts: 1.86 us -> 3.83 us  [gathered(): copies = jnp.broadcast_to(block[None], (count,) + block.shape)]
    unnamed x20, local copies, waits for them, and re-layouts: 8.24 us -> 6.41 us
    dot_general x1 -> x0, matrix products: 1.83 us -> none  [shards(): mixed_in = jnp.dot(normed, w_flat, preferred_element_type=jnp.float32)]
  transfers between devices with their start and end apart: 4 -> 4, of which waited for: 3 -> 2; matrix products, arithmetic and copies ran while one was open for 13% -> 19% of each run, Pallas kernels for 4% -> 8%
where the time goes in v15:
time: 157 us; the launch traced here: 156 us
  blocking collectives  93.9 us (60%)
  local copies, waits for them, and re-layouts  27.3 us (17%)
  Pallas kernels  12.9 us (8%)
  starting transfers between devices  11.8 us (8%)
  other arithmetic  5.02 us (3%)
  waiting for transfers between devices  2.55 us (2%)
  matrix products  2.19 us (1%)
    all_to_all x2, blocking collectives, reduced(): parts = lax.all_to_all(stack, name, 0, 0)  57.1 us
    all_gather x1, blocking collectives, shards(): stacked = lax.all_gather(bases_in, CH[0], axis=0)  29.6 us
    transpose x2, local copies, waits for them, and re-layouts, shards(): value.reshape(*sizes, chans, *value.shape[1:])  7.52 us
    all_to_all x1, blocking collectives, gathered(): return lax.all_to_all(copies, name, 0, 0)  7.27 us
    pallas_call x1, Pallas kernels, normed_projection(): pl.pallas_call(norm_kernel, out_shape=jax.ShapeDtypeStruct((tok, w.shape[...  7.03 us
    unnamed x20, local copies, waits for them, and re-layouts  6.41 us
    pallas_call x2, Pallas kernels, causal_filter(): pl.pallas_call(filter_kernel, out_shape=jax.ShapeDtypeStruct((count, chan...  5.86 us
    another operation x1, local copies, waits for them, and re-layouts, shards(): value.reshape(*sizes, chans, *value.shape[1:])  4.67 us
  transfers between devices with their start and end apart: 4, of which 2 were waited for; matrix products, arithmetic and copies ran while one was open for 19% of the time, Pallas kernels for 8%

profile of v15, /device:TPU:32, one launch (start us, length us, event | category | flops | bytes accessed | tf_op | source)
XLA Modules:
  0.0 156.0 jit_solution(4054075869114900042)
XLA Ops:
  0.0 29.6 %all-gather = bf16[1536,128]{1,0:T(8,128)(2,1)S(1)} all-gather(bf16[384,128]{1,0:T(8,128)(2,1)} %param.7), channel_id=2, replica_groups=mesh['z_lo'=4,'y'=4,'z_hi'=4,'x'=4,'core'=2] {'z_hi'}, dimensions={0}, use_global_device_ids=true | all-gather | bytes 491520 | tf_op jit(solution)/shard_map/all_gather | solution.py:107
  29.6 1.5 broadcast_in_dim.6
  31.1 4.4 %all-to-all-start = ((bf16[4,4,384,128]{3,2,1,0:T(8,128)(2,1)}), bf16[4,4,384,128]{3,2,1,0:T(8,128)(2,1)}, u32[]{:S(2)}, u32[]{:S(2)}) async-start(bf16[4,4,384,128]{3,2,1,0:T(8,128)(2,1)} %broadcast_in_dim.6), calls=%async_computation | async-start | bytes 3145728 | tf_op jit(solution)/shard_map/all_to_all | solution.py:23
  35.5 0.7 copy.10
  36.1 0.9 constant_dynamic-slice_fusion
  37.0 0.8 copy.43
  37.9 1.9 %collective-permute-start.1 = (bf16[4,4,128,128]{2,3,1,0:T(8,128)(2,1)}, bf16[4,4,128,128]{2,3,1,0:T(8,128)(2,1)}, u32[]{:S(2)}, u32[]{:S(2)}) collective-permute-start(bf16[4,4,128,128]{2,3,1,0:T(8,128)(2,1)} %bitcast.77), channel_id=1, source_target_pairs={{0,1},{1,0},{2,3},{3,2},{4,5},{5,4},{6,7},{7,6},{8,9},{9,8},{10,11... | collective-permute-start | bytes 1572872 | tf_op jit(solution)/shard_map/ppermute | solution.py:144
  39.8 4.8 %copy.13 = bf16[4096,3,128]{0,2,1:T(8,128)(2,1)} copy(bf16[4096,3,128]{2,0,1:T(8,128)(2,1)} %param.9) | data formatting | bytes 6291456 | tf_op args[2]
  44.5 4.7 %reshape_reshape.3 = bf16[4,4,2,128,384]{3,2,1,0,4:T(2,128)(2,1)S(1)} reshape(bf16[4096,3,128]{0,2,1:T(8,128)(2,1)} %copy.13) | data formatting | bytes 6291456 | tf_op jit(solution)/shard_map/reshape;reshape | solution.py:111
  49.3 6.9 %copy.14 = bf16[2,4,4,128,384]{4,3,2,1,0:T(8,128)(2,1)} copy(bf16[2,4,4,128,384]{3,0,1,2,4:T(2,128)(2,1)S(1)} %bitcast.81) | data formatting | bytes 6291456 | tf_op jit(solution)/shard_map/transpose | solution.py:111
  56.2 0.6 copy.12
  57.0 0.6 convert_bitcast_fusion.filt_ref
  57.6 2.3 %broadcast_in_dim.7 = bf16[2,4,4,384,128]{4,3,2,1,0:T(8,128)(2,1)S(1)} broadcast(bf16[4,4,384,128]{3,2,1,0:T(8,128)(2,1)} %all-to-all-done), dimensions={1,2,3,4} | broadcast | bytes 4718592 | tf_op jit(solution)/shard_map/broadcast_in_dim | solution.py:22
  59.9 7.3 %all_to_all.20 = bf16[2,4,4,384,128]{4,3,2,1,0:T(8,128)(2,1)} all-to-all(bf16[2,4,4,384,128]{4,3,2,1,0:T(8,128)(2,1)S(1)} %broadcast_in_dim.7), channel_id=1, replica_groups=mesh['z_lo'=4,'y'=4,'z_hi'=4,'x'=4,'core'=2] {'core'}, dimensions={0} | all-to-all | bytes 6291456 | tf_op jit(solution)/shard_map/all_to_all | solution.py:23
  67.2 7.0 %shard_map.73 = bf16[384,384]{1,0:T(8,128)(2,1)} custom-call(bf16[32,384,128]{2,1,0:T(8,128)(2,1)} %bitcast.80, f32[32,128]{1,0:T(8,128)} %bitcast.92, bf16[4096,384]{1,0:T(8,128)(2,1)} %bitcast.79), custom_call_target="tpu_custom_call" | custom-call | tf_op jit(solution)/shard_map/pallas_call | solution.py:94
  74.2 1.4 slice_convert_fusion.2
  75.7 0.9 slice.149
  77.5 0.2 copy.19
  78.2 3.6 %collective-permute-start = (bf16[129,384]{1,0:T(8,128)(2,1)S(1)}, bf16[129,384]{1,0:T(8,128)(2,1)S(1)}, u32[]{:S(2)}, u32[]{:S(2)}) collective-permute-start(bf16[129,384]{1,0:T(8,128)(2,1)S(1)} %slice.149), channel_id=1, source_target_pairs={{0,32},{32,64},{64,96},{96,128},{128,160},{160,192},{192,224},{224... | collective-permute-start | bytes 297224 | tf_op jit(solution)/shard_map/ppermute | solution.py:18
  81.8 0.7 fusion.8.ext_ref
  82.5 2.9 %shard_map.74 = f32[192,128]{1,0:T(8,128)} custom-call(f32[320,128]{1,0:T(8,128)} %fusion.8.ext_ref, f32[128,128]{1,0:T(8,128)} %convert_bitcast_fusion.filt_ref), custom_call_target="tpu_custom_call" | custom-call | tf_op jit(solution)/shard_map/pallas_call | solution.py:72
  85.4 1.9 %collective-permute-done = bf16[129,384]{1,0:T(8,128)(2,1)S(1)} collective-permute-done((bf16[129,384]{1,0:T(8,128)(2,1)S(1)}, bf16[129,384]{1,0:T(8,128)(2,1)S(1)}, u32[]{:S(2)}, u32[]{:S(2)}) %collective-permute-start) | collective-permute-done | bytes 99104 | tf_op jit(solution)/shard_map/ppermute | solution.py:18
  88.4 0.8 maximum_convert_fusion.ext_ref
  89.1 2.9 %shard_map.75 = f32[192,128]{1,0:T(8,128)} custom-call(f32[320,128]{1,0:T(8,128)} %maximum_convert_fusion.ext_ref, f32[128,128]{1,0:T(8,128)} %convert_bitcast_fusion.filt_ref), custom_call_target="tpu_custom_call" | custom-call | tf_op jit(solution)/shard_map/pallas_call | solution.py:72
  92.1 1.0 fusion.4
  93.1 1.9 %collective-permute-start.2 = (bf16[384,128]{1,0:T(8,128)(2,1)S(1)}, bf16[384,128]{1,0:T(8,128)(2,1)S(1)}, u32[]{:S(2)}, u32[]{:S(2)}) collective-permute-start(bf16[384,128]{1,0:T(8,128)(2,1)S(1)} %fusion.4), channel_id=1, source_target_pairs={{0,1},{1,0},{2,3},{3,2},{4,5},{5,4},{6,7},{7,6},{8,9},{9,8},{10,11... | collective-permute-start | bytes 294920 | tf_op jit(solution)/shard_map/ppermute | solution.py:144
  95.0 0.6 fusion.1
  95.6 0.7 collective-permute-done.2
  96.2 1.6 %fusion = bf16[4,4,384,128]{2,3,1,0:T(8,128)(2,1)S(1)} fusion(f32[4,4,128,384]{3,2,1,0:T(8,128)S(1)} %fusion.1, bf16[4,4,128,128]{2,3,1,0:T(8,128)(2,1)} %collective-permute-done.1, bf16[384,128]{1,0:T(8,128)(2,1)S(1)} %collective-permute-done.2), kind=kOutput, calls=%fused_computation.1 | convolution fusion | flops 202899456 | bytes 5341184 | tf_op jit(solution)/shard_map/tk,xzki->xzti/dot_general | solution.py:146
  97.9 25.6 %all_to_all.21 = bf16[4,4,384,128]{2,3,1,0:T(8,128)(2,1)S(1)} all-to-all(bf16[4,4,384,128]{2,3,1,0:T(8,128)(2,1)S(1)} %fusion), channel_id=1, replica_groups=mesh['z_lo'=4,'y'=4,'z_hi'=4,'x'=4,'core'=2] {'x'}, dimensions={0} | all-to-all | bytes 3145728 | tf_op jit(solution)/shard_map/all_to_all | solution.py:27
  123.6 31.5 %all_to_all.22 = bf16[4,384,128]{1,2,0:T(8,128)(2,1)S(1)} all-to-all(bf16[4,384,128]{1,2,0:T(8,128)(2,1)S(1)} %fusion.2), channel_id=1, replica_groups=mesh['z_lo'=4,'y'=4,'z_hi'=4,'x'=4,'core'=2] {'z_hi'}, dimensions={0} | all-to-all | bytes 786432 | tf_op jit(solution)/shard_map/all_to_all | solution.py:27
  155.2 0.8 copy.29
  (45 shorter events, 2.7 us)
Async XLA Ops:
  0.0 35.5 %copy-start.1 = (bf16[128,4096]{1,0:T(8,128)(2,1)S(1)}, bf16[128,4096]{1,0:T(8,128)(2,1)}, u32[]{:S(2)}) copy-start(bf16[128,4096]{1,0:T(8,128)(2,1)} %param.13) | copy-start | bytes 3145732
  31.1 26.5 %all-to-all-start = ((bf16[4,4,384,128]{3,2,1,0:T(8,128)(2,1)}), bf16[4,4,384,128]{3,2,1,0:T(8,128)(2,1)}, u32[]{:S(2)}, u32[]{:S(2)}) async-start(bf16[4,4,384,128]{3,2,1,0:T(8,128)(2,1)} %broadcast_in_dim.6), calls=%async_computation | async-start | bytes 3145728 | tf_op jit(solution)/shard_map/all_to_all | solution.py:23
  37.9 57.7 %collective-permute-start.1 = (bf16[4,4,128,128]{2,3,1,0:T(8,128)(2,1)}, bf16[4,4,128,128]{2,3,1,0:T(8,128)(2,1)}, u32[]{:S(2)}, u32[]{:S(2)}) collective-permute-start(bf16[4,4,128,128]{2,3,1,0:T(8,128)(2,1)} %bitcast.77), channel_id=1, source_target_pairs={{0,1},{1,0},{2,3},{3,2},{4,5},{5,4},{6,7},{7,6},{8,9},{9,8},{10,11... | collective-permute-start | bytes 1572872 | tf_op jit(solution)/shard_map/ppermute | solution.py:144
  49.2 6.9 %copy-start.4 = (f32[4096]{0:T(1024)S(1)}, f32[4096]{0:T(1024)}, u32[]{:S(2)}) copy-start(f32[4096]{0:T(1024)} %param.8) | copy-start | bytes 49156
  49.2 7.6 %copy-start.5 = (f32[3,3,128]{2,1,0:T(4,128)S(1)}, f32[3,3,128]{2,1,0:T(4,128)}, u32[]{:S(2)}) copy-start(f32[3,3,128]{2,1,0:T(4,128)} %param.10) | copy-start | bytes 13828
  49.3 7.6 %copy-start.3 = (bf16[128,128]{1,0:T(8,128)(2,1)S(1)}, bf16[128,128]{1,0:T(8,128)(2,1)}, u32[]{:S(2)}) copy-start(bf16[128,128]{1,0:T(8,128)(2,1)} %param.11) | copy-start | bytes 98308
  78.1 10.2 %slice-start = ((bf16[384,384]{1,0:T(8,128)(2,1)}), bf16[2,384]{1,0:T(2,128)(2,1)S(1)}, s32[]{:S(2)}) async-start(bf16[384,384]{1,0:T(8,128)(2,1)} %shard_map.73), calls=%async_computation.4 | async-start | bytes 3072 | tf_op jit(solution)/shard_map/slice | solution.py:126
  78.1 13.9 %copy-start.6 = (f32[128]{0:T(128)S(1)}, f32[128]{0:T(128)}, u32[]{:S(2)}) copy-start(f32[128]{0:T(128)} %param.12) | copy-start | bytes 1540
  78.2 16.8 %copy-start = (bf16[128,4,4,1,128]{0,4,3,2,1:T(8,128)(2,1)S(1)}, bf16[128,4,4,1,128]{0,4,3,2,1:T(8,128)(2,1)}, u32[]{:S(2)}) copy-start(bf16[128,4,4,1,128]{0,4,3,2,1:T(8,128)(2,1)} %get-tuple-element.10) | copy-start | bytes 1572868
  78.2 9.1 %collective-permute-start = (bf16[129,384]{1,0:T(8,128)(2,1)S(1)}, bf16[129,384]{1,0:T(8,128)(2,1)S(1)}, u32[]{:S(2)}, u32[]{:S(2)}) collective-permute-start(bf16[129,384]{1,0:T(8,128)(2,1)S(1)} %slice.149), channel_id=1, source_target_pairs={{0,32},{32,64},{64,96},{96,128},{128,160},{160,192},{192,224},{224... | collective-permute-start | bytes 297224 | tf_op jit(solution)/shard_map/ppermute | solution.py:18
  85.4 6.6 %copy-start.2 = (f32[192,128]{1,0:T(8,128)S(1)}, f32[192,128]{1,0:T(8,128)}, u32[]{:S(2)}) copy-start(f32[192,128]{1,0:T(8,128)} %shard_map.74) | copy-start | bytes 294916
  93.1 3.2 %collective-permute-start.2 = (bf16[384,128]{1,0:T(8,128)(2,1)S(1)}, bf16[384,128]{1,0:T(8,128)(2,1)S(1)}, u32[]{:S(2)}, u32[]{:S(2)}) collective-permute-start(bf16[384,128]{1,0:T(8,128)(2,1)S(1)} %fusion.4), channel_id=1, source_target_pairs={{0,1},{1,0},{2,3},{3,2},{4,5},{5,4},{6,7},{7,6},{8,9},{9,8},{10,11... | collective-permute-start | bytes 294920 | tf_op jit(solution)/shard_map/ppermute | solution.py:144

commit v16 on v11

--- a/solution.py
+++ b/solution.py
@@ -10,7 +10,7 @@
 CTX = tuple(name for name, _ in CTX_PARTS)
 CH = tuple(name for name, _ in CH_PARTS)
 CTX_COUNT = 16
-FILTER_ROWS = 64
+FILTER_ROWS = 96
 
 
 def passed_along(value, axis, count, steps):

time: 143 us -> 143 us (level)
  no operation moved by 1% of the time
where the time goes in v16:
time: 143 us; the launch traced here: 142 us
  blocking collectives  91.8 us (64%)
  local copies, waits for them, and re-layouts  13.7 us (10%)
  starting transfers between devices  11.7 us (8%)
  waiting for transfers between devices  9.66 us (7%)
  Pallas kernels  5.67 us (4%)
  other arithmetic  5.46 us (4%)
  matrix products  4.01 us (3%)
    all_to_all x2, blocking collectives, reduced(): parts = lax.all_to_all(stack, name, 0, 0)  56.1 us
    all_gather x1, blocking collectives, shards(): stacked = lax.all_gather(bases_in, CH[0], axis=0)  29.4 us
    unnamed x20, local copies, waits for them, and re-layouts  8.24 us
    all_to_all x1, waiting for transfers between devices, gathered(): return lax.all_to_all(copies, name, 0, 0)  6.73 us
    all_to_all x1, blocking collectives, gathered(): return lax.all_to_all(copies, name, 0, 0)  6.26 us
    pallas_call x2, Pallas kernels, causal_filter(): pl.pallas_call(filter_kernel, out_shape=jax.ShapeDtypeStruct((count, chan...  5.67 us
    all_to_all x1, starting transfers between devices, gathered(): return lax.all_to_all(copies, name, 0, 0)  4.29 us
    ppermute x2, starting transfers between devices, shards(): partner = lambda value: lax.ppermute(value, CH[2], [(0, 1), (1, 0)])  3.96 us
  transfers between devices with their start and end apart: 4, of which 3 were waited for; matrix products, arithmetic and copies ran while one was open for 13% of the time, Pallas kernels for 4%

profile of v16, /device:TPU:32, one launch (start us, length us, event | category | flops | bytes accessed | tf_op | source)
XLA Modules:
  0.0 142.3 jit_solution(14793215590618844070)
XLA Ops:
  0.0 29.4 %all-gather = bf16[1536,128]{1,0:T(8,128)(2,1)S(1)} all-gather(bf16[384,128]{1,0:T(8,128)(2,1)} %param.7), channel_id=2, replica_groups=mesh['z_lo'=4,'y'=4,'z_hi'=4,'x'=4,'core'=2] {'z_hi'}, dimensions={0}, use_global_device_ids=true | all-gather | bytes 491520 | tf_op jit(solution)/shard_map/all_gather | solution.py:85
  29.7 1.4 broadcast_in_dim.6
  31.0 4.3 %all-to-all-start = ((bf16[4,4,384,128]{2,3,1,0:T(8,128)(2,1)}), bf16[4,4,384,128]{2,3,1,0:T(8,128)(2,1)S(1)}, u32[]{:S(2)}, u32[]{:S(2)}) async-start(bf16[4,4,384,128]{2,3,1,0:T(8,128)(2,1)} %broadcast_in_dim.6), calls=%async_computation | async-start | bytes 3145728 | tf_op jit(solution)/shard_map/all_to_all | solution.py:23
  35.3 1.6 %copy.51 = bf16[128,4096]{0,1:T(8,128)(2,1)S(1)} copy(bf16[128,4096]{1,0:T(8,128)(2,1)} %param.13) | data formatting | bytes 2097152 | tf_op args[6]
  37.1 0.8 copy.92
  37.9 2.0 %collective-permute-start.1 = (bf16[4,4,128,128]{2,3,1,0:T(8,128)(2,1)}, bf16[4,4,128,128]{2,3,1,0:T(8,128)(2,1)}, u32[]{:S(2)}, u32[]{:S(2)}) collective-permute-start(bf16[4,4,128,128]{2,3,1,0:T(8,128)(2,1)} %bitcast.79), channel_id=1, source_target_pairs={{0,1},{1,0},{2,3},{3,2},{4,5},{5,4},{6,7},{7,6},{8,9},{9,8},{10,11... | collective-permute-start | bytes 1572872 | tf_op jit(solution)/shard_map/ppermute | solution.py:122
  40.0 4.7 %copy.56 = bf16[4096,3,128]{0,2,1:T(8,128)(2,1)} copy(bf16[4096,3,128]{2,0,1:T(8,128)(2,1)} %param.9) | data formatting | bytes 6291456 | tf_op args[2]
  44.8 0.6 convert_bitcast_fusion.filt_ref
  45.5 6.7 %all-to-all-done = bf16[4,4,384,128]{2,3,1,0:T(8,128)(2,1)S(1)} async-done(((bf16[4,4,384,128]{2,3,1,0:T(8,128)(2,1)}), bf16[4,4,384,128]{2,3,1,0:T(8,128)(2,1)S(1)}, u32[]{:S(2)}, u32[]{:S(2)}) %all-to-all-start) | async-done | bytes 1572896 | tf_op jit(solution)/shard_map/all_to_all | solution.py:23
  52.4 0.5 broadcast_in_dim.7
  52.9 6.3 %all_to_all.20 = bf16[2,4,4,384,128]{3,4,1,2,0:T(8,128)(2,1)S(1)} all-to-all(bf16[2,4,4,384,128]{3,4,1,2,0:T(8,128)(2,1)S(1)} %broadcast_in_dim.7), channel_id=1, replica_groups=mesh['z_lo'=4,'y'=4,'z_hi'=4,'x'=4,'core'=2] {'core'}, dimensions={0} | all-to-all | bytes 6291456 | tf_op jit(solution)/shard_map/all_to_all | solution.py:23
  59.1 0.8 fusion
  60.0 0.9 fusion.3
  60.9 1.0 copy-done.1
  61.8 1.8 %convolution_convert_fusion = bf16[384,384]{1,0:T(8,128)(2,1)S(1)} fusion(bf16[384,4096]{0,1:T(8,128)(2,1)S(1)} %bitcast.83, bf16[4096,384]{0,1:T(8,128)(2,1)S(1)} %bitcast.82), kind=kOutput, calls=%fused_computation.8 | convolution fusion | flops 1208107008 | bytes 6586368 | tf_op jit(solution)/shard_map/dot_general | solution.py:92
  63.9 0.2 copy.59
  64.3 0.2 copy.61
  64.8 0.2 copy.63
  65.4 3.5 %collective-permute-start = (bf16[129,384]{1,0:T(8,128)(2,1)S(1)}, bf16[129,384]{1,0:T(8,128)(2,1)S(1)}, u32[]{:S(2)}, u32[]{:S(2)}) collective-permute-start(bf16[129,384]{1,0:T(8,128)(2,1)S(1)} %slice.149), channel_id=1, source_target_pairs={{0,32},{32,64},{64,96},{96,128},{128,160},{160,192},{192,224},{224... | collective-permute-start | bytes 297224 | tf_op jit(solution)/shard_map/ppermute | solution.py:18
  68.9 0.7 fusion.12.ext_ref
  69.6 2.8 %shard_map.73 = f32[192,128]{1,0:T(8,128)} custom-call(f32[320,128]{1,0:T(8,128)} %fusion.12.ext_ref, f32[128,128]{1,0:T(8,128)} %convert_bitcast_fusion.filt_ref), custom_call_target="tpu_custom_call" | custom-call | tf_op jit(solution)/shard_map/pallas_call | solution.py:72
  72.5 2.2 %collective-permute-done = bf16[129,384]{1,0:T(8,128)(2,1)S(1)} collective-permute-done((bf16[129,384]{1,0:T(8,128)(2,1)S(1)}, bf16[129,384]{1,0:T(8,128)(2,1)S(1)}, u32[]{:S(2)}, u32[]{:S(2)}) %collective-permute-start) | collective-permute-done | bytes 99104 | tf_op jit(solution)/shard_map/ppermute | solution.py:18
  75.8 0.8 maximum_convert_fusion.ext_ref
  76.6 2.8 %shard_map.74 = f32[192,128]{1,0:T(8,128)} custom-call(f32[320,128]{1,0:T(8,128)} %maximum_convert_fusion.ext_ref, f32[128,128]{1,0:T(8,128)} %convert_bitcast_fusion.filt_ref), custom_call_target="tpu_custom_call" | custom-call | tf_op jit(solution)/shard_map/pallas_call | solution.py:72
  79.4 1.0 fusion.8
  80.4 1.9 %collective-permute-start.2 = (bf16[384,128]{1,0:T(8,128)(2,1)S(1)}, bf16[384,128]{1,0:T(8,128)(2,1)S(1)}, u32[]{:S(2)}, u32[]{:S(2)}) collective-permute-start(bf16[384,128]{1,0:T(8,128)(2,1)S(1)} %fusion.8), channel_id=1, source_target_pairs={{0,1},{1,0},{2,3},{3,2},{4,5},{5,4},{6,7},{7,6},{8,9},{9,8},{10,11... | collective-permute-start | bytes 294920 | tf_op jit(solution)/shard_map/ppermute | solution.py:122
  82.3 0.6 fusion.5
  82.9 0.7 collective-permute-done.2
  83.6 1.6 %fusion.4 = bf16[4,4,384,128]{2,3,1,0:T(8,128)(2,1)S(1)} fusion(f32[4,4,128,384]{3,2,1,0:T(8,128)S(1)} %fusion.5, bf16[4,4,128,128]{2,3,1,0:T(8,128)(2,1)} %collective-permute-done.1, bf16[384,128]{1,0:T(8,128)(2,1)S(1)} %collective-permute-done.2), kind=kOutput, calls=%fused_computation.7 | convolution fusion | flops 202899456 | bytes 5341184 | tf_op jit(solution)/shard_map/tk,xzki->xzti/dot_general | solution.py:124
  85.2 23.8 %all_to_all.21 = bf16[4,4,384,128]{2,3,1,0:T(8,128)(2,1)S(1)} all-to-all(bf16[4,4,384,128]{2,3,1,0:T(8,128)(2,1)S(1)} %fusion.4), channel_id=1, replica_groups=mesh['z_lo'=4,'y'=4,'z_hi'=4,'x'=4,'core'=2] {'x'}, dimensions={0} | all-to-all | bytes 3145728 | tf_op jit(solution)/shard_map/all_to_all | solution.py:27
  109.1 32.3 %all_to_all.22 = bf16[4,384,128]{1,2,0:T(8,128)(2,1)S(1)} all-to-all(bf16[4,384,128]{1,2,0:T(8,128)(2,1)S(1)} %fusion.6), channel_id=1, replica_groups=mesh['z_lo'=4,'y'=4,'z_hi'=4,'x'=4,'core'=2] {'z_hi'}, dimensions={0} | all-to-all | bytes 786432 | tf_op jit(solution)/shard_map/all_to_all | solution.py:27
  141.5 0.8 copy.75
  (47 shorter events, 2.9 us)
Async XLA Ops:
  31.0 21.2 %all-to-all-start = ((bf16[4,4,384,128]{2,3,1,0:T(8,128)(2,1)}), bf16[4,4,384,128]{2,3,1,0:T(8,128)(2,1)S(1)}, u32[]{:S(2)}, u32[]{:S(2)}) async-start(bf16[4,4,384,128]{2,3,1,0:T(8,128)(2,1)} %broadcast_in_dim.6), calls=%async_computation | async-start | bytes 3145728 | tf_op jit(solution)/shard_map/all_to_all | solution.py:23
  37.9 6.7 %copy-start.5 = (f32[3,3,128]{2,1,0:T(4,128)S(1)}, f32[3,3,128]{2,1,0:T(4,128)}, u32[]{:S(2)}) copy-start(f32[3,3,128]{2,1,0:T(4,128)} %param.10) | copy-start | bytes 13828
  37.9 6.8 %copy-start.3 = (bf16[128,128]{1,0:T(8,128)(2,1)S(1)}, bf16[128,128]{1,0:T(8,128)(2,1)}, u32[]{:S(2)}) copy-start(bf16[128,128]{1,0:T(8,128)(2,1)} %param.11) | copy-start | bytes 98308
  37.9 44.9 %collective-permute-start.1 = (bf16[4,4,128,128]{2,3,1,0:T(8,128)(2,1)}, bf16[4,4,128,128]{2,3,1,0:T(8,128)(2,1)}, u32[]{:S(2)}, u32[]{:S(2)}) collective-permute-start(bf16[4,4,128,128]{2,3,1,0:T(8,128)(2,1)} %bitcast.79), channel_id=1, source_target_pairs={{0,1},{1,0},{2,3},{3,2},{4,5},{5,4},{6,7},{7,6},{8,9},{9,8},{10,11... | collective-permute-start | bytes 1572872 | tf_op jit(solution)/shard_map/ppermute | solution.py:122
  59.1 0.8 copy-start.4
  60.0 1.9 %copy-start.1 = (bf16[4096,3,128]{0,2,1:T(8,128)(2,1)S(1)}, bf16[4096,3,128]{0,2,1:T(8,128)(2,1)}, u32[]{:S(2)}) copy-start(bf16[4096,3,128]{0,2,1:T(8,128)(2,1)} %copy.56) | copy-start | bytes 9437188
  63.7 5.9 %copy-start = (bf16[384,384]{1,0:T(8,128)(2,1)}, bf16[384,384]{1,0:T(8,128)(2,1)S(1)}, u32[]{:S(2)}) copy-start(bf16[384,384]{1,0:T(8,128)(2,1)S(1)} %convolution_convert_fusion) | copy-start | bytes 884740
  65.4 14.0 %copy-start.6 = (f32[128]{0:T(128)S(1)}, f32[128]{0:T(128)}, u32[]{:S(2)}) copy-start(f32[128]{0:T(128)} %param.12) | copy-start | bytes 1540
  65.4 9.3 %collective-permute-start = (bf16[129,384]{1,0:T(8,128)(2,1)S(1)}, bf16[129,384]{1,0:T(8,128)(2,1)S(1)}, u32[]{:S(2)}, u32[]{:S(2)}) collective-permute-start(bf16[129,384]{1,0:T(8,128)(2,1)S(1)} %slice.149), channel_id=1, source_target_pairs={{0,32},{32,64},{64,96},{96,128},{128,160},{160,192},{192,224},{224... | collective-permute-start | bytes 297224 | tf_op jit(solution)/shard_map/ppermute | solution.py:18
  69.6 6.1 %slice-start = ((bf16[384,384]{1,0:T(8,128)(2,1)}), bf16[2,384]{1,0:T(2,128)(2,1)S(1)}, s32[]{:S(2)}) async-start(bf16[384,384]{1,0:T(8,128)(2,1)} %copy-done), calls=%async_computation.4 | async-start | bytes 3072 | tf_op jit(solution)/shard_map/slice | solution.py:104
  72.5 6.9 %copy-start.2 = (f32[192,128]{1,0:T(8,128)S(1)}, f32[192,128]{1,0:T(8,128)}, u32[]{:S(2)}) copy-start(f32[192,128]{1,0:T(8,128)} %shard_map.73) | copy-start | bytes 294916
  80.4 3.2 %collective-permute-start.2 = (bf16[384,128]{1,0:T(8,128)(2,1)S(1)}, bf16[384,128]{1,0:T(8,128)(2,1)S(1)}, u32[]{:S(2)}, u32[]{:S(2)}) collective-permute-start(bf16[384,128]{1,0:T(8,128)(2,1)S(1)} %fusion.8), channel_id=1, source_target_pairs={{0,1},{1,0},{2,3},{3,2},{4,5},{5,4},{6,7},{7,6},{8,9},{9,8},{10,11... | collective-permute-start | bytes 294920 | tf_op jit(solution)/shard_map/ppermute | solution.py:122
